TPU v7x, 128 devices: a whole 4x4x4 slice. The times are simulated.
128 devices in a mesh: grp: 4 (over x_hi, core), dev: 32 (over z, y, x_lo).
Axes of the slice: x: 4 (x_hi: 2, x_lo: 2; x = x_hi * 2 + x_lo), y: 4, z: 4, core: 2. Of those that a mesh axis runs over, the one named last changes fastest.
Arguments:
- voltages: bfloat16 [2048, 16384], P(('grp', 'dev')), may hold values from -6 to 6
- filter_taps: float32 [4, 4096], replicated, may hold values from -0.046875 to 0.046875
- dipole_cells: int32 [2048, 2], replicated, may hold values from 0 to 254
- kernel_bits: int32 [2048, 2], replicated, may hold values from 1 to 3
- sky_model: float32 [2048, 256, 256], P('grp', 'dev'), may hold values from 0 to 2
Outputs:
- residual_images: float32 [2048, 256, 256], P('grp', 'dev')
- broadband: float32 [256, 256], P('dev')
Inputs may be any that keep to these rules, and one draw needn't show every extreme that they name: `dipole_cells`: grid row and column of a dipole's first kernel cell; the kernel may also reach index plus one. `kernel_bits`: bit 0 gives weight 1 to the cell at the index, bit 1 to the cell at the index plus one.
All inputs are finite; a program needn't handle non-finite values.
Results may differ from a plain program's by a relative error of at most 0.005.
Values may be sent and summed in bfloat16 or wider, within the bound.
No kernel may reach another device: no remote copies, remote signals or barrier semaphores. Data moves between devices by JAX's collectives and lax.ppermute only.
A program may use at most 192 MiB of HBM per device.

v0:
```python
import math

import jax
import jax.numpy as jnp
from jax import lax
from jax.sharding import PartitionSpec as P


def spectrum_table(points, channels):
    sample_idx = lax.broadcasted_iota(jnp.int32, (points, channels), 0)
    channel_idx = lax.broadcasted_iota(jnp.int32, (points, channels), 1)
    angle = (sample_idx * channel_idx % points).astype(jnp.float32) * (2.0 * math.pi / points)
    return jnp.stack([jnp.cos(angle), -jnp.sin(angle)])


def transform_table(length):
    out_idx = lax.broadcasted_iota(jnp.int32, (length, length), 0)
    in_idx = lax.broadcasted_iota(jnp.int32, (length, length), 1)
    angle = (out_idx * in_idx % length).astype(jnp.float32) * (2.0 * math.pi / length)
    cosine = jnp.cos(angle)
    sine = jnp.sin(angle)
    return jnp.stack([jnp.stack([cosine, sine]), jnp.stack([-sine, cosine])])


def split_table(table):
    upper_part = table.astype(jnp.bfloat16)
    lower_part = (table - upper_part.astype(jnp.float32)).astype(jnp.bfloat16)
    return (upper_part, lower_part)


def one_hot(cell_col, bit_col, length):
    rows_iota = lax.broadcasted_iota(jnp.int32, (length, cell_col.shape[0]), 0)
    lower = (rows_iota == cell_col[None, :]) * (bit_col % 2)[None, :]
    upper = (rows_iota == cell_col[None, :] + 1) * (bit_col // 2)[None, :]
    return (lower + upper).astype(jnp.bfloat16)


def group_major(values, groups, members):
    width = values.shape[1]
    return values.reshape(groups, members, -1, width).transpose(1, 0, 2, 3).reshape(values.shape)


def channelize(voltages, filter_taps):
    tap_count, points = filter_taps.shape
    dipoles = voltages.shape[0]
    segments = voltages.reshape(dipoles, -1, points)
    frame_count = segments.shape[1] - tap_count + 1
    framed = jnp.zeros((dipoles, frame_count, points), jnp.float32)
    for tap_index in range(tap_count):
        framed = framed + filter_taps[tap_index][None, None, :] * segments[
            :, tap_index : tap_index + frame_count, :
        ].astype(jnp.float32)
    table = spectrum_table(points, points // 2)
    spectra = jnp.einsum("afn,qnk->qfka", framed, table, precision=lax.Precision.HIGHEST)
    return spectra.astype(jnp.bfloat16)


def block_length(channels, row_bytes, target):
    length = 1
    while (
        length * 2 <= channels
        and channels % (length * 2) == 0
        and (length * 2 * row_bytes <= target)
    ):
        length = length * 2
    return length


def grid_half(spectra, row_kernel, col_kernel, w_table):
    parts, frame_count, channels, dipoles = spectra.shape
    col_count = col_kernel.shape[0]
    grid_len = row_kernel.shape[0]
    span = block_length(channels, 4 * frame_count * col_count * dipoles, 2**22)
    blocks = channels // span
    portions = spectra.reshape(parts, frame_count, blocks, span, dipoles).transpose(2, 0, 1, 3, 4)

    def single(portion):
        spread = portion[:, :, :, None, :] * col_kernel[None, None, None, :, :]
        aperture = jnp.einsum(
            "qfcva,ua->qfcvu", spread, row_kernel, preferred_element_type=jnp.float32
        )
        half_turn = jnp.einsum(
            "pqUu,qfcvu->pfcvU", w_table, aperture, precision=lax.Precision.HIGHEST
        )
        return half_turn.astype(jnp.bfloat16)

    halves = lax.map(single, portions)
    return halves.transpose(1, 2, 0, 3, 4, 5).reshape(
        parts, frame_count, channels, col_count, grid_len
    )


def image_power(half_turn, table_upper, table_lower, norm_scale, form):
    sky_image = jnp.einsum(form, table_upper, half_turn, preferred_element_type=jnp.float32)
    sky_image = sky_image + jnp.einsum(
        form, table_lower, half_turn, preferred_element_type=jnp.float32
    )
    return jnp.sum(sky_image * sky_image, axis=(0, 1)) * norm_scale


def body(voltages, filter_taps, dipole_cells, kernel_bits, sky_model):
    groups = lax.axis_size("grp")
    members = lax.axis_size("dev")
    dipoles = dipole_cells.shape[0]
    grid_len = sky_model.shape[2]
    rows_mine = sky_model.shape[1]
    spectra = channelize(voltages, filter_taps)
    w_table = transform_table(grid_len)
    table_upper, table_lower = split_table(w_table)
    norm_scale = 1.0 / (spectra.shape[1] * dipoles)
    turned = lax.all_to_all(spectra, "grp", split_axis=2, concat_axis=3, tiled=True)
    everyone = lax.all_gather(turned, "dev", axis=3, tiled=True)
    order_cells = group_major(dipole_cells, groups, members)
    order_bits = group_major(kernel_bits, groups, members)
    row_kernel = one_hot(order_cells[:, 0], order_bits[:, 0], grid_len)
    col_full = one_hot(order_cells[:, 1], order_bits[:, 1], grid_len)
    col_mine = lax.dynamic_slice_in_dim(col_full, lax.axis_index("dev") * rows_mine, rows_mine, 0)
    half_turn = grid_half(everyone, row_kernel, col_mine, w_table)
    power_sum = image_power(
        lax.all_to_all(half_turn, "dev", split_axis=4, concat_axis=3, tiled=True),
        table_upper,
        table_lower,
        norm_scale,
        "tksw,khnwm->thnms",
    )
    residual_images = power_sum - sky_model
    channel_total = residual_images.shape[0] * groups
    broadband = lax.psum(jnp.sum(residual_images, axis=0), "grp") / channel_total
    return (residual_images, broadband)


def solution(mesh):
    in_specs = (P(("grp", "dev"), None), P(), P(), P(), P("grp", "dev", None))
    out_specs = (P("grp", "dev", None), P("dev", None))
    return jax.shard_map(body, mesh=mesh, in_specs=in_specs, out_specs=out_specs, check_vma=False)
```

profile of v0, /device:TPU:0, one launch (start us, length us, event | category | flops | bytes accessed | tf_op | source)
XLA Modules:
  0.0 504.8 jit_solution(7157894593650749076)
XLA Ops:
  7.2 133.6 %sine_negate_fusion = (f32[1,4096,2048]{2,1,0:T(8,128)}, f32[1,4096,2048]{2,1,0:T(8,128)}) fusion(), kind=kLoop, calls=%fused_computation.33 | loop fusion | flops 125829120 | bytes 67108864 | tf_op jit(solution)/shard_map/neg | solution.py:13
  141.3 0.8 fusion.82
  142.1 39.7 %fusion.36 = bf16[2,1,2048,16]{2,3,0,1:T(8,128)(2,1)S(1)} fusion(f32[1,4096,2048]{2,1,0:T(8,128)} %get-tuple-element.148, f32[1,4096,2048]{2,1,0:T(8,128)} %get-tuple-element.149, bf16[16,1,4096]{2,1,0:T(2,128)(2,1)S(1)} %get-tuple-element.133, bf16[16,1,4096]{2,1,0:T(2,128)(2,1)S(1)} %get-tuple-element.131, ...), kind=kOutput, calls=%fused_computation.44 | convolution fusion | flops 3238789120 | bytes 67829760 | tf_op jit(solution)/shard_map/afn,qnk->qfka/dot_general | solution.py:54
  181.8 0.7 copy.78
  182.5 1.1 reshape.325
  183.6 10.3 %all_to_all.33 = bf16[4,2,8192]{2,1,0:T(2,128)(2,1)S(1)} all-to-all(bf16[4,2,8192]{2,1,0:T(2,128)(2,1)S(1)} %reshape.325), channel_id=1, replica_groups=mesh['grp'=4,'dev'=32] {'grp'}, dimensions={0} | all-to-all | bytes 262144 | tf_op jit(solution)/shard_map/all_to_all | solution.py:111
  193.9 0.7 reshape.326
  194.6 0.7 copy.99
  195.4 0.7 copy.80
  196.8 1.0 fusion.73
  197.8 1.0 fusion.67
  199.1 162.2 %all-gather.2.cloned.1.call-done = bf16[2,1,512,2048]{2,3,0,1:T(8,128)(2,1)} async-done(((bf16[2,1,512,64]{2,3,0,1:T(8,128)(2,1)}), bf16[2,1,512,2048]{2,3,0,1:T(8,128)(2,1)}) %all-gather.2.cloned.1.call-update) | async-done | bytes 4194320 | tf_op jit(solution)/shard_map/all_gather | solution.py:112
  361.3 6.3 %copy.81 = bf16[2,1,512,2048]{3,2,0,1:T(8,128)(2,1)} copy(bf16[2,1,512,2048]{2,3,0,1:T(8,128)(2,1)} %all-gather.2.cloned.1.call-done) | data formatting | bytes 8388608 | tf_op jit(solution)/shard_map/all_gather | solution.py:112
  367.5 46.8 %while.11 = (s32[]{:T(128)}, bf16[8,2,1,64,8,256]{5,4,3,0,1,2:T(8,128)(2,1)}, bf16[8,2,1,64,2048]{4,3,0,1,2:T(8,128)(2,1)}, bf16[8,2048]{1,0:T(8,128)(2,1)S(1)},...) while((s32[]{:T(128)}, ...), condition=%wide.region_1.2_spmd.clone, body=%wide.region_0.1_spmd.clone.sunk | while | flops 2689859584 | bytes 7406185 | solution.py:87
  367.5 1.1 constant_dynamic-slice_fusion.2
  368.6 0.5 copy.137
  369.2 1.5 fusion.99
  370.7 1.9 fusion.100
  372.6 0.8 copy_dynamic-update-slice_fusion.2
  373.4 1.1 constant_dynamic-slice_fusion.2
  374.5 0.5 copy.137
  375.0 1.5 fusion.99
  376.5 1.9 fusion.100
  378.4 0.8 copy_dynamic-update-slice_fusion.2
  379.2 1.1 constant_dynamic-slice_fusion.2
  380.3 0.5 copy.137
  380.9 1.5 fusion.99
  382.4 1.9 fusion.100
  384.3 0.8 copy_dynamic-update-slice_fusion.2
  385.1 1.1 constant_dynamic-slice_fusion.2
  386.2 0.5 copy.137
  386.7 1.5 fusion.99
  388.2 1.9 fusion.100
  390.1 0.8 copy_dynamic-update-slice_fusion.2
  390.9 1.1 constant_dynamic-slice_fusion.2
  392.0 0.5 copy.137
  392.6 1.5 fusion.99
  394.1 1.9 fusion.100
  395.9 0.8 copy_dynamic-update-slice_fusion.2
  396.8 1.1 constant_dynamic-slice_fusion.2
  397.9 0.5 copy.137
  398.4 1.5 fusion.99
  399.9 1.9 fusion.100
  401.8 0.8 copy_dynamic-update-slice_fusion.2
  402.6 1.1 constant_dynamic-slice_fusion.2
  403.7 0.5 copy.137
  404.3 1.5 fusion.99
  405.8 1.9 fusion.100
  407.6 0.8 copy_dynamic-update-slice_fusion.2
  408.5 1.1 constant_dynamic-slice_fusion.2
  410.1 1.5 fusion.99
  411.6 1.9 fusion.100
  413.5 0.8 copy_dynamic-update-slice_fusion.2
  414.3 8.6 %copy.86 = bf16[2,1,512,8,256]{2,3,1,0,4:T(8,128)(2,1)} copy(bf16[2,1,512,8,256]{4,3,2,0,1:T(8,128)(2,1)} %bitcast.21) | data formatting | bytes 8388608 | tf_op jit(solution)/shard_map/reshape | solution.py:88
  422.9 37.0 %all_to_all.34 = bf16[2,1,512,8,256]{2,3,1,0,4:T(8,128)(2,1)S(1)} all-to-all(bf16[2,1,512,8,256]{2,3,1,0,4:T(8,128)(2,1)} %copy.86), channel_id=1, replica_groups=mesh['grp'=4,'dev'=32] {'dev'}, dimensions={4} | all-to-all | bytes 8388608 | tf_op jit(solution)/shard_map/all_to_all | solution.py:120
  459.9 2.4 copy.133
  462.3 2.6 copy.88
  464.9 7.5 %copy.95 = bf16[2,512,256,8,1]{2,1,0,4,3:T(8,128)(2,1)} copy(bf16[2,512,256,8,1]{1,3,2,0,4:T(8,128)(2,1)} %bitcast.108) | data formatting | bytes 8388608 | tf_op jit(solution)/shard_map/reshape.23
  472.4 4.8 fusion.41
  477.3 4.6 fusion.32
  481.8 3.8 fusion.81
  485.6 4.4 copy.92
  490.1 7.2 %psum.7 = f32[8,256]{1,0:T(8,128)S(1)} all-reduce(f32[8,256]{1,0:T(8,128)S(1)} %get-tuple-element.128), channel_id=1, replica_groups=mesh['grp'=4,'dev'=32] {'grp'}, use_global_device_ids=true, to_apply=%region_4.5 | all-reduce | flops 2048 | bytes 16384 | tf_op jit(solution)/shard_map/psum | solution.py:128
  497.3 0.6 broadcast_multiply_fusion
  (32 shorter events, 2.0 us)
Async XLA Ops:
  7.2 133.7 %copy-start.2 = (bf16[16,16384]{1,0:T(8,128)(2,1)S(1)}, bf16[16,16384]{1,0:T(8,128)(2,1)}, u32[]{:S(2)}) copy-start(bf16[16,16384]{1,0:T(8,128)(2,1)} %param.7) | copy-start | bytes 1572868
  7.2 134.8 %copy-start.3 = (f32[4,4096]{1,0:T(4,128)S(1)}, f32[4,4096]{1,0:T(4,128)}, u32[]{:S(2)}) copy-start(f32[4,4096]{1,0:T(4,128)} %param.8) | copy-start | bytes 196612
  7.2 354.1 %all-gather.2.cloned.1.call-start = ((), (), s32[]{:S(2)}) async-start(), calls=%async_computation.2 | async-start | bytes 4325376 | tf_op jit(solution)/shard_map/all_gather | solution.py:112
  181.8 14.3 %copy-start.4 = (s32[2048,2]{0,1:T(2,128)S(1)}, s32[2048,2]{0,1:T(2,128)}, u32[]{:S(2)}) copy-start(s32[2048,2]{0,1:T(2,128)} %param.10) | copy-start | bytes 49156
  181.8 14.7 %copy-start.5 = (s32[2048,2]{0,1:T(2,128)S(1)}, s32[2048,2]{0,1:T(2,128)}, u32[]{:S(2)}) copy-start(s32[2048,2]{0,1:T(2,128)} %param.9) | copy-start | bytes 49156
  472.4 4.8 copy-start
  477.2 4.6 copy-start.1
Sparse Core Ops, SparseCore 0:
  196.2 165.0 all-gather.1
where the time goes:
time: 507 us; the launch traced here: 505 us
  waiting for transfers between devices  162 us (32%)
  other arithmetic  140 us (28%)
  matrix products  76 us (15%)
  local copies, waits for them, and re-layouts  57.2 us (11%)
  blocking collectives  54.5 us (11%)
  between operations  14.3 us (3%)
    all_gather x1, waiting for transfers between devices, body(): everyone = lax.all_gather(turned, 'dev', axis=3, tiled=True)  162 us
    neg x1, other arithmetic, spectrum_table(): return jnp.stack([jnp.cos(angle), -jnp.sin(angle)])  134 us
    dot_general x1, matrix products, channelize(): jnp.einsum('afn,qnk->qfka', framed, table, precision=lax.Precision.HIGHEST)  39.7 us
    all_to_all x1, blocking collectives, body(): lax.all_to_all(half_turn, 'dev', split_axis=4, concat_axis=3, tiled=True)  37 us
    dot_general x8, matrix products, single(): jnp.einsum('pqUu,qfcvu->pfcvU', w_table, aperture, precision=lax.Precisio...  14.9 us
    dynamic_slice x16, local copies, waits for them, and re-layouts, grid_half(): halves = lax.map(single, portions)  12.9 us
    dot_general x8, matrix products, single(): jnp.einsum('qfcva,ua->qfcvu', spread, row_kernel, preferred_element_type=...  12 us
    all_to_all x1, blocking collectives, body(): lax.all_to_all(spectra, 'grp', split_axis=2, concat_axis=3, tiled=True)  10.3 us
  transfers between devices with their start and end apart: 1, of which 1 were waited for; matrix products, arithmetic and copies ran while one was open for 1% of the time, Pallas kernels for 0%

commit v1 on v0

--- a/solution.py
+++ b/solution.py
@@ -4,13 +4,6 @@
 import jax.numpy as jnp
 from jax import lax
 from jax.sharding import PartitionSpec as P
-
-
-def spectrum_table(points, channels):
-    sample_idx = lax.broadcasted_iota(jnp.int32, (points, channels), 0)
-    channel_idx = lax.broadcasted_iota(jnp.int32, (points, channels), 1)
-    angle = (sample_idx * channel_idx % points).astype(jnp.float32) * (2.0 * math.pi / points)
-    return jnp.stack([jnp.cos(angle), -jnp.sin(angle)])
 
 
 def transform_table(length):
@@ -35,12 +28,14 @@
     return (lower + upper).astype(jnp.bfloat16)
 
 
-def group_major(values, groups, members):
-    width = values.shape[1]
-    return values.reshape(groups, members, -1, width).transpose(1, 0, 2, 3).reshape(values.shape)
+def dft_table(length, count, total, scale):
+    sample_idx = lax.broadcasted_iota(jnp.int32, (length, count), 0)
+    channel_idx = lax.broadcasted_iota(jnp.int32, (length, count), 1)
+    angle = (sample_idx * channel_idx * scale % total).astype(jnp.float32) * (2.0 * math.pi / total)
+    return jnp.cos(angle), jnp.sin(angle)
 
 
-def channelize(voltages, filter_taps):
+def channelize(voltages, filter_taps, channels):
     tap_count, points = filter_taps.shape
     dipoles = voltages.shape[0]
     segments = voltages.reshape(dipoles, -1, points)
@@ -50,8 +45,27 @@
         framed = framed + filter_taps[tap_index][None, None, :] * segments[
             :, tap_index : tap_index + frame_count, :
         ].astype(jnp.float32)
-    table = spectrum_table(points, points // 2)
-    spectra = jnp.einsum("afn,qnk->qfka", framed, table, precision=lax.Precision.HIGHEST)
+    outer = 64
+    inner = points // outer
+    kept = channels // outer
+    exact = lax.Precision.HIGHEST
+    pieces = framed.reshape(dipoles, frame_count, outer, inner)
+    cos_a, sin_a = dft_table(outer, outer, outer, 1)
+    first_re = jnp.einsum("afnm,nk->afkm", pieces, cos_a, precision=exact)
+    first_im = -jnp.einsum("afnm,nk->afkm", pieces, sin_a, precision=exact)
+    cos_t, sin_t = dft_table(outer, inner, points, 1)
+    cos_t = cos_t[None, None]
+    sin_t = sin_t[None, None]
+    twist_re = first_re * cos_t + first_im * sin_t
+    twist_im = first_im * cos_t - first_re * sin_t
+    cos_b, sin_b = dft_table(inner, kept, inner, 1)
+    spec_re = jnp.einsum("afkm,mj->fjka", twist_re, cos_b, precision=exact) + jnp.einsum(
+        "afkm,mj->fjka", twist_im, sin_b, precision=exact
+    )
+    spec_im = jnp.einsum("afkm,mj->fjka", twist_im, cos_b, precision=exact) - jnp.einsum(
+        "afkm,mj->fjka", twist_re, sin_b, precision=exact
+    )
+    spectra = jnp.stack([spec_re, spec_im]).reshape(2, frame_count, channels, dipoles)
     return spectra.astype(jnp.bfloat16)
 
 
@@ -104,16 +118,21 @@
     dipoles = dipole_cells.shape[0]
     grid_len = sky_model.shape[2]
     rows_mine = sky_model.shape[1]
-    spectra = channelize(voltages, filter_taps)
+    channels = sky_model.shape[0] * groups
+    spectra = channelize(voltages, filter_taps, channels)
+    parts, frame_count, _, local = spectra.shape
+    block = channels // groups
     w_table = transform_table(grid_len)
     table_upper, table_lower = split_table(w_table)
-    norm_scale = 1.0 / (spectra.shape[1] * dipoles)
-    turned = lax.all_to_all(spectra, "grp", split_axis=2, concat_axis=3, tiled=True)
-    everyone = lax.all_gather(turned, "dev", axis=3, tiled=True)
-    order_cells = group_major(dipole_cells, groups, members)
-    order_bits = group_major(kernel_bits, groups, members)
-    row_kernel = one_hot(order_cells[:, 0], order_bits[:, 0], grid_len)
-    col_full = one_hot(order_cells[:, 1], order_bits[:, 1], grid_len)
+    norm_scale = 1.0 / (frame_count * dipoles)
+    by_block = spectra.reshape(parts, frame_count, groups, block, local).transpose(2, 0, 1, 3, 4)
+    outgoing = jnp.broadcast_to(
+        by_block[:, None], (groups, members, parts, frame_count, block, local)
+    ).reshape(groups * members, parts, frame_count, block, local)
+    incoming = lax.all_to_all(outgoing, ("grp", "dev"), split_axis=0, concat_axis=0, tiled=True)
+    everyone = incoming.transpose(1, 2, 3, 0, 4).reshape(parts, frame_count, block, dipoles)
+    row_kernel = one_hot(dipole_cells[:, 0], kernel_bits[:, 0], grid_len)
+    col_full = one_hot(dipole_cells[:, 1], kernel_bits[:, 1], grid_len)
     col_mine = lax.dynamic_slice_in_dim(col_full, lax.axis_index("dev") * rows_mine, rows_mine, 0)
     half_turn = grid_half(everyone, row_kernel, col_mine, w_table)
     power_sum = image_power(

time: 507 us -> 261 us (0.51)
  other arithmetic: 140 us -> 7.4 us
  waiting for transfers between devices: 162 us -> 50.1 us
  matrix products: 76 us -> 42.2 us
  local copies, waits for them, and re-layouts: 57.2 us -> 82.6 us
  between operations: 14.3 us -> 0.9 us
  starting transfers between devices: 0.04 us -> 11.9 us
  blocking collectives: 54.5 us -> 63.4 us
    all_gather x1 -> x0, waiting for transfers between devices: 162 us -> none  [body(): everyone = lax.all_gather(turned, 'dev', axis=3, tiled=True)]
    neg x1 -> x0, other arithmetic: 134 us -> none  [spectrum_table(): return jnp.stack([jnp.cos(angle), -jnp.sin(angle)])]
    all_to_all x0 -> x1, waiting for transfers between devices: none -> 50.1 us  [body(): lax.all_to_all(outgoing, ('grp', 'dev'), split_axis=0, concat_axis=0, til...]
    dot_general x1 -> x6, matrix products: 39.7 us -> 7.69 us  [the longest x1 1.57 us: channelize(): jnp.einsum('afkm,mj->fjka', twist_re, sin_b, precision=exact)]
    all_to_all x1, blocking collectives: 37 us -> 55.6 us  [body(): lax.all_to_all(half_turn, 'dev', split_axis=4, concat_axis=3, tiled=True)]
    unnamed x15 -> x10, local copies, waits for them, and re-layouts: 6.24 us -> 20.9 us
    dynamic_slice x16 -> x0, local copies, waits for them, and re-layouts: 12.9 us -> none  [grid_half(): halves = lax.map(single, portions)]
    all_to_all x0 -> x1, starting transfers between devices: none -> 11.9 us  [body(): lax.all_to_all(outgoing, ('grp', 'dev'), split_axis=0, concat_axis=0, til...]
where the time goes in v1:
time: 261 us; the launch traced here: 259 us
  local copies, waits for them, and re-layouts  82.6 us (32%)
  blocking collectives  63.4 us (24%)
  waiting for transfers between devices  50.1 us (19%)
  matrix products  42.2 us (16%)
  starting transfers between devices  11.9 us (5%)
  other arithmetic  7.4 us (3%)
    all_to_all x1, blocking collectives, body(): lax.all_to_all(half_turn, 'dev', split_axis=4, concat_axis=3, tiled=True)  55.6 us
    all_to_all x1, waiting for transfers between devices, body(): lax.all_to_all(outgoing, ('grp', 'dev'), split_axis=0, concat_axis=0, til...  50.1 us
    unnamed x10, local copies, waits for them, and re-layouts  20.9 us
    dot_general x8, matrix products, single(): jnp.einsum('pqUu,qfcvu->pfcvU', w_table, aperture, precision=lax.Precisio...  14.9 us
    dot_general x8, matrix products, single(): jnp.einsum('qfcva,ua->qfcvu', spread, row_kernel, preferred_element_type=...  12 us
    all_to_all x1, starting transfers between devices, body(): lax.all_to_all(outgoing, ('grp', 'dev'), split_axis=0, concat_axis=0, til...  11.9 us
    mul x8, local copies, waits for them, and re-layouts, single(): spread = portion[:, :, :, None, :] * col_kernel[None, None, None, :, :]  11.2 us
    another operation x1, local copies, waits for them, and re-layouts, grid_half(): spectra.reshape(parts, frame_count, blocks, span, dipoles)  11.2 us
  transfers between devices with their start and end apart: 1, of which 1 were waited for; matrix products, arithmetic and copies ran while one was open for 1% of the time, Pallas kernels for 0%

profile of v1, /device:TPU:0, one launch (start us, length us, event | category | flops | bytes accessed | tf_op | source)
XLA Modules:
  0.0 258.7 jit_solution(15088007733421116890)
XLA Ops:
  0.8 0.1 fusion.72
  0.9 1.1 fusion.115
  2.0 1.4 reshape.331
  3.4 1.1 fusion.114
  4.6 0.7 multiply_add_fusion.1
  5.2 0.2 reshape.332
  5.5 0.7 fusion.22
  6.2 0.7 convolution_bitcast_fusion.1
  7.1 1.6 fusion.34
  8.6 1.6 fusion.32
  10.2 1.6 fusion.25
  11.9 1.6 fusion.26
  13.7 2.5 broadcast_in_dim.13
  16.3 11.9 %all-to-all-start = ((bf16[128,2,1,512,16]{3,4,1,2,0:T(8,128)(2,1)}), bf16[128,2,1,512,16]{3,4,1,2,0:T(8,128)(2,1)}, u32[]{:S(2)}, u32[]{:S(2)}) async-start(bf16[128,2,1,512,16]{3,4,1,2,0:T(8,128)(2,1)} %bitcast.148), calls=%async_computation | async-start | bytes 8388608 | tf_op jit(solution)/shard_map/all_to_all | solution.py:132
  28.2 1.0 fusion.47
  29.2 1.0 fusion.45
  30.5 50.1 %all-to-all-done = bf16[128,2,1,512,16]{3,4,1,2,0:T(8,128)(2,1)} async-done(((bf16[128,2,1,512,16]{3,4,1,2,0:T(8,128)(2,1)}), bf16[128,2,1,512,16]{3,4,1,2,0:T(8,128)(2,1)}, u32[]{:S(2)}, u32[]{:S(2)}) %all-to-all-start) | async-done | bytes 4194336 | tf_op jit(solution)/shard_map/all_to_all | solution.py:132
  80.6 4.7 %copy.73 = bf16[2,1,512,128,16]{2,4,3,0,1:T(8,128)(2,1)} copy(bf16[2,1,512,128,16]{2,4,0,1,3:T(8,128)(2,1)} %bitcast.23) | data formatting | bytes 8388608 | tf_op jit(solution)/shard_map/transpose | solution.py:133
  85.3 11.2 %reshape_reshape.3 = bf16[2,1,8,64,2048]{3,2,4,0,1:T(8,128)(2,1)} reshape(bf16[2,1,512,128,16]{2,4,3,0,1:T(8,128)(2,1)} %copy.73) | data formatting | bytes 8388608 | tf_op jit(solution)/shard_map/reshape;reshape | solution.py:89
  96.5 14.3 %copy.74 = bf16[8,2,1,64,2048]{4,1,3,2,0:T(2,128)(2,1)} copy(bf16[8,2,1,64,2048]{3,0,4,1,2:T(8,128)(2,1)} %bitcast.147) | data formatting | bytes 8388608
  110.8 45.0 %while.11 = (s32[]{:T(128)}, bf16[8,2,1,64,8,256]{5,4,3,0,1,2:T(8,128)(2,1)}, bf16[8,2,1,64,2048]{4,1,3,2,0:T(2,128)(2,1)}, bf16[8,2048]{1,0:T(8,128)(2,1)S(1)},...) while((s32[]{:T(128)}, ...), condition=%wide.region_1.2_spmd.clone, body=%wide.region_0.1_spmd.clone.sunk | while | flops 2689859584 | bytes 6357109 | solution.py:101
  110.8 1.4 dynamic-slice_bitcast_fusion.2
  112.2 1.5 fusion.133
  113.7 1.9 fusion.134
  115.6 0.8 copy_dynamic-update-slice_fusion.2
  116.4 1.4 dynamic-slice_bitcast_fusion.2
  117.8 1.5 fusion.133
  119.3 1.9 fusion.134
  121.2 0.8 copy_dynamic-update-slice_fusion.2
  122.0 1.4 dynamic-slice_bitcast_fusion.2
  123.5 1.5 fusion.133
  125.0 1.9 fusion.134
  126.8 0.8 copy_dynamic-update-slice_fusion.2
  127.7 1.4 dynamic-slice_bitcast_fusion.2
  129.1 1.5 fusion.133
  130.6 1.9 fusion.134
  132.5 0.8 copy_dynamic-update-slice_fusion.2
  133.3 1.4 dynamic-slice_bitcast_fusion.2
  134.7 1.5 fusion.133
  136.2 1.9 fusion.134
  138.1 0.8 copy_dynamic-update-slice_fusion.2
  138.9 1.4 dynamic-slice_bitcast_fusion.2
  140.3 1.5 fusion.133
  141.8 1.9 fusion.134
  143.7 0.8 copy_dynamic-update-slice_fusion.2
  144.5 1.4 dynamic-slice_bitcast_fusion.2
  146.0 1.5 fusion.133
  147.5 1.9 fusion.134
  149.3 0.8 copy_dynamic-update-slice_fusion.2
  150.2 1.4 dynamic-slice_bitcast_fusion.2
  151.6 1.5 fusion.133
  153.1 1.9 fusion.134
  155.0 0.8 copy_dynamic-update-slice_fusion.2
  155.8 8.6 %copy.76 = bf16[2,1,512,8,256]{2,3,1,0,4:T(8,128)(2,1)} copy(bf16[2,1,512,8,256]{4,3,2,0,1:T(8,128)(2,1)} %bitcast.151) | data formatting | bytes 8388608 | tf_op jit(solution)/shard_map/reshape | solution.py:102
  164.4 55.6 %all_to_all.20 = bf16[2,1,512,8,256]{2,3,1,0,4:T(8,128)(2,1)S(1)} all-to-all(bf16[2,1,512,8,256]{2,3,1,0,4:T(8,128)(2,1)} %copy.76), channel_id=1, replica_groups=mesh['grp'=4,'dev'=32] {'dev'}, dimensions={4} | all-to-all | bytes 8388608 | tf_op jit(solution)/shard_map/all_to_all | solution.py:139
  220.0 2.4 copy.107
  222.4 2.6 %copy.78 = bf16[2,1,512,32,8,8]{2,5,4,3,0,1:T(8,128)(2,1)} copy(bf16[2,1,512,32,8,8]{2,5,3,4,0,1:T(8,128)(2,1)S(1)} %bitcast.149) | data formatting | bytes 8388608 | tf_op jit(solution)/shard_map/all_to_all | solution.py:139
  225.1 7.5 %copy.85 = bf16[2,512,256,8,1]{2,1,0,4,3:T(8,128)(2,1)} copy(bf16[2,512,256,8,1]{1,3,2,0,4:T(8,128)(2,1)} %bitcast.150) | data formatting | bytes 8388608 | tf_op jit(solution)/shard_map/reshape.36
  232.5 4.8 %fusion.29 = f32[512,8,2,256,1]{3,0,4,2,1:T(8,128)S(1)} fusion(bf16[2,512,256,8,1]{2,1,0,4,3:T(8,128)(2,1)} %copy.85, f32[1,2,256,256]{3,2,1,0:T(8,128)S(1)} %get-tuple-element.146, f32[1,2,256,256]{3,2,1,0:T(8,128)S(1)} %get-tuple-element.145), kind=kOutput, calls=%fused_computation.41 | convolution fusion | flops 2148532224 | bytes 13631488 | tf_op jit(solution)/shard_map/tksw,khnwm->thnms/dot_general | solution.py:108
  237.4 2.7 %fusion.21 = f32[512,8,256]{2,0,1:T(8,128)S(1)} fusion(f32[512,8,2,256,1]{3,0,4,2,1:T(8,128)S(1)} %fusion.29, bf16[2,512,256,8,1]{2,1,0,4,3:T(8,128)(2,1)S(1)} %copy-done, f32[1,2,256,256]{3,2,1,0:T(8,128)S(1)} %get-tuple-element.146, f32[1,2,256,256]{3,2,1,0:T(8,128)S(1)} %get-tuple-element.145), kind=kOutput, calls=%fused_computation.24 | convolution fusion | flops 2154037248 | bytes 17825792 | tf_op jit(solution)/shard_map/tksw,khnwm->thnms/dot_general | solution.py:109
  240.1 3.5 %fusion.113 = (f32[8,256]{1,0:T(8,128)S(1)}, f32[512,8,256]{2,0,1:T(8,128)}) fusion(f32[512,8,256]{2,1,0:T(8,128)S(1)} %copy-done.1, f32[512,8,256]{2,0,1:T(8,128)S(1)} %fusion.21), kind=kLoop, calls=%fused_computation.152 | loop fusion | flops 3143680 | bytes 12591104 | tf_op jit(solution)/shard_map/reduce_sum | solution.py:147
  243.6 7.8 %psum.7 = f32[8,256]{1,0:T(8,128)S(1)} all-reduce(f32[8,256]{1,0:T(8,128)S(1)} %get-tuple-element.139), channel_id=1, replica_groups=mesh['grp'=4,'dev'=32] {'grp'}, use_global_device_ids=true, to_apply=%region_4.5 | all-reduce | flops 2048 | bytes 16384 | tf_op jit(solution)/shard_map/psum | solution.py:147
  251.4 0.6 broadcast_multiply_fusion
  252.0 6.6 %copy.82 = f32[512,8,256]{2,1,0:T(8,128)} copy(f32[512,8,256]{2,0,1:T(8,128)} %get-tuple-element.140) | data formatting | bytes 8388608
  (23 shorter events, 0.9 us)
Async XLA Ops:
  16.3 64.4 %all-to-all-start = ((bf16[128,2,1,512,16]{3,4,1,2,0:T(8,128)(2,1)}), bf16[128,2,1,512,16]{3,4,1,2,0:T(8,128)(2,1)}, u32[]{:S(2)}, u32[]{:S(2)}) async-start(bf16[128,2,1,512,16]{3,4,1,2,0:T(8,128)(2,1)} %bitcast.148), calls=%async_computation | async-start | bytes 8388608 | tf_op jit(solution)/shard_map/all_to_all | solution.py:132
  28.2 2.2 copy-start.2
  28.2 2.3 copy-start.3
  232.5 4.8 %copy-start = (bf16[2,512,256,8,1]{2,1,0,4,3:T(8,128)(2,1)S(1)}, bf16[2,512,256,8,1]{2,1,0,4,3:T(8,128)(2,1)}, u32[]{:S(2)}) copy-start(bf16[2,512,256,8,1]{2,1,0,4,3:T(8,128)(2,1)} %copy.85) | copy-start | bytes 12582916
  237.4 2.7 %copy-start.1 = (f32[512,8,256]{2,1,0:T(8,128)S(1)}, f32[512,8,256]{2,1,0:T(8,128)}, u32[]{:S(2)}) copy-start(f32[512,8,256]{2,1,0:T(8,128)} %param.11) | copy-start | bytes 12582916

commit v2 on v1

v2 whole, which is shorter than its diff:
```python
import math

import jax
import jax.numpy as jnp
from jax import lax
from jax.sharding import PartitionSpec as P


def dft_table(length, count, total, scale):
    sample_idx = lax.broadcasted_iota(jnp.int32, (length, count), 0)
    channel_idx = lax.broadcasted_iota(jnp.int32, (length, count), 1)
    angle = (sample_idx * channel_idx * scale % total).astype(jnp.float32) * (2.0 * math.pi / total)
    return jnp.cos(angle), jnp.sin(angle)


def channelize(voltages, filter_taps, channels):
    tap_count, points = filter_taps.shape
    dipoles = voltages.shape[0]
    segments = voltages.reshape(dipoles, -1, points)
    frame_count = segments.shape[1] - tap_count + 1
    framed = jnp.zeros((dipoles, frame_count, points), jnp.float32)
    for tap_index in range(tap_count):
        framed = framed + filter_taps[tap_index][None, None, :] * segments[
            :, tap_index : tap_index + frame_count, :
        ].astype(jnp.float32)
    outer = 64
    inner = points // outer
    kept = channels // outer
    exact = lax.Precision.HIGHEST
    pieces = framed.reshape(dipoles, frame_count, outer, inner)
    cos_a, sin_a = dft_table(outer, outer, outer, 1)
    first_re = jnp.einsum("afnm,nk->afkm", pieces, cos_a, precision=exact)
    first_im = -jnp.einsum("afnm,nk->afkm", pieces, sin_a, precision=exact)
    cos_t, sin_t = dft_table(outer, inner, points, 1)
    cos_t = cos_t[None, None]
    sin_t = sin_t[None, None]
    twist_re = first_re * cos_t + first_im * sin_t
    twist_im = first_im * cos_t - first_re * sin_t
    cos_b, sin_b = dft_table(inner, kept, inner, 1)
    spec_re = jnp.einsum("afkm,mj->fajk", twist_re, cos_b, precision=exact) + jnp.einsum(
        "afkm,mj->fajk", twist_im, sin_b, precision=exact
    )
    spec_im = jnp.einsum("afkm,mj->fajk", twist_im, cos_b, precision=exact) - jnp.einsum(
        "afkm,mj->fajk", twist_re, sin_b, precision=exact
    )
    spectra = jnp.stack([spec_re, spec_im]).reshape(2, frame_count, dipoles, channels)
    return spectra.astype(jnp.bfloat16)


def row_phases(cells, bits, rows, grid_len):
    scale = 2.0 * math.pi / grid_len
    near = (cells[:, None] * rows[None, :] % grid_len).astype(jnp.float32) * scale
    far = ((cells[:, None] + 1) * rows[None, :] % grid_len).astype(jnp.float32) * scale
    low = (bits % 2).astype(jnp.float32)[:, None]
    high = (bits // 2).astype(jnp.float32)[:, None]
    real = low * jnp.cos(near) + high * jnp.cos(far)
    imag = -(low * jnp.sin(near) + high * jnp.sin(far))
    return real, imag


def column_weights(cells, bits, grid_len):
    cols = lax.broadcasted_iota(jnp.int32, (cells.shape[0], grid_len), 1)
    lower = (cols == cells[:, None]) * (bits % 2)[:, None]
    upper = (cols == cells[:, None] + 1) * (bits // 2)[:, None]
    return (lower + upper).astype(jnp.float32)


def column_transform(grid_len):
    out_idx = lax.broadcasted_iota(jnp.int32, (grid_len, grid_len), 0)
    in_idx = lax.broadcasted_iota(jnp.int32, (grid_len, grid_len), 1)
    angle = (out_idx * in_idx % grid_len).astype(jnp.float32) * (2.0 * math.pi / grid_len)
    cosine = jnp.cos(angle)
    sine = jnp.sin(angle)
    return jnp.concatenate(
        [jnp.concatenate([cosine, -sine], axis=1), jnp.concatenate([sine, cosine], axis=1)], axis=0
    )


def body(voltages, filter_taps, dipole_cells, kernel_bits, sky_model):
    groups = lax.axis_size("grp")
    members = lax.axis_size("dev")
    dipoles = dipole_cells.shape[0]
    grid_len = sky_model.shape[2]
    rows_mine = sky_model.shape[1]
    channels = sky_model.shape[0] * groups
    spectra = channelize(voltages, filter_taps, channels)
    parts, frame_count, local, _ = spectra.shape
    block = channels // groups
    by_block = spectra.reshape(parts, frame_count, local, groups, block).transpose(3, 0, 1, 2, 4)
    outgoing = jnp.broadcast_to(
        by_block[:, None], (groups, members, parts, frame_count, local, block)
    ).reshape(groups * members, parts, frame_count, local, block)
    incoming = lax.all_to_all(outgoing, ("grp", "dev"), split_axis=0, concat_axis=0, tiled=True)
    rows = lax.axis_index("dev") * rows_mine + lax.broadcasted_iota(jnp.int32, (rows_mine,), 0)
    phase_re, phase_im = row_phases(dipole_cells[:, 0], kernel_bits[:, 0], rows, grid_len)
    col_w = column_weights(dipole_cells[:, 1], kernel_bits[:, 1], grid_len)
    spread = jnp.stack(
        [phase_re[:, :, None] * col_w[:, None, :], phase_im[:, :, None] * col_w[:, None, :]], axis=1
    ).astype(jnp.bfloat16)
    spread = spread.reshape(groups * members, local, 2 * rows_mine * grid_len)
    products = jnp.einsum(
        "sqfak,saj->qfkj", incoming, spread, preferred_element_type=jnp.float32
    ).reshape(parts, frame_count, block, 2, rows_mine, grid_len)
    half_re = products[0, :, :, 0] - products[1, :, :, 1]
    half_im = products[0, :, :, 1] + products[1, :, :, 0]
    halves = jnp.concatenate([half_re, half_im], axis=-1)
    sky_image = jnp.einsum(
        "fkmv,vw->fkmw", halves, column_transform(grid_len), precision=lax.Precision.HIGH
    )
    norm_scale = 1.0 / (frame_count * dipoles)
    power_sum = jnp.sum(sky_image * sky_image, axis=0)
    power_sum = (power_sum[..., :grid_len] + power_sum[..., grid_len:]) * norm_scale
    residual_images = power_sum - sky_model
    channel_total = residual_images.shape[0] * groups
    broadband = lax.psum(jnp.sum(residual_images, axis=0), "grp") / channel_total
    return (residual_images, broadband)


def solution(mesh):
    in_specs = (P(("grp", "dev"), None), P(), P(), P(), P("grp", "dev", None))
    out_specs = (P("grp", "dev", None), P("dev", None))
    return jax.shard_map(body, mesh=mesh, in_specs=in_specs, out_specs=out_specs, check_vma=False)
```

time: 261 us -> 158 us (0.61)
  blocking collectives: 63.4 us -> 9.17 us
  waiting for transfers between devices: 50.1 us -> 0.01 us
  other arithmetic: 7.4 us -> 28.2 us
  local copies, waits for them, and re-layouts: 82.6 us -> 69.4 us
  matrix products: 42.2 us -> 36.8 us
    all_to_all x1 -> x0, blocking collectives: 55.6 us -> none  [body(): lax.all_to_all(half_turn, 'dev', split_axis=4, concat_axis=3, tiled=True)]
    all_to_all x1, waiting for transfers between devices: 50.1 us -> 0.01 us  [body(): lax.all_to_all(outgoing, ('grp', 'dev'), split_axis=0, concat_axis=0, til...]
    convert_element_type x0 -> x1, local copies, waits for them, and re-layouts: none -> 25.6 us  [body(): spread = jnp.stack([phase_re[:, :, None] * col_w[:, None, :], phase_im[:,...]
    dot_general x0 -> x1, local copies, waits for them, and re-layouts: none -> 24 us  [body(): jnp.einsum('sqfak,saj->qfkj', incoming, spread, preferred_element_type=jn...]
    another operation x5 -> x3, local copies, waits for them, and re-layouts: 19.1 us -> 0.47 us  [the longest x2 0.26 us: channelize(): jnp.stack([spec_re, spec_im]).reshape(2, frame_count, dipoles, channels)]
    unnamed x10 -> x7, local copies, waits for them, and re-layouts: 20.9 us -> 4.45 us
    another operation x2, other arithmetic: 0.17 us -> 16 us  [transform_table(): return jnp.stack([jnp.stack([cosine, sine]), jnp.stack([-sine, cosine])])]
    mul x8 -> x0, local copies, waits for them, and re-layouts: 11.2 us -> none  [single(): spread = portion[:, :, :, None, :] * col_kernel[None, None, None, :, :]]
  transfers between devices with their start and end apart: 1 -> 1, of which waited for: 1 -> 0; matrix products, arithmetic and copies ran while one was open for 1% -> 45% of each run, Pallas kernels for 0% -> 0%
where the time goes in v2:
time: 158 us; the launch traced here: 156 us
  local copies, waits for them, and re-layouts  69.4 us (44%)
  matrix products  36.8 us (23%)
  other arithmetic  28.2 us (18%)
  starting transfers between devices  11.9 us (8%)
  blocking collectives  9.17 us (6%)
    convert_element_type x1, local copies, waits for them, and re-layouts, body(): spread = jnp.stack([phase_re[:, :, None] * col_w[:, None, :], phase_im[:,...  25.6 us
    dot_general x1, local copies, waits for them, and re-layouts, body(): jnp.einsum('sqfak,saj->qfkj', incoming, spread, preferred_element_type=jn...  24 us
    dot_general x1, matrix products, body(): jnp.einsum('sqfak,saj->qfkj', incoming, spread, preferred_element_type=jn...  21.9 us
    all_to_all x1, starting transfers between devices, body(): lax.all_to_all(outgoing, ('grp', 'dev'), split_axis=0, concat_axis=0, til...  11.9 us
    another operation x1, other arithmetic  9.27 us
    psum x1, blocking collectives, body(): lax.psum(jnp.sum(residual_images, axis=0), 'grp') / channel_total  9.17 us
    all_to_all x1, local copies, waits for them, and re-layouts, body(): lax.all_to_all(outgoing, ('grp', 'dev'), split_axis=0, concat_axis=0, til...  7.86 us
    dot_general x1, matrix products, body(): jnp.einsum('fkmv,vw->fkmw', halves, column_transform(grid_len), precision...  7.27 us
  transfers between devices with their start and end apart: 1, of which 0 were waited for; matrix products, arithmetic and copies ran while one was open for 45% of the time, Pallas kernels for 0%

profile of v2, /device:TPU:0, one launch (start us, length us, event | category | flops | bytes accessed | tf_op | source)
XLA Modules:
  0.0 156.4 jit_solution(15429447887228727846)
XLA Ops:
  0.6 1.4 reshape.473
  2.1 1.1 fusion.108
  3.2 1.1 fusion.109
  4.3 0.7 multiply_add_fusion.1
  4.9 0.2 reshape.474
  5.2 0.7 convolution_bitcast_fusion
  5.9 0.7 fusion.12
  6.6 0.1 fusion.67
  6.8 0.1 fusion.66
  6.9 0.1 copy.66
  7.0 0.1 copy.67
  7.1 1.6 %fusion.24 = f32[32,16,64]{2,0,1:T(8,128)S(1)} fusion(f32[64,16,1,64]{3,0,1,2:T(8,128)S(1)} %fusion.12, f32[64,16,1,64]{3,0,1,2:T(8,128)S(1)} %convolution_bitcast_fusion, f32[64,64]{1,0:T(8,128)S(1)} %copy.67, f32[64,64]{1,0:T(8,128)S(1)} %copy.66), kind=kOutput, calls=%fused_computation.39 | convolution fusion | flops 25391104 | bytes 688128 | tf_op jit(solution)/shard_map/afkm,mj->fajk/dot_general | solution.py:40
  8.7 1.6 fusion.26
  10.2 1.6 %fusion.16 = bf16[1,16,32,64]{3,2,1,0:T(8,128)(2,1)S(1)} fusion(f32[32,16,64]{2,0,1:T(8,128)S(1)} %fusion.24, f32[64,16,1,64]{3,0,1,2:T(8,128)S(1)} %convolution_bitcast_fusion, f32[64,16,1,64]{3,0,1,2:T(8,128)S(1)} %fusion.12, f32[64,64]{1,0:T(8,128)S(1)} %copy.67, f32[64,64]{1,0:T(8,128)S(1)} %copy.66), kind=kOutput, calls=%fused_computation.30 | convolution fusion | flops 25456640 | bytes 753664 | tf_op jit(solution)/shard_map/afkm,mj->fajk/dot_general | solution.py:40
  11.8 0.1 stack.15
  11.9 1.6 %fusion.15 = bf16[1,16,32,64]{3,2,1,0:T(8,128)(2,1)S(1)} fusion(f32[32,16,64]{2,0,1:T(8,128)S(1)} %fusion.26, f32[64,16,1,64]{3,0,1,2:T(8,128)S(1)} %fusion.12, f32[64,16,1,64]{3,0,1,2:T(8,128)S(1)} %convolution_bitcast_fusion, f32[64,64]{1,0:T(8,128)S(1)} %copy.67, f32[64,64]{1,0:T(8,128)S(1)} %copy.66), kind=kOutput, calls=%fused_computation.29 | convolution fusion | flops 25456640 | bytes 753664 | tf_op jit(solution)/shard_map/afkm,mj->fajk/dot_general | solution.py:43
  13.5 0.1 stack.16
  13.6 0.1 maximum_bitcast_fusion.6
  13.8 2.5 %broadcast_in_dim.7 = bf16[4,32,2,16,512]{4,3,2,1,0:T(8,128)(2,1)} broadcast(bf16[4,2,16,512]{3,2,1,0:T(8,128)(2,1)S(1)} %copy.68), dimensions={0,2,3,4} | broadcast | bytes 4325376 | tf_op jit(solution)/shard_map/broadcast_in_dim | solution.py:90
  16.3 0.0 copy-start.1
  16.3 0.0 copy-start.2
  16.3 11.9 %all-to-all-start = ((bf16[128,2,1,16,512]{4,3,1,2,0:T(8,128)(2,1)}), bf16[128,2,1,16,512]{4,3,1,2,0:T(8,128)(2,1)}, u32[]{:S(2)}, u32[]{:S(2)}) async-start(bf16[128,2,1,16,512]{4,3,1,2,0:T(8,128)(2,1)} %bitcast.107), calls=%async_computation | async-start | bytes 8388608 | tf_op jit(solution)/shard_map/all_to_all | solution.py:93
  28.2 0.0 copy-done.1
  28.2 0.1 and_select_fusion.1
  28.3 0.0 copy-done.2
  28.3 0.1 and_select_fusion
  28.4 0.6 multiply_add_fusion.4
  29.0 0.3 copy.71
  29.4 0.3 copy.72
  29.7 1.2 add_convert_fusion
  30.9 9.3 %multiply_convert_fusion.1 = (bf16[2048,1,8,256]{3,2,1,0:T(8,128)(2,1)S(1)}, bf16[2048,1,8,256]{3,2,1,0:T(8,128)(2,1)S(1)}) fusion(f32[2048,256]{1,0:T(8,128)S(1)} %add_convert_fusion, f32[2048,8]{1,0:T(8,128)S(1)} %copy.71, f32[2048,8]{1,0:T(8,128)S(1)} %copy.72), kind=kLoop, calls=%fused_computation.5 | loop fusion | flops 16777216 | bytes 19005440 | tf_op jit(solution)/shard_map/convert
  40.1 6.7 %pad_maximum_fusion = bf16[2048,2,8,256]{3,2,1,0:T(8,128)(2,1)} fusion(bf16[2048,1,8,256]{3,2,1,0:T(8,128)(2,1)S(1)} %get-tuple-element.21, bf16[2048,1,8,256]{3,2,1,0:T(8,128)(2,1)S(1)} %get-tuple-element.20), kind=kLoop, calls=%fused_computation | loop fusion | flops 8388608 | bytes 33554432 | tf_op jit(solution)/shard_map/stack | solution.py:97
  46.8 25.6 %convert_element_type.121 = bf16[128,16,4096]{2,1,0:T(8,128)(2,1)} reshape(bf16[2048,2,8,256]{3,2,1,0:T(8,128)(2,1)} %pad_maximum_fusion) | data formatting | bytes 33554432 | tf_op jit(solution)/shard_map/convert_element_type | solution.py:99
  72.4 24.0 %copy.73 = bf16[4096,16,128]{2,1,0:T(8,128)(2,1)} copy(bf16[4096,16,128]{0,1,2:T(8,128)(2,1)} %bitcast.103) | data formatting | bytes 33554432 | tf_op jit(solution)/shard_map/sqfak,saj->qfkj/dot_general | solution.py:101
  96.5 1.0 fusion.37
  97.4 1.7 %fusion.35 = (f32[256,256]{1,0:T(8,128)S(1)}, f32[256,256]{1,0:T(8,128)}) fusion(), kind=kLoop, calls=%fused_computation.57 | loop fusion | flops 917504 | bytes 524288 | tf_op jit(solution)/shard_map/sin | solution.py:73
  99.2 0.0 all-to-all-done
  99.2 7.9 %copy.70 = bf16[128,2,1,16,512]{0,4,3,1,2:T(8,128)(2,1)} copy(bf16[128,2,1,16,512]{4,3,1,2,0:T(8,128)(2,1)} %all-to-all-done) | data formatting | bytes 8388608 | tf_op jit(solution)/shard_map/all_to_all | solution.py:93
  107.0 21.9 %fusion = f32[2,512,2,8,256,1]{1,4,5,3,2,0:T(8,128)S(1)} fusion(bf16[2,8,256,16,128]{4,3,2,1,0:T(8,128)(2,1)} %bitcast.106, bf16[128,2,1,16,512]{0,4,3,1,2:T(8,128)(2,1)} %copy.70), kind=kOutput, calls=%fused_computation.1 | convolution fusion | flops 17179869184 | bytes 37748736 | tf_op jit(solution)/shard_map/sqfak,saj->qfkj/dot_general | solution.py:101
  128.9 1.0 fusion.8
  129.9 0.0 copy-start
  129.9 1.0 fusion.9
  130.9 0.0 copy-done
  131.0 7.3 %fusion.11 = f32[512,8,512]{2,0,1:T(8,128)S(1)} fusion(f32[1,512,8,256]{1,3,2,0:T(8,128)S(1)} %fusion.8, f32[1,512,8,256]{1,3,2,0:T(8,128)S(1)} %fusion.9, f32[256,256]{1,0:T(8,128)S(1)} %copy-done, f32[256,256]{1,0:T(8,128)S(1)} %get-tuple-element.40, f32[256,256]{1,0:T(8,128)S(1)} %fusion.37), kind=kOutput, calls=%fused_computation.18 | convolution fusion | flops 6447431680 | bytes 17563648 | tf_op jit(solution)/shard_map/fkmv,vw->fkmw/dot_general | solution.py:107
  138.2 3.9 %fusion.106 = (f32[8,256]{1,0:T(8,128)S(1)}, f32[512,8,256]{2,0,1:T(8,128)S(1)}) fusion(f32[512,8,256]{2,1,0:T(8,128)} %param.9, f32[512,8,512]{2,0,1:T(8,128)S(1)} %fusion.11), kind=kLoop, calls=%fused_computation.157 | loop fusion | flops 4192256 | bytes 16785408 | tf_op jit(solution)/shard_map/reduce_sum | solution.py:115
  142.2 4.4 %copy.79 = f32[512,8,256]{2,1,0:T(8,128)} copy(f32[512,8,256]{2,0,1:T(8,128)S(1)} %get-tuple-element.15) | data formatting | bytes 8388608
  146.6 9.2 %psum.7 = f32[8,256]{1,0:T(8,128)S(1)} all-reduce(f32[8,256]{1,0:T(8,128)S(1)} %get-tuple-element.14), channel_id=1, replica_groups=mesh['grp'=4,'dev'=32] {'grp'}, use_global_device_ids=true, to_apply=%region_1.2 | all-reduce | flops 2048 | bytes 16384 | tf_op jit(solution)/shard_map/psum | solution.py:115
  155.8 0.6 broadcast_multiply_fusion
  (3 shorter events, 0.1 us)
Async XLA Ops:
  16.3 11.9 %copy-start.1 = (s32[2048,2]{0,1:T(2,128)S(1)}, s32[2048,2]{0,1:T(2,128)}, u32[]{:S(2)}) copy-start(s32[2048,2]{0,1:T(2,128)} %param.8) | copy-start | bytes 49156
  16.3 12.0 %copy-start.2 = (s32[2048,2]{0,1:T(2,128)S(1)}, s32[2048,2]{0,1:T(2,128)}, u32[]{:S(2)}) copy-start(s32[2048,2]{0,1:T(2,128)} %param.7) | copy-start | bytes 49156
  16.3 82.9 %all-to-all-start = ((bf16[128,2,1,16,512]{4,3,1,2,0:T(8,128)(2,1)}), bf16[128,2,1,16,512]{4,3,1,2,0:T(8,128)(2,1)}, u32[]{:S(2)}, u32[]{:S(2)}) async-start(bf16[128,2,1,16,512]{4,3,1,2,0:T(8,128)(2,1)} %bitcast.107), calls=%async_computation | async-start | bytes 8388608 | tf_op jit(solution)/shard_map/all_to_all | solution.py:93
  129.9 1.0 copy-start

commit v3 on v2

--- a/solution.py
+++ b/solution.py
@@ -4,6 +4,8 @@
 import jax.numpy as jnp
 from jax import lax
 from jax.sharding import PartitionSpec as P
+
+CHUNKS = 1
 
 
 def dft_table(length, count, total, scale):
@@ -76,6 +78,30 @@
     )
 
 
+def image_chunk(incoming, spread, transform, sky_part, parts, frame_count, rows_mine, grid_len, norm_scale):
+    _, _, span, sources, local = incoming.shape
+    stacked = incoming.reshape(parts * frame_count, span, sources * local)
+    products = jnp.einsum(
+        "xkd,dj->xkj", stacked, spread, preferred_element_type=jnp.float32
+    ).reshape(parts, frame_count, span, 2, rows_mine, grid_len)
+    half_re = products[0, :, :, 0] - products[1, :, :, 1]
+    half_im = products[0, :, :, 1] + products[1, :, :, 0]
+    halves = jnp.concatenate([half_re, half_im], axis=-1)
+    sky_image = jnp.einsum("fkmv,vw->fkmw", halves, transform, precision=lax.Precision.HIGH)
+    power_sum = jnp.sum(sky_image * sky_image, axis=0)
+    power_sum = (power_sum[..., :grid_len] + power_sum[..., grid_len:]) * norm_scale
+    return power_sum - sky_part
+
+
+def group_sum(value, groups):
+    stride = 1
+    while stride < groups:
+        pairs = [(i, i ^ stride) for i in range(groups)]
+        value = value + lax.ppermute(value, "grp", pairs)
+        stride = stride * 2
+    return value
+
+
 def body(voltages, filter_taps, dipole_cells, kernel_bits, sky_model):
     groups = lax.axis_size("grp")
     members = lax.axis_size("dev")
@@ -86,33 +112,34 @@
     spectra = channelize(voltages, filter_taps, channels)
     parts, frame_count, local, _ = spectra.shape
     block = channels // groups
-    by_block = spectra.reshape(parts, frame_count, local, groups, block).transpose(3, 0, 1, 2, 4)
-    outgoing = jnp.broadcast_to(
-        by_block[:, None], (groups, members, parts, frame_count, local, block)
-    ).reshape(groups * members, parts, frame_count, local, block)
-    incoming = lax.all_to_all(outgoing, ("grp", "dev"), split_axis=0, concat_axis=0, tiled=True)
+    chunks = CHUNKS
+    span = block // chunks
+    by_block = spectra.reshape(parts, frame_count, local, groups, chunks, span)
     rows = lax.axis_index("dev") * rows_mine + lax.broadcasted_iota(jnp.int32, (rows_mine,), 0)
     phase_re, phase_im = row_phases(dipole_cells[:, 0], kernel_bits[:, 0], rows, grid_len)
     col_w = column_weights(dipole_cells[:, 1], kernel_bits[:, 1], grid_len)
     spread = jnp.stack(
         [phase_re[:, :, None] * col_w[:, None, :], phase_im[:, :, None] * col_w[:, None, :]], axis=1
     ).astype(jnp.bfloat16)
-    spread = spread.reshape(groups * members, local, 2 * rows_mine * grid_len)
-    products = jnp.einsum(
-        "sqfak,saj->qfkj", incoming, spread, preferred_element_type=jnp.float32
-    ).reshape(parts, frame_count, block, 2, rows_mine, grid_len)
-    half_re = products[0, :, :, 0] - products[1, :, :, 1]
-    half_im = products[0, :, :, 1] + products[1, :, :, 0]
-    halves = jnp.concatenate([half_re, half_im], axis=-1)
-    sky_image = jnp.einsum(
-        "fkmv,vw->fkmw", halves, column_transform(grid_len), precision=lax.Precision.HIGH
-    )
+    spread = spread.reshape(dipoles, 2 * rows_mine * grid_len)
+    transform = column_transform(grid_len)
     norm_scale = 1.0 / (frame_count * dipoles)
-    power_sum = jnp.sum(sky_image * sky_image, axis=0)
-    power_sum = (power_sum[..., :grid_len] + power_sum[..., grid_len:]) * norm_scale
-    residual_images = power_sum - sky_model
+    results = []
+    for chunk in range(chunks):
+        piece = by_block[:, :, :, :, chunk].transpose(0, 1, 4, 3, 2)
+        outgoing = jnp.broadcast_to(
+            piece[:, :, :, :, None], (parts, frame_count, span, groups, members, local)
+        ).reshape(parts, frame_count, span, groups * members, local)
+        incoming = lax.all_to_all(outgoing, ("grp", "dev"), split_axis=3, concat_axis=3, tiled=True)
+        sky_part = sky_model[chunk * span : (chunk + 1) * span]
+        results.append(
+            image_chunk(
+                incoming, spread, transform, sky_part, parts, frame_count, rows_mine, grid_len, norm_scale
+            )
+        )
+    residual_images = jnp.concatenate(results, axis=0)
     channel_total = residual_images.shape[0] * groups
-    broadband = lax.psum(jnp.sum(residual_images, axis=0), "grp") / channel_total
+    broadband = group_sum(jnp.sum(residual_images, axis=0), groups) / channel_total
     return (residual_images, broadband)
 
 

time: 158 us -> 130 us (0.82)
  local copies, waits for them, and re-layouts: 69.4 us -> 17.4 us
  waiting for transfers between devices: 0.01 us -> 39.4 us
  blocking collectives: 9.17 us -> 0 us
  other arithmetic: 28.2 us -> 21.8 us
    all_to_all x1, waiting for transfers between devices: 0.01 us -> 38.3 us  [body(): lax.all_to_all(outgoing, ('grp', 'dev'), split_axis=3, concat_axis=3, til...]
    convert_element_type x1 -> x0, local copies, waits for them, and re-layouts: 25.6 us -> none  [body(): spread = jnp.stack([phase_re[:, :, None] * col_w[:, None, :], phase_im[:,...]
    dot_general x1 -> x0, local copies, waits for them, and re-layouts: 24 us -> none  [body(): jnp.einsum('sqfak,saj->qfkj', incoming, spread, preferred_element_type=jn...]
    psum x1 -> x0, blocking collectives: 9.17 us -> none  [body(): lax.psum(jnp.sum(residual_images, axis=0), 'grp') / channel_total]
    another operation x2 -> x1, other arithmetic: 16 us -> 10.3 us
    all_to_all x1, local copies, waits for them, and re-layouts: 7.86 us -> 5.01 us  [body(): lax.all_to_all(outgoing, ('grp', 'dev'), split_axis=3, concat_axis=3, til...]
    unnamed x7 -> x9, local copies, waits for them, and re-layouts: 4.45 us -> 5.6 us
  transfers between devices with their start and end apart: 1 -> 3, of which waited for: 0 -> 2; matrix products, arithmetic and copies ran while one was open for 45% -> 14% of each run, Pallas kernels for 0% -> 0%
where the time goes in v3:
time: 130 us; the launch traced here: 129 us
  waiting for transfers between devices  39.4 us (30%)
  matrix products  36.4 us (28%)
  other arithmetic  21.8 us (17%)
  local copies, waits for them, and re-layouts  17.4 us (13%)
  starting transfers between devices  13.4 us (10%)
    all_to_all x1, waiting for transfers between devices, body(): lax.all_to_all(outgoing, ('grp', 'dev'), split_axis=3, concat_axis=3, til...  38.3 us
    dot_general x1, matrix products, image_chunk(): jnp.einsum('xkd,dj->xkj', stacked, spread, preferred_element_type=jnp.flo...  21.4 us
    all_to_all x1, starting transfers between devices, body(): lax.all_to_all(outgoing, ('grp', 'dev'), split_axis=3, concat_axis=3, til...  11.9 us
    another operation x1, other arithmetic  10.3 us
    dot_general x1, matrix products, image_chunk(): jnp.einsum('fkmv,vw->fkmw', halves, transform, precision=lax.Precision.HIGH)  7.26 us
    unnamed x9, local copies, waits for them, and re-layouts  5.6 us
    all_to_all x1, local copies, waits for them, and re-layouts, body(): lax.all_to_all(outgoing, ('grp', 'dev'), split_axis=3, concat_axis=3, til...  5.01 us
    reduce_sum x1, other arithmetic, body(): jnp.sum(residual_images, axis=0)  3.94 us
  transfers between devices with their start and end apart: 3, of which 2 were waited for; matrix products, arithmetic and copies ran while one was open for 14% of the time, Pallas kernels for 0%

profile of v3, /device:TPU:0, one launch (start us, length us, event | category | flops | bytes accessed | tf_op | source)
XLA Modules:
  0.0 129.2 jit_solution(7218692429357967542)
XLA Ops:
  0.6 1.4 %reshape.471 = bf16[16,4,4096]{2,1,0:T(4,128)(2,1)S(1)} reshape(bf16[16,16384]{1,0:T(8,128)(2,1)} %param.5) | data formatting | bytes 1048576 | tf_op jit(solution)/shard_map/reshape | solution.py:21
  2.1 1.1 fusion.108
  3.2 1.1 fusion.109
  4.3 0.7 multiply_add_fusion.1
  4.9 0.2 reshape.472
  5.2 0.7 convolution_bitcast_fusion
  5.9 0.7 fusion.11
  6.6 0.1 fusion.66
  6.8 0.1 fusion.65
  6.9 0.1 copy.48
  7.0 0.1 copy.49
  7.1 1.6 %fusion.23 = f32[32,16,64]{2,0,1:T(8,128)S(1)} fusion(f32[64,16,1,64]{3,0,1,2:T(8,128)S(1)} %fusion.11, f32[64,16,1,64]{3,0,1,2:T(8,128)S(1)} %convolution_bitcast_fusion, f32[64,64]{1,0:T(8,128)S(1)} %copy.49, f32[64,64]{1,0:T(8,128)S(1)} %copy.48), kind=kOutput, calls=%fused_computation.38 | convolution fusion | flops 25391104 | bytes 688128 | tf_op jit(solution)/shard_map/afkm,mj->fajk/dot_general | solution.py:42
  8.7 1.6 %fusion.25 = f32[32,16,64]{2,0,1:T(8,128)S(1)} fusion(f32[64,16,1,64]{3,0,1,2:T(8,128)S(1)} %convolution_bitcast_fusion, f32[64,16,1,64]{3,0,1,2:T(8,128)S(1)} %fusion.11, f32[64,64]{1,0:T(8,128)S(1)} %copy.49, f32[64,64]{1,0:T(8,128)S(1)} %copy.48), kind=kOutput, calls=%fused_computation.40 | convolution fusion | flops 25391104 | bytes 688128 | tf_op jit(solution)/shard_map/afkm,mj->fajk/dot_general | solution.py:45
  10.2 1.6 %fusion.15 = bf16[1,16,32,64]{3,2,1,0:T(8,128)(2,1)S(1)} fusion(f32[32,16,64]{2,0,1:T(8,128)S(1)} %fusion.23, f32[64,16,1,64]{3,0,1,2:T(8,128)S(1)} %convolution_bitcast_fusion, f32[64,16,1,64]{3,0,1,2:T(8,128)S(1)} %fusion.11, f32[64,64]{1,0:T(8,128)S(1)} %copy.49, f32[64,64]{1,0:T(8,128)S(1)} %copy.48), kind=kOutput, calls=%fused_computation.29 | convolution fusion | flops 25456640 | bytes 753664 | tf_op jit(solution)/shard_map/afkm,mj->fajk/dot_general | solution.py:42
  11.8 0.1 stack.15
  11.9 1.6 %fusion.14 = bf16[1,16,32,64]{3,2,1,0:T(8,128)(2,1)S(1)} fusion(f32[32,16,64]{2,0,1:T(8,128)S(1)} %fusion.25, f32[64,16,1,64]{3,0,1,2:T(8,128)S(1)} %fusion.11, f32[64,16,1,64]{3,0,1,2:T(8,128)S(1)} %convolution_bitcast_fusion, f32[64,64]{1,0:T(8,128)S(1)} %copy.49, f32[64,64]{1,0:T(8,128)S(1)} %copy.48), kind=kOutput, calls=%fused_computation.28 | convolution fusion | flops 25456640 | bytes 753664 | tf_op jit(solution)/shard_map/afkm,mj->fajk/dot_general | solution.py:45
  13.5 0.1 stack.16
  13.6 0.1 maximum_bitcast_fusion.8
  13.8 2.5 %broadcast_in_dim.7 = bf16[2,512,4,32,16]{1,4,0,3,2:T(8,128)(2,1)} broadcast(bf16[2,512,4,16]{1,3,0,2:T(8,128)(2,1)S(1)} %copy.50), dimensions={0,1,2,4} | broadcast | bytes 4325376 | tf_op jit(solution)/shard_map/broadcast_in_dim | solution.py:130
  16.3 0.0 copy-start.2
  16.3 0.0 copy-start.3
  16.3 11.9 %all-to-all-start = ((bf16[2,1,512,128,16]{2,4,0,1,3:T(8,128)(2,1)}), bf16[2,1,512,128,16]{2,4,0,1,3:T(8,128)(2,1)}, u32[]{:S(2)}, u32[]{:S(2)}) async-start(bf16[2,1,512,128,16]{2,4,0,1,3:T(8,128)(2,1)} %bitcast.100), calls=%async_computation | async-start | bytes 8388608 | tf_op jit(solution)/shard_map/all_to_all | solution.py:133
  28.2 1.0 fusion.36
  29.2 1.7 %fusion.34 = (f32[256,256]{1,0:T(8,128)S(1)}, f32[256,256]{1,0:T(8,128)}) fusion(), kind=kLoop, calls=%fused_computation.56 | loop fusion | flops 917504 | bytes 524288 | tf_op jit(solution)/shard_map/sin | solution.py:75
  30.9 0.0 copy-done.2
  30.9 0.1 and_select_fusion.1
  31.0 0.0 copy-done.3
  31.0 0.1 and_select_fusion
  31.1 0.6 multiply_add_fusion.4
  31.7 0.4 add_convert_fusion
  32.1 10.3 %multiply_convert_fusion.1 = (bf16[2048,1,8,256]{0,3,2,1:T(8,128)(2,1)}, bf16[2048,1,8,256]{0,3,2,1:T(8,128)(2,1)}) fusion(f32[2048,256]{0,1:T(8,128)S(1)} %add_convert_fusion, f32[2048,8]{0,1:T(8,128)S(1)} %get-tuple-element.28, f32[2048,8]{0,1:T(8,128)S(1)} %get-tuple-element.29), kind=kLoop, calls=%fused_computation.5 | loop fusion | flops 16777216 | bytes 19005440 | tf_op jit(solution)/shard_map/convert
  42.4 38.3 %all-to-all-done = bf16[2,1,512,128,16]{2,4,0,1,3:T(8,128)(2,1)} async-done(((bf16[2,1,512,128,16]{2,4,0,1,3:T(8,128)(2,1)}), bf16[2,1,512,128,16]{2,4,0,1,3:T(8,128)(2,1)}, u32[]{:S(2)}, u32[]{:S(2)}) %all-to-all-start) | async-done | bytes 4194336 | tf_op jit(solution)/shard_map/all_to_all | solution.py:133
  80.7 0.0 copy-start
  80.7 5.0 %copy.51 = bf16[2,1,512,128,16]{2,4,3,0,1:T(8,128)(2,1)} copy(bf16[2,1,512,128,16]{2,4,0,1,3:T(8,128)(2,1)} %all-to-all-done) | data formatting | bytes 8388608 | tf_op jit(solution)/shard_map/all_to_all | solution.py:133
  85.7 1.1 copy-done
  86.8 21.4 %fusion = f32[2,512,2,8,256]{1,4,3,2,0:T(8,128)S(1)} fusion(bf16[2,512,2048,1,1]{1,2,4,3,0:T(8,128)(2,1)} %bitcast.101, bf16[2048,1,8,256]{0,3,2,1:T(8,128)(2,1)} %get-tuple-element.19, bf16[2048,1,8,256]{0,3,2,1:T(8,128)(2,1)S(1)} %copy-done), kind=kOutput, calls=%fused_computation.1 | convolution fusion | flops 17213423616 | bytes 37748736 | tf_op jit(solution)/shard_map/xkd,dj->xkj/dot_general | solution.py:84
  108.2 1.0 fusion.8
  109.3 0.0 copy-start.1
  109.3 1.0 fusion.9
  110.3 0.0 copy-done.1
  110.3 7.3 %fusion.10 = f32[512,8,512]{2,0,1:T(8,128)S(1)} fusion(f32[1,512,8,256]{1,3,2,0:T(8,128)S(1)} %fusion.8, f32[1,512,8,256]{1,3,2,0:T(8,128)S(1)} %fusion.9, f32[256,256]{1,0:T(8,128)S(1)} %copy-done.1, f32[256,256]{1,0:T(8,128)S(1)} %get-tuple-element.38, f32[256,256]{1,0:T(8,128)S(1)} %fusion.36), kind=kOutput, calls=%fused_computation.17 | convolution fusion | flops 6447431680 | bytes 17563648 | tf_op jit(solution)/shard_map/fkmv,vw->fkmw/dot_general | solution.py:90
  117.6 3.9 %fusion.106 = (f32[8,256]{1,0:T(8,128)S(1)}, f32[512,8,256]{2,0,1:T(8,128)S(1)}) fusion(f32[512,8,256]{2,1,0:T(8,128)} %param.9, f32[512,8,512]{2,0,1:T(8,128)S(1)} %fusion.10), kind=kLoop, calls=%fused_computation.157 | loop fusion | flops 4192256 | bytes 16785408 | tf_op jit(solution)/shard_map/reduce_sum | solution.py:142
  121.5 0.1 collective-permute-start
  121.6 1.2 collective-permute-done
  122.8 1.4 %collective-permute-start.1 = (f32[8,256]{1,0:T(8,128)S(1)}, f32[8,256]{1,0:T(8,128)S(1)}, u32[]{:S(2)}, u32[]{:S(2)}) collective-permute-start(f32[8,256]{1,0:T(8,128)S(1)} %add.202), channel_id=1, source_target_pairs={{0,64},{32,96},{64,0},{96,32},{1,65},{33,97},{65,1},{97,33},{2,66}... | collective-permute-start | bytes 24584 | tf_op jit(solution)/shard_map/ppermute | solution.py:100
  124.2 4.4 %copy.57 = f32[512,8,256]{2,1,0:T(8,128)} copy(f32[512,8,256]{2,0,1:T(8,128)S(1)} %get-tuple-element.13) | data formatting | bytes 8388608
  128.6 0.0 collective-permute-done.1
  128.6 0.6 add_multiply_fusion
  (4 shorter events, 0.1 us)
Async XLA Ops:
  16.3 14.6 %copy-start.2 = (s32[2048,2]{0,1:T(2,128)S(1)}, s32[2048,2]{0,1:T(2,128)}, u32[]{:S(2)}) copy-start(s32[2048,2]{0,1:T(2,128)} %param.8) | copy-start | bytes 49156
  16.3 14.7 %copy-start.3 = (s32[2048,2]{0,1:T(2,128)S(1)}, s32[2048,2]{0,1:T(2,128)}, u32[]{:S(2)}) copy-start(s32[2048,2]{0,1:T(2,128)} %param.7) | copy-start | bytes 49156
  16.3 64.3 %all-to-all-start = ((bf16[2,1,512,128,16]{2,4,0,1,3:T(8,128)(2,1)}), bf16[2,1,512,128,16]{2,4,0,1,3:T(8,128)(2,1)}, u32[]{:S(2)}, u32[]{:S(2)}) async-start(bf16[2,1,512,128,16]{2,4,0,1,3:T(8,128)(2,1)} %bitcast.100), calls=%async_computation | async-start | bytes 8388608 | tf_op jit(solution)/shard_map/all_to_all | solution.py:133
  80.7 6.2 %copy-start = (bf16[2048,1,8,256]{0,3,2,1:T(8,128)(2,1)S(1)}, bf16[2048,1,8,256]{0,3,2,1:T(8,128)(2,1)}, u32[]{:S(2)}) copy-start(bf16[2048,1,8,256]{0,3,2,1:T(8,128)(2,1)} %get-tuple-element.18) | copy-start | bytes 25165828
  109.3 1.0 copy-start.1
  121.5 1.3 collective-permute-start
  122.8 5.9 %collective-permute-start.1 = (f32[8,256]{1,0:T(8,128)S(1)}, f32[8,256]{1,0:T(8,128)S(1)}, u32[]{:S(2)}, u32[]{:S(2)}) collective-permute-start(f32[8,256]{1,0:T(8,128)S(1)} %add.202), channel_id=1, source_target_pairs={{0,64},{32,96},{64,0},{96,32},{1,65},{33,97},{65,1},{97,33},{2,66}... | collective-permute-start | bytes 24584 | tf_op jit(solution)/shard_map/ppermute | solution.py:100

commit v4 on v3

--- a/solution.py
+++ b/solution.py
@@ -8,10 +8,10 @@
 CHUNKS = 1
 
 
-def dft_table(length, count, total, scale):
+def dft_table(length, count, total):
     sample_idx = lax.broadcasted_iota(jnp.int32, (length, count), 0)
     channel_idx = lax.broadcasted_iota(jnp.int32, (length, count), 1)
-    angle = (sample_idx * channel_idx * scale % total).astype(jnp.float32) * (2.0 * math.pi / total)
+    angle = (sample_idx * channel_idx % total).astype(jnp.float32) * (2.0 * math.pi / total)
     return jnp.cos(angle), jnp.sin(angle)
 
 
@@ -28,24 +28,22 @@
     outer = 64
     inner = points // outer
     kept = channels // outer
-    exact = lax.Precision.HIGHEST
-    pieces = framed.reshape(dipoles, frame_count, outer, inner)
-    cos_a, sin_a = dft_table(outer, outer, outer, 1)
-    first_re = jnp.einsum("afnm,nk->afkm", pieces, cos_a, precision=exact)
-    first_im = -jnp.einsum("afnm,nk->afkm", pieces, sin_a, precision=exact)
-    cos_t, sin_t = dft_table(outer, inner, points, 1)
-    cos_t = cos_t[None, None]
-    sin_t = sin_t[None, None]
-    twist_re = first_re * cos_t + first_im * sin_t
-    twist_im = first_im * cos_t - first_re * sin_t
-    cos_b, sin_b = dft_table(inner, kept, inner, 1)
-    spec_re = jnp.einsum("afkm,mj->fajk", twist_re, cos_b, precision=exact) + jnp.einsum(
-        "afkm,mj->fajk", twist_im, sin_b, precision=exact
+    near = lax.Precision.HIGH
+    pieces = framed.reshape(dipoles * frame_count, outer, inner)
+    cos_a, sin_a = dft_table(outer, outer, outer)
+    first = jnp.einsum(
+        "xnm,nk->xkm", pieces, jnp.concatenate([cos_a, -sin_a], axis=1), precision=near
+    ).reshape(dipoles * frame_count, 2, outer, inner)
+    cos_t, sin_t = dft_table(outer, inner, points)
+    twist_re = first[:, 0] * cos_t + first[:, 1] * sin_t
+    twist_im = first[:, 1] * cos_t - first[:, 0] * sin_t
+    twisted = jnp.concatenate([twist_re, twist_im], axis=2)
+    cos_b, sin_b = dft_table(inner, kept, inner)
+    table = jnp.concatenate(
+        [jnp.concatenate([cos_b, -sin_b], axis=1), jnp.concatenate([sin_b, cos_b], axis=1)], axis=0
     )
-    spec_im = jnp.einsum("afkm,mj->fajk", twist_im, cos_b, precision=exact) - jnp.einsum(
-        "afkm,mj->fajk", twist_re, sin_b, precision=exact
-    )
-    spectra = jnp.stack([spec_re, spec_im]).reshape(2, frame_count, dipoles, channels)
+    spec = jnp.einsum("xkm,mj->xjk", twisted, table, precision=near)
+    spectra = spec.reshape(dipoles, frame_count, 2, channels).transpose(2, 1, 0, 3)
     return spectra.astype(jnp.bfloat16)
 
 

time: 130 us -> 127 us (0.977)
  matrix products: 36.4 us -> 30 us
  local copies, waits for them, and re-layouts: 17.4 us -> 20 us
    dot_general x6 -> x1, matrix products: 7.71 us -> 0.95 us  [channelize(): spec = jnp.einsum('xkm,mj->xjk', twisted, table, precision=near)]
    unnamed x9 -> x11, local copies, waits for them, and re-layouts: 5.6 us -> 6.29 us
  transfers between devices with their start and end apart: 3 -> 3, of which waited for: 2 -> 2; matrix products, arithmetic and copies ran while one was open for 14% -> 15% of each run, Pallas kernels for 0% -> 0%
where the time goes in v4:
time: 127 us; the launch traced here: 126 us
  waiting for transfers between devices  39.4 us (31%)
  matrix products  30 us (24%)
  other arithmetic  22 us (17%)
  local copies, waits for them, and re-layouts  20 us (16%)
  starting transfers between devices  13.4 us (11%)
    all_to_all x1, waiting for transfers between devices, body(): lax.all_to_all(outgoing, ('grp', 'dev'), split_axis=3, concat_axis=3, til...  38.3 us
    dot_general x1, matrix products, image_chunk(): jnp.einsum('xkd,dj->xkj', stacked, spread, preferred_element_type=jnp.flo...  21.4 us
    all_to_all x1, starting transfers between devices, body(): lax.all_to_all(outgoing, ('grp', 'dev'), split_axis=3, concat_axis=3, til...  11.9 us
    another operation x1, other arithmetic  10.3 us
    dot_general x1, matrix products, image_chunk(): jnp.einsum('fkmv,vw->fkmw', halves, transform, precision=lax.Precision.HIGH)  7.27 us
    unnamed x11, local copies, waits for them, and re-layouts  6.29 us
    all_to_all x1, local copies, waits for them, and re-layouts, body(): lax.all_to_all(outgoing, ('grp', 'dev'), split_axis=3, concat_axis=3, til...  5.01 us
    reduce_sum x1, other arithmetic, body(): jnp.sum(residual_images, axis=0)  3.94 us
  transfers between devices with their start and end apart: 3, of which 2 were waited for; matrix products, arithmetic and copies ran while one was open for 15% of the time, Pallas kernels for 0%

profile of v4, /device:TPU:0, one launch (start us, length us, event | category | flops | bytes accessed | tf_op | source)
XLA Modules:
  0.0 125.7 jit_solution(13812868091547260459)
XLA Ops:
  0.6 0.1 sine_negate_fusion
  0.8 0.1 fusion.62
  0.9 0.1 fusion.69
  1.0 0.1 fusion.72
  1.1 1.4 %reshape.405 = bf16[16,4,4096]{2,1,0:T(4,128)(2,1)S(1)} reshape(bf16[16,16384]{1,0:T(8,128)(2,1)} %param.5) | data formatting | bytes 1048576 | tf_op jit(solution)/shard_map/reshape | solution.py:21
  2.5 1.1 fusion.80
  3.7 1.1 fusion.81
  4.8 0.7 multiply_add_fusion
  5.4 0.2 reshape.406
  5.6 0.2 copy.33
  5.9 0.4 fusion.48
  6.3 0.6 reshape.407
  6.9 1.1 fusion.79
  8.0 0.3 copy.52
  8.4 0.3 copy.53
  8.7 0.1 fusion.21
  8.9 0.9 fusion.11
  9.8 0.2 convert_element_type.118
  10.1 0.1 squeeze_reshape.3
  10.2 2.5 %broadcast_in_dim.7 = bf16[2,512,4,32,16]{1,4,0,3,2:T(8,128)(2,1)} broadcast(bf16[2,512,4,16]{1,3,0,2:T(8,128)(2,1)S(1)} %copy.36), dimensions={0,1,2,4} | broadcast | bytes 4325376 | tf_op jit(solution)/shard_map/broadcast_in_dim | solution.py:128
  12.8 0.0 copy-start.2
  12.8 0.0 copy-start.3
  12.8 11.9 %all-to-all-start = ((bf16[2,1,512,128,16]{2,4,0,1,3:T(8,128)(2,1)}), bf16[2,1,512,128,16]{2,4,0,1,3:T(8,128)(2,1)}, u32[]{:S(2)}, u32[]{:S(2)}) async-start(bf16[2,1,512,128,16]{2,4,0,1,3:T(8,128)(2,1)} %bitcast.82), calls=%async_computation | async-start | bytes 8388608 | tf_op jit(solution)/shard_map/all_to_all | solution.py:131
  24.7 1.0 fusion.31
  25.7 1.7 %fusion.29 = (f32[256,256]{1,0:T(8,128)S(1)}, f32[256,256]{1,0:T(8,128)}) fusion(), kind=kLoop, calls=%fused_computation.49 | loop fusion | flops 917504 | bytes 524288 | tf_op jit(solution)/shard_map/sin | solution.py:73
  27.4 0.0 copy-done.2
  27.4 0.1 and_select_fusion.1
  27.5 0.0 copy-done.3
  27.5 0.1 and_select_fusion
  27.6 0.6 multiply_add_fusion.1
  28.2 0.4 add_convert_fusion
  28.6 10.3 %multiply_convert_fusion.1 = (bf16[2048,1,8,256]{0,3,2,1:T(8,128)(2,1)}, bf16[2048,1,8,256]{0,3,2,1:T(8,128)(2,1)}) fusion(f32[2048,256]{0,1:T(8,128)S(1)} %add_convert_fusion, f32[2048,8]{0,1:T(8,128)S(1)} %get-tuple-element.28, f32[2048,8]{0,1:T(8,128)S(1)} %get-tuple-element.29), kind=kLoop, calls=%fused_computation.5 | loop fusion | flops 16777216 | bytes 19005440 | tf_op jit(solution)/shard_map/convert
  38.9 38.3 %all-to-all-done = bf16[2,1,512,128,16]{2,4,0,1,3:T(8,128)(2,1)} async-done(((bf16[2,1,512,128,16]{2,4,0,1,3:T(8,128)(2,1)}), bf16[2,1,512,128,16]{2,4,0,1,3:T(8,128)(2,1)}, u32[]{:S(2)}, u32[]{:S(2)}) %all-to-all-start) | async-done | bytes 4194336 | tf_op jit(solution)/shard_map/all_to_all | solution.py:131
  77.1 0.0 copy-start
  77.1 5.0 %copy.37 = bf16[2,1,512,128,16]{2,4,3,0,1:T(8,128)(2,1)} copy(bf16[2,1,512,128,16]{2,4,0,1,3:T(8,128)(2,1)} %all-to-all-done) | data formatting | bytes 8388608 | tf_op jit(solution)/shard_map/all_to_all | solution.py:131
  82.2 1.1 copy-done
  83.3 21.4 %fusion = f32[2,512,2,8,256]{1,4,3,2,0:T(8,128)S(1)} fusion(bf16[2,512,2048,1,1]{1,2,4,3,0:T(8,128)(2,1)} %bitcast.83, bf16[2048,1,8,256]{0,3,2,1:T(8,128)(2,1)} %get-tuple-element.15, bf16[2048,1,8,256]{0,3,2,1:T(8,128)(2,1)S(1)} %copy-done), kind=kOutput, calls=%fused_computation.1 | convolution fusion | flops 17213423616 | bytes 37748736 | tf_op jit(solution)/shard_map/xkd,dj->xkj/dot_general | solution.py:82
  104.7 1.0 fusion.8
  105.7 0.0 copy-start.1
  105.7 1.0 fusion.9
  106.8 0.0 copy-done.1
  106.8 7.3 %fusion.10 = f32[512,8,512]{2,0,1:T(8,128)S(1)} fusion(f32[1,512,8,256]{1,3,2,0:T(8,128)S(1)} %fusion.8, f32[1,512,8,256]{1,3,2,0:T(8,128)S(1)} %fusion.9, f32[256,256]{1,0:T(8,128)S(1)} %copy-done.1, f32[256,256]{1,0:T(8,128)S(1)} %get-tuple-element.44, f32[256,256]{1,0:T(8,128)S(1)} %fusion.31), kind=kOutput, calls=%fused_computation.17 | convolution fusion | flops 6447431680 | bytes 17563648 | tf_op jit(solution)/shard_map/fkmv,vw->fkmw/dot_general | solution.py:88
  114.0 3.9 %fusion.77 = (f32[8,256]{1,0:T(8,128)S(1)}, f32[512,8,256]{2,0,1:T(8,128)S(1)}) fusion(f32[512,8,256]{2,1,0:T(8,128)} %param.9, f32[512,8,512]{2,0,1:T(8,128)S(1)} %fusion.10), kind=kLoop, calls=%fused_computation.134 | loop fusion | flops 4192256 | bytes 16785408 | tf_op jit(solution)/shard_map/reduce_sum | solution.py:140
  118.0 0.1 collective-permute-start
  118.1 1.2 collective-permute-done
  119.2 1.4 %collective-permute-start.1 = (f32[8,256]{1,0:T(8,128)S(1)}, f32[8,256]{1,0:T(8,128)S(1)}, u32[]{:S(2)}, u32[]{:S(2)}) collective-permute-start(f32[8,256]{1,0:T(8,128)S(1)} %add.186), channel_id=1, source_target_pairs={{0,64},{32,96},{64,0},{96,32},{1,65},{33,97},{65,1},{97,33},{2,66}... | collective-permute-start | bytes 24584 | tf_op jit(solution)/shard_map/ppermute | solution.py:98
  120.7 4.4 %copy.43 = f32[512,8,256]{2,1,0:T(8,128)} copy(f32[512,8,256]{2,0,1:T(8,128)S(1)} %get-tuple-element.9) | data formatting | bytes 8388608
  125.1 0.0 collective-permute-done.1
  125.1 0.6 add_multiply_fusion
  (4 shorter events, 0.1 us)
Async XLA Ops:
  12.8 14.6 %copy-start.2 = (s32[2048,2]{0,1:T(2,128)S(1)}, s32[2048,2]{0,1:T(2,128)}, u32[]{:S(2)}) copy-start(s32[2048,2]{0,1:T(2,128)} %param.8) | copy-start | bytes 49156
  12.8 14.7 %copy-start.3 = (s32[2048,2]{0,1:T(2,128)S(1)}, s32[2048,2]{0,1:T(2,128)}, u32[]{:S(2)}) copy-start(s32[2048,2]{0,1:T(2,128)} %param.7) | copy-start | bytes 49156
  12.8 64.4 %all-to-all-start = ((bf16[2,1,512,128,16]{2,4,0,1,3:T(8,128)(2,1)}), bf16[2,1,512,128,16]{2,4,0,1,3:T(8,128)(2,1)}, u32[]{:S(2)}, u32[]{:S(2)}) async-start(bf16[2,1,512,128,16]{2,4,0,1,3:T(8,128)(2,1)} %bitcast.82), calls=%async_computation | async-start | bytes 8388608 | tf_op jit(solution)/shard_map/all_to_all | solution.py:131
  77.1 6.2 %copy-start = (bf16[2048,1,8,256]{0,3,2,1:T(8,128)(2,1)S(1)}, bf16[2048,1,8,256]{0,3,2,1:T(8,128)(2,1)}, u32[]{:S(2)}) copy-start(bf16[2048,1,8,256]{0,3,2,1:T(8,128)(2,1)} %get-tuple-element.14) | copy-start | bytes 25165828
  105.7 1.0 copy-start.1
  118.0 1.3 collective-permute-start
  119.2 5.9 %collective-permute-start.1 = (f32[8,256]{1,0:T(8,128)S(1)}, f32[8,256]{1,0:T(8,128)S(1)}, u32[]{:S(2)}, u32[]{:S(2)}) collective-permute-start(f32[8,256]{1,0:T(8,128)S(1)} %add.186), channel_id=1, source_target_pairs={{0,64},{32,96},{64,0},{96,32},{1,65},{33,97},{65,1},{97,33},{2,66}... | collective-permute-start | bytes 24584 | tf_op jit(solution)/shard_map/ppermute | solution.py:98

commit v5 on v4

--- a/solution.py
+++ b/solution.py
@@ -50,44 +50,27 @@
 def row_phases(cells, bits, rows, grid_len):
     scale = 2.0 * math.pi / grid_len
     near = (cells[:, None] * rows[None, :] % grid_len).astype(jnp.float32) * scale
-    far = ((cells[:, None] + 1) * rows[None, :] % grid_len).astype(jnp.float32) * scale
+    step = (rows % grid_len).astype(jnp.float32)[None, :] * scale
     low = (bits % 2).astype(jnp.float32)[:, None]
     high = (bits // 2).astype(jnp.float32)[:, None]
-    real = low * jnp.cos(near) + high * jnp.cos(far)
-    imag = -(low * jnp.sin(near) + high * jnp.sin(far))
+    base_re = jnp.cos(near)
+    base_im = jnp.sin(near)
+    shift_re = low + high * jnp.cos(step)
+    shift_im = high * jnp.sin(step)
+    real = base_re * shift_re - base_im * shift_im
+    imag = -(base_im * shift_re + base_re * shift_im)
     return real, imag
 
 
-def column_weights(cells, bits, grid_len):
-    cols = lax.broadcasted_iota(jnp.int32, (cells.shape[0], grid_len), 1)
-    lower = (cols == cells[:, None]) * (bits % 2)[:, None]
-    upper = (cols == cells[:, None] + 1) * (bits // 2)[:, None]
-    return (lower + upper).astype(jnp.float32)
-
-
-def column_transform(grid_len):
-    out_idx = lax.broadcasted_iota(jnp.int32, (grid_len, grid_len), 0)
-    in_idx = lax.broadcasted_iota(jnp.int32, (grid_len, grid_len), 1)
-    angle = (out_idx * in_idx % grid_len).astype(jnp.float32) * (2.0 * math.pi / grid_len)
-    cosine = jnp.cos(angle)
-    sine = jnp.sin(angle)
-    return jnp.concatenate(
-        [jnp.concatenate([cosine, -sine], axis=1), jnp.concatenate([sine, cosine], axis=1)], axis=0
-    )
-
-
-def image_chunk(incoming, spread, transform, sky_part, parts, frame_count, rows_mine, grid_len, norm_scale):
+def image_chunk(incoming, spread, sky_part, parts, frame_count, rows_mine, grid_len, norm_scale):
     _, _, span, sources, local = incoming.shape
     stacked = incoming.reshape(parts * frame_count, span, sources * local)
     products = jnp.einsum(
         "xkd,dj->xkj", stacked, spread, preferred_element_type=jnp.float32
     ).reshape(parts, frame_count, span, 2, rows_mine, grid_len)
-    half_re = products[0, :, :, 0] - products[1, :, :, 1]
-    half_im = products[0, :, :, 1] + products[1, :, :, 0]
-    halves = jnp.concatenate([half_re, half_im], axis=-1)
-    sky_image = jnp.einsum("fkmv,vw->fkmw", halves, transform, precision=lax.Precision.HIGH)
-    power_sum = jnp.sum(sky_image * sky_image, axis=0)
-    power_sum = (power_sum[..., :grid_len] + power_sum[..., grid_len:]) * norm_scale
+    sky_re = products[0, :, :, 0] - products[1, :, :, 1]
+    sky_im = products[0, :, :, 1] + products[1, :, :, 0]
+    power_sum = jnp.sum(sky_re * sky_re + sky_im * sky_im, axis=0) * norm_scale
     return power_sum - sky_part
 
 
@@ -115,12 +98,16 @@
     by_block = spectra.reshape(parts, frame_count, local, groups, chunks, span)
     rows = lax.axis_index("dev") * rows_mine + lax.broadcasted_iota(jnp.int32, (rows_mine,), 0)
     phase_re, phase_im = row_phases(dipole_cells[:, 0], kernel_bits[:, 0], rows, grid_len)
-    col_w = column_weights(dipole_cells[:, 1], kernel_bits[:, 1], grid_len)
+    cols = lax.broadcasted_iota(jnp.int32, (grid_len,), 0)
+    col_re, col_im = row_phases(dipole_cells[:, 1], kernel_bits[:, 1], cols, grid_len)
     spread = jnp.stack(
-        [phase_re[:, :, None] * col_w[:, None, :], phase_im[:, :, None] * col_w[:, None, :]], axis=1
+        [
+            phase_re[:, :, None] * col_re[:, None, :] - phase_im[:, :, None] * col_im[:, None, :],
+            phase_re[:, :, None] * col_im[:, None, :] + phase_im[:, :, None] * col_re[:, None, :],
+        ],
+        axis=1,
     ).astype(jnp.bfloat16)
     spread = spread.reshape(dipoles, 2 * rows_mine * grid_len)
-    transform = column_transform(grid_len)
     norm_scale = 1.0 / (frame_count * dipoles)
     results = []
     for chunk in range(chunks):
@@ -132,7 +119,7 @@
         sky_part = sky_model[chunk * span : (chunk + 1) * span]
         results.append(
             image_chunk(
-                incoming, spread, transform, sky_part, parts, frame_count, rows_mine, grid_len, norm_scale
+                incoming, spread, sky_part, parts, frame_count, rows_mine, grid_len, norm_scale
             )
         )
     residual_images = jnp.concatenate(results, axis=0)

time: 127 us -> 117 us (0.921)
  matrix products: 30 us -> 22.5 us
  waiting for transfers between devices: 39.4 us -> 36.4 us
    sub x1 -> x2, other arithmetic: 1.02 us -> 9.31 us  [row_phases(): real = base_re * shift_re - base_im * shift_im]
    dot_general x1 -> x0, matrix products: 7.27 us -> none  [image_chunk(): jnp.einsum('fkmv,vw->fkmw', halves, transform, precision=lax.Precision.HIGH)]
    all_to_all x1, waiting for transfers between devices: 38.3 us -> 35.3 us  [body(): lax.all_to_all(outgoing, ('grp', 'dev'), split_axis=3, concat_axis=3, til...]
    another operation x1, other arithmetic: 10.3 us -> 7.56 us
    sin x1 -> x2, other arithmetic: 1.72 us -> 0.1 us  [row_phases(): shift_im = high * jnp.sin(step)]
    add x2 -> x0, other arithmetic: 1.63 us -> none  [the longest x1 1.02 us: image_chunk(): half_im = products[0, :, :, 1] + products[1, :, :, 0]]
    unnamed x11 -> x9, local copies, waits for them, and re-layouts: 6.29 us -> 6.29 us
  transfers between devices with their start and end apart: 3 -> 3, of which waited for: 2 -> 2; matrix products, arithmetic and copies ran while one was open for 15% -> 19% of each run, Pallas kernels for 0% -> 0%
where the time goes in v5:
time: 117 us; the launch traced here: 116 us
  waiting for transfers between devices  36.4 us (31%)
  matrix products  22.5 us (19%)
  other arithmetic  22.4 us (19%)
  local copies, waits for them, and re-layouts  20 us (17%)
  starting transfers between devices  13.4 us (11%)
    all_to_all x1, waiting for transfers between devices, body(): lax.all_to_all(outgoing, ('grp', 'dev'), split_axis=3, concat_axis=3, til...  35.3 us
    dot_general x1, matrix products, image_chunk(): jnp.einsum('xkd,dj->xkj', stacked, spread, preferred_element_type=jnp.flo...  21.1 us
    all_to_all x1, starting transfers between devices, body(): lax.all_to_all(outgoing, ('grp', 'dev'), split_axis=3, concat_axis=3, til...  11.9 us
    sub x2, other arithmetic, row_phases(): real = base_re * shift_re - base_im * shift_im  9.31 us
    another operation x1, other arithmetic  7.56 us
    unnamed x9, local copies, waits for them, and re-layouts  6.29 us
    all_to_all x1, local copies, waits for them, and re-layouts, body(): lax.all_to_all(outgoing, ('grp', 'dev'), split_axis=3, concat_axis=3, til...  5.01 us
    reduce_sum x1, other arithmetic, body(): jnp.sum(residual_images, axis=0)  3.46 us
  transfers between devices with their start and end apart: 3, of which 2 were waited for; matrix products, arithmetic and copies ran while one was open for 19% of the time, Pallas kernels for 0%

profile of v5, /device:TPU:0, one launch (start us, length us, event | category | flops | bytes accessed | tf_op | source)
XLA Modules:
  0.0 115.6 jit_solution(7100465584422029448)
XLA Ops:
  0.6 0.1 fusion.71
  0.7 0.1 fusion.67
  0.8 0.1 fusion.59
  1.0 0.1 sine_negate_fusion
  1.1 1.1 fusion.88
  2.2 1.4 %reshape.561 = bf16[16,4,4096]{2,1,0:T(4,128)(2,1)S(1)} reshape(bf16[16,16384]{1,0:T(8,128)(2,1)} %param.5) | data formatting | bytes 1048576 | tf_op jit(solution)/shard_map/reshape | solution.py:21
  3.6 1.1 fusion.87
  4.8 0.7 multiply_add_fusion.1
  5.4 0.2 reshape.562
  5.6 0.2 copy.27
  5.9 0.4 fusion.43
  6.3 0.6 reshape.563
  6.9 1.1 fusion.86
  8.0 0.3 copy.42
  8.4 0.3 copy.43
  8.7 0.1 fusion.25
  8.9 0.9 fusion.19
  9.8 0.2 convert_element_type.130
  10.1 0.1 squeeze_reshape.3
  10.2 2.5 %broadcast_in_dim.7 = bf16[2,512,4,32,16]{1,4,0,3,2:T(8,128)(2,1)} broadcast(bf16[2,512,4,16]{1,3,0,2:T(8,128)(2,1)S(1)} %copy.30), dimensions={0,1,2,4} | broadcast | bytes 4325376 | tf_op jit(solution)/shard_map/broadcast_in_dim | solution.py:115
  12.8 0.0 copy-start.2
  12.8 0.0 copy-start.1
  12.8 11.9 %all-to-all-start = ((bf16[2,1,512,128,16]{2,4,0,1,3:T(8,128)(2,1)}), bf16[2,1,512,128,16]{2,4,0,1,3:T(8,128)(2,1)}, u32[]{:S(2)}, u32[]{:S(2)}) async-start(bf16[2,1,512,128,16]{2,4,0,1,3:T(8,128)(2,1)} %bitcast.71), calls=%async_computation | async-start | bytes 8388608 | tf_op jit(solution)/shard_map/all_to_all | solution.py:118
  24.7 0.1 fusion.82
  24.8 0.0 copy-done.2
  24.8 0.0 copy-done.1
  24.8 0.1 fusion.65
  24.9 0.1 fusion.69
  25.0 0.4 fusion.27
  25.3 8.9 %fusion.10 = (f32[2048,256]{0,1:T(8,128)S(1)}, f32[2048,256]{0,1:T(8,128)S(1)}) fusion(f32[256]{0:T(256)S(1)} %get-tuple-element.44, f32[256]{0:T(256)S(1)} %get-tuple-element.45, f32[2048]{0:T(1024)S(1)} %bitcast.83, f32[2048]{0:T(1024)S(1)} %bitcast.82, s32[2048]{0:T(1024)S(1)} %bitcast.81), kind=kLoop, calls=%fused_computation.20 | loop fusion | flops 12582912 | bytes 4220928 | tf_op jit(solution)/shard_map/sub | solution.py:60
  34.3 7.6 %subtract_convert_fusion = (bf16[2048,1,8,256]{0,3,2,1:T(8,128)(2,1)}, bf16[2048,1,8,256]{0,3,2,1:T(8,128)(2,1)}) fusion(f32[2048,256]{0,1:T(8,128)S(1)} %get-tuple-element.29, f32[2048,8]{0,1:T(8,128)S(1)} %get-tuple-element.31, f32[2048,256]{0,1:T(8,128)S(1)} %get-tuple-element.28, f32[2048,8]{0,1:T(8,128)S(1)} %get-tuple-element.30), kind=kLoop, calls=%fused_computation.5 | loop fusion | flops 33554432 | bytes 21102592 | tf_op jit(solution)/shard_map/convert
  41.9 35.3 %all-to-all-done = bf16[2,1,512,128,16]{2,4,0,1,3:T(8,128)(2,1)} async-done(((bf16[2,1,512,128,16]{2,4,0,1,3:T(8,128)(2,1)}), bf16[2,1,512,128,16]{2,4,0,1,3:T(8,128)(2,1)}, u32[]{:S(2)}, u32[]{:S(2)}) %all-to-all-start) | async-done | bytes 4194336 | tf_op jit(solution)/shard_map/all_to_all | solution.py:118
  77.1 0.0 copy-start
  77.1 5.0 %copy.31 = bf16[2,1,512,128,16]{2,4,3,0,1:T(8,128)(2,1)} copy(bf16[2,1,512,128,16]{2,4,0,1,3:T(8,128)(2,1)} %all-to-all-done) | data formatting | bytes 8388608 | tf_op jit(solution)/shard_map/all_to_all | solution.py:118
  82.2 1.1 copy-done
  83.3 21.1 %fusion.3 = f32[2,1,512,2,8,256]{5,2,4,3,0,1:T(8,128)S(1)} fusion(bf16[2,512,2048,1,1]{1,2,4,3,0:T(8,128)(2,1)} %bitcast.72, bf16[2048,1,8,256]{0,3,2,1:T(8,128)(2,1)} %get-tuple-element.15, bf16[2048,1,8,256]{0,3,2,1:T(8,128)(2,1)S(1)} %copy-done), kind=kOutput, calls=%fused_computation.6 | convolution fusion | flops 17213423616 | bytes 37748736 | tf_op jit(solution)/shard_map/xkd,dj->xkj/dot_general | solution.py:68
  104.4 3.5 %fusion.84 = (f32[8,256]{1,0:T(8,128)S(1)}, f32[512,8,256]{2,0,1:T(8,128)S(1)}) fusion(f32[512,8,256]{2,1,0:T(8,128)} %param.9, f32[2,1,512,2,8,256]{5,2,4,3,0,1:T(8,128)S(1)} %fusion.3), kind=kLoop, calls=%fused_computation.136 | loop fusion | flops 8386560 | bytes 25174016 | tf_op jit(solution)/shard_map/reduce_sum | solution.py:127
  107.9 0.1 collective-permute-start
  107.9 1.2 %collective-permute-done = f32[8,256]{1,0:T(8,128)S(1)} collective-permute-done((f32[8,256]{1,0:T(8,128)S(1)}, f32[8,256]{1,0:T(8,128)S(1)}, u32[]{:S(2)}, u32[]{:S(2)}) %collective-permute-start) | collective-permute-done | bytes 8224 | tf_op jit(solution)/shard_map/ppermute | solution.py:81
  109.1 1.5 %collective-permute-start.1 = (f32[8,256]{1,0:T(8,128)S(1)}, f32[8,256]{1,0:T(8,128)S(1)}, u32[]{:S(2)}, u32[]{:S(2)}) collective-permute-start(f32[8,256]{1,0:T(8,128)S(1)} %add.236), channel_id=1, source_target_pairs={{0,64},{32,96},{64,0},{96,32},{1,65},{33,97},{65,1},{97,33},{2,66}... | collective-permute-start | bytes 24584 | tf_op jit(solution)/shard_map/ppermute | solution.py:81
  110.6 4.4 %copy.34 = f32[512,8,256]{2,1,0:T(8,128)} copy(f32[512,8,256]{2,0,1:T(8,128)S(1)} %get-tuple-element.9) | data formatting | bytes 8388608
  115.0 0.0 collective-permute-done.1
  115.0 0.6 add_multiply_fusion
  (5 shorter events, 0.1 us)
Async XLA Ops:
  12.8 12.0 %copy-start.2 = (s32[2048,2]{0,1:T(2,128)S(1)}, s32[2048,2]{0,1:T(2,128)}, u32[]{:S(2)}) copy-start(s32[2048,2]{0,1:T(2,128)} %param.7) | copy-start | bytes 49156
  12.8 12.1 %copy-start.1 = (s32[2048,2]{0,1:T(2,128)S(1)}, s32[2048,2]{0,1:T(2,128)}, u32[]{:S(2)}) copy-start(s32[2048,2]{0,1:T(2,128)} %param.8) | copy-start | bytes 49156
  12.8 64.4 %all-to-all-start = ((bf16[2,1,512,128,16]{2,4,0,1,3:T(8,128)(2,1)}), bf16[2,1,512,128,16]{2,4,0,1,3:T(8,128)(2,1)}, u32[]{:S(2)}, u32[]{:S(2)}) async-start(bf16[2,1,512,128,16]{2,4,0,1,3:T(8,128)(2,1)} %bitcast.71), calls=%async_computation | async-start | bytes 8388608 | tf_op jit(solution)/shard_map/all_to_all | solution.py:118
  77.1 6.2 %copy-start = (bf16[2048,1,8,256]{0,3,2,1:T(8,128)(2,1)S(1)}, bf16[2048,1,8,256]{0,3,2,1:T(8,128)(2,1)}, u32[]{:S(2)}) copy-start(bf16[2048,1,8,256]{0,3,2,1:T(8,128)(2,1)} %get-tuple-element.14) | copy-start | bytes 25165828
  107.9 1.3 %collective-permute-start = (f32[8,256]{1,0:T(8,128)S(1)}, f32[8,256]{1,0:T(8,128)S(1)}, u32[]{:S(2)}, u32[]{:S(2)}) collective-permute-start(f32[8,256]{1,0:T(8,128)S(1)} %get-tuple-element.8), channel_id=1, source_target_pairs={{0,32},{32,0},{64,96},{96,64},{1,33},{33,1},{65,97},{97,65},{2,34}... | collective-permute-start | bytes 24584 | tf_op jit(solution)/shard_map/ppermute | solution.py:81
  109.1 5.9 %collective-permute-start.1 = (f32[8,256]{1,0:T(8,128)S(1)}, f32[8,256]{1,0:T(8,128)S(1)}, u32[]{:S(2)}, u32[]{:S(2)}) collective-permute-start(f32[8,256]{1,0:T(8,128)S(1)} %add.236), channel_id=1, source_target_pairs={{0,64},{32,96},{64,0},{96,32},{1,65},{33,97},{65,1},{97,33},{2,66}... | collective-permute-start | bytes 24584 | tf_op jit(solution)/shard_map/ppermute | solution.py:81

commit v6 on v5

--- a/solution.py
+++ b/solution.py
@@ -1,8 +1,11 @@
+import functools
 import math
 
 import jax
 import jax.numpy as jnp
 from jax import lax
+from jax.experimental import pallas as pl
+from jax.experimental.pallas import tpu as pltpu
 from jax.sharding import PartitionSpec as P
 
 CHUNKS = 1
@@ -62,16 +65,61 @@
     return real, imag
 
 
-def image_chunk(incoming, spread, sky_part, parts, frame_count, rows_mine, grid_len, norm_scale):
-    _, _, span, sources, local = incoming.shape
-    stacked = incoming.reshape(parts * frame_count, span, sources * local)
-    products = jnp.einsum(
-        "xkd,dj->xkj", stacked, spread, preferred_element_type=jnp.float32
-    ).reshape(parts, frame_count, span, 2, rows_mine, grid_len)
-    sky_re = products[0, :, :, 0] - products[1, :, :, 1]
-    sky_im = products[0, :, :, 1] + products[1, :, :, 0]
-    power_sum = jnp.sum(sky_re * sky_re + sky_im * sky_im, axis=0) * norm_scale
-    return power_sum - sky_part
+def image_kernel(norm_scale, spectra_ref, spread_ref, sky_ref, out_ref, band_ref):
+    contract = (((0,), (0,)), ((), ()))
+    sources, _, _, local, span = spectra_ref.shape
+    spec_re = spectra_ref[:, 0, 0].reshape(sources * local, span)
+    spec_im = spectra_ref[:, 1, 0].reshape(sources * local, span)
+    table_re = spread_ref[0, 0]
+    table_im = spread_ref[1, 0]
+    f32 = jnp.float32
+    sky_re = lax.dot_general(spec_re, table_re, contract, preferred_element_type=f32) - lax.dot_general(
+        spec_im, table_im, contract, preferred_element_type=f32
+    )
+    sky_im = lax.dot_general(spec_re, table_im, contract, preferred_element_type=f32) + lax.dot_general(
+        spec_im, table_re, contract, preferred_element_type=f32
+    )
+    power = (sky_re * sky_re + sky_im * sky_im) * norm_scale
+    row = pl.program_id(0)
+    for index in range(out_ref.shape[1]):
+
+        @pl.when(row == index)
+        def _():
+            residual = power - sky_ref[:, index, :]
+            out_ref[:, index, :] = residual
+            band_ref[0] = jnp.sum(residual, axis=0, keepdims=True)
+
+
+def image_block(incoming, spread, sky_model, norm_scale):
+    sources, parts, frame_count, local, span = incoming.shape
+    dipoles = sources * local
+    _, rows_mine, _, grid_len = spread.shape
+    stacked = incoming
+    flat_sky = sky_model
+    residual, band = pl.pallas_call(
+        functools.partial(image_kernel, norm_scale),
+        grid=(rows_mine,),
+        in_specs=[
+            pl.BlockSpec((sources, parts, frame_count, local, span), lambda m: (0, 0, 0, 0, 0)),
+            pl.BlockSpec((2, 1, dipoles, grid_len), lambda m: (0, m, 0, 0)),
+            pl.BlockSpec((span, rows_mine, grid_len), lambda m: (0, 0, 0)),
+        ],
+        out_specs=[
+            pl.BlockSpec((span, rows_mine, grid_len), lambda m: (0, 0, 0)),
+            pl.BlockSpec((1, 1, grid_len), lambda m: (m, 0, 0)),
+        ],
+        out_shape=[
+            jax.ShapeDtypeStruct((span, rows_mine, grid_len), jnp.float32),
+            jax.ShapeDtypeStruct((rows_mine, 1, grid_len), jnp.float32),
+        ],
+        compiler_params=pltpu.CompilerParams(vmem_limit_bytes=48 * 1024 * 1024),
+        cost_estimate=pl.CostEstimate(
+            flops=8 * span * dipoles * rows_mine * grid_len,
+            transcendentals=0,
+            bytes_accessed=2 * stacked.size + 2 * spread.size + 8 * flat_sky.size,
+        ),
+    )(stacked, spread, flat_sky)
+    return residual, band.reshape(rows_mine, grid_len)
 
 
 def group_sum(value, groups):
@@ -102,29 +150,20 @@
     col_re, col_im = row_phases(dipole_cells[:, 1], kernel_bits[:, 1], cols, grid_len)
     spread = jnp.stack(
         [
-            phase_re[:, :, None] * col_re[:, None, :] - phase_im[:, :, None] * col_im[:, None, :],
-            phase_re[:, :, None] * col_im[:, None, :] + phase_im[:, :, None] * col_re[:, None, :],
+            phase_re.T[:, :, None] * col_re[None] - phase_im.T[:, :, None] * col_im[None],
+            phase_re.T[:, :, None] * col_im[None] + phase_im.T[:, :, None] * col_re[None],
         ],
-        axis=1,
+        axis=0,
     ).astype(jnp.bfloat16)
-    spread = spread.reshape(dipoles, 2 * rows_mine * grid_len)
     norm_scale = 1.0 / (frame_count * dipoles)
-    results = []
-    for chunk in range(chunks):
-        piece = by_block[:, :, :, :, chunk].transpose(0, 1, 4, 3, 2)
-        outgoing = jnp.broadcast_to(
-            piece[:, :, :, :, None], (parts, frame_count, span, groups, members, local)
-        ).reshape(parts, frame_count, span, groups * members, local)
-        incoming = lax.all_to_all(outgoing, ("grp", "dev"), split_axis=3, concat_axis=3, tiled=True)
-        sky_part = sky_model[chunk * span : (chunk + 1) * span]
-        results.append(
-            image_chunk(
-                incoming, spread, sky_part, parts, frame_count, rows_mine, grid_len, norm_scale
-            )
-        )
-    residual_images = jnp.concatenate(results, axis=0)
+    piece = by_block.reshape(parts, frame_count, local, groups, block).transpose(3, 0, 1, 2, 4)
+    outgoing = jnp.broadcast_to(
+        piece[:, None], (groups, members, parts, frame_count, local, block)
+    ).reshape(groups * members, parts, frame_count, local, block)
+    incoming = lax.all_to_all(outgoing, ("grp", "dev"), split_axis=0, concat_axis=0, tiled=True)
+    residual_images, band = image_block(incoming, spread, sky_model, norm_scale)
     channel_total = residual_images.shape[0] * groups
-    broadband = group_sum(jnp.sum(residual_images, axis=0), groups) / channel_total
+    broadband = group_sum(band, groups) / channel_total
     return (residual_images, broadband)
 
 

time: 117 us -> 112 us (0.957)
  Pallas kernels: 0 us -> 28.3 us
  matrix products: 22.5 us -> 1.37 us
  local copies, waits for them, and re-layouts: 20 us -> 8.4 us
    pallas_call x0 -> x1, Pallas kernels: none -> 28.3 us  [image_block(): pl.pallas_call(functools.partial(image_kernel, norm_scale), grid=(rows_mi...]
    dot_general x1 -> x0, matrix products: 21.1 us -> none  [image_chunk(): jnp.einsum('xkd,dj->xkj', stacked, spread, preferred_element_type=jnp.flo...]
    unnamed x9, local copies, waits for them, and re-layouts: 6.29 us -> 0.71 us
    all_to_all x1 -> x0, local copies, waits for them, and re-layouts: 5.01 us -> none  [body(): lax.all_to_all(outgoing, ('grp', 'dev'), split_axis=3, concat_axis=3, til...]
    all_to_all x1, waiting for transfers between devices: 35.3 us -> 30.9 us  [body(): lax.all_to_all(outgoing, ('grp', 'dev'), split_axis=0, concat_axis=0, til...]
    another operation x1 -> x2, other arithmetic: 7.56 us -> 11.8 us  [the longest x1 6.77 us: body(): jnp.stack([phase_re.T[:, :, None] * col_re[None] - phase_im.T[:, :, None]...]
    ppermute x2, waiting for transfers between devices: 1.16 us -> 4.89 us  [group_sum(): value = value + lax.ppermute(value, 'grp', pairs)]
    reduce_sum x1 -> x0, other arithmetic: 3.46 us -> none  [body(): jnp.sum(residual_images, axis=0)]
  transfers between devices with their start and end apart: 3 -> 3, of which waited for: 2 -> 3; matrix products, arithmetic and copies ran while one was open for 19% -> 19% of each run, Pallas kernels for 0% -> 0%
where the time goes in v6:
time: 112 us; the launch traced here: 111 us
  waiting for transfers between devices  35.8 us (32%)
  Pallas kernels  28.3 us (25%)
  other arithmetic  23.4 us (21%)
  starting transfers between devices  13.3 us (12%)
  local copies, waits for them, and re-layouts  8.4 us (8%)
  matrix products  1.37 us (1%)
    all_to_all x1, waiting for transfers between devices, body(): lax.all_to_all(outgoing, ('grp', 'dev'), split_axis=0, concat_axis=0, til...  30.9 us
    pallas_call x1, Pallas kernels, image_block(): pl.pallas_call(functools.partial(image_kernel, norm_scale), grid=(rows_mi...  28.3 us
    all_to_all x1, starting transfers between devices, body(): lax.all_to_all(outgoing, ('grp', 'dev'), split_axis=0, concat_axis=0, til...  11.9 us
    sub x2, other arithmetic, row_phases(): real = base_re * shift_re - base_im * shift_im  9.47 us
    another operation x1, other arithmetic, body(): jnp.stack([phase_re.T[:, :, None] * col_re[None] - phase_im.T[:, :, None]...  6.77 us
    another operation x1, other arithmetic  5.01 us
    ppermute x2, waiting for transfers between devices, group_sum(): value = value + lax.ppermute(value, 'grp', pairs)  4.89 us
    broadcast_in_dim x1, local copies, waits for them, and re-layouts, body(): jnp.broadcast_to(piece[:, None], (groups, members, parts, frame_count, lo...  2.55 us
  transfers between devices with their start and end apart: 3, of which 3 were waited for; matrix products, arithmetic and copies ran while one was open for 19% of the time, Pallas kernels for 0%

profile of v6, /device:TPU:0, one launch (start us, length us, event | category | flops | bytes accessed | tf_op | source)
XLA Modules:
  0.0 111.4 jit_solution(1424709956935357316)
XLA Ops:
  0.6 0.0 copy-start.1
  0.6 0.1 sine_negate_fusion
  0.8 0.1 fusion.49
  0.9 0.1 fusion.57
  1.0 0.1 fusion.61
  1.1 1.4 %reshape.528 = bf16[16,4,4096]{2,1,0:T(4,128)(2,1)S(1)} reshape(bf16[16,16384]{1,0:T(8,128)(2,1)} %param.5) | data formatting | bytes 1048576 | tf_op jit(solution)/shard_map/reshape | solution.py:24
  2.6 1.1 %fusion.75 = (bf16[16,1,4096]{2,1,0:T(2,128)(2,1)S(1)}, bf16[16,1,4096]{2,1,0:T(2,128)(2,1)S(1)}, bf16[16,1,4096]{2,1,0:T(2,128)(2,1)S(1)}, bf16[16,1,4096]{2,1,0:T(2,128)(2,1)S(1)}) fusion(bf16[16,4,4096]{2,1,0:T(4,128)(2,1)S(1)} %reshape.528), kind=kLoop, calls=%fused_computation.127 | loop fusion | bytes 1048576 | tf_op jit(solution)/shard_map/slice | solution.py:28
  3.7 0.0 copy-done.1
  3.8 0.7 multiply_add_fusion.1
  4.4 0.2 reshape.529
  4.7 0.2 copy.14
  4.9 0.4 fusion.33
  5.3 0.6 reshape.530
  5.9 1.1 fusion.74
  7.0 0.3 copy.23
  7.4 0.3 copy.24
  7.7 0.1 fusion.15
  7.9 0.9 fusion.9
  8.8 0.2 convert_element_type.124
  9.1 0.1 reshape_reshape.3
  9.2 2.5 %broadcast_in_dim.7 = bf16[4,32,2,16,512]{4,3,2,1,0:T(8,128)(2,1)} broadcast(bf16[4,2,16,512]{3,2,1,0:T(8,128)(2,1)S(1)} %bitcast.58), dimensions={0,2,3,4} | broadcast | bytes 4325376 | tf_op jit(solution)/shard_map/broadcast_in_dim | solution.py:160
  11.8 0.0 copy-start.2
  11.8 0.0 copy-start
  11.8 11.9 %all-to-all-start = ((bf16[128,2,1,16,512]{4,3,2,1,0:T(8,128)(2,1)}), bf16[128,2,1,16,512]{4,3,2,1,0:T(8,128)(2,1)}, u32[]{:S(2)}, u32[]{:S(2)}) async-start(bf16[128,2,1,16,512]{4,3,2,1,0:T(8,128)(2,1)} %bitcast.54), calls=%async_computation | async-start | bytes 8388608 | tf_op jit(solution)/shard_map/all_to_all | solution.py:163
  23.7 0.1 fusion.71
  23.8 0.0 copy-done.2
  23.8 0.0 copy-done
  23.8 0.1 fusion.55
  23.9 0.1 fusion.59
  24.0 0.4 fusion.17
  24.4 9.1 %fusion = (f32[2048,256]{1,0:T(8,128)S(1)}, f32[2048,256]{1,0:T(8,128)S(1)}) fusion(f32[256]{0:T(256)S(1)} %get-tuple-element.40, f32[256]{0:T(256)S(1)} %get-tuple-element.41, f32[2048]{0:T(1024)S(1)} %bitcast.65, f32[2048]{0:T(1024)S(1)} %bitcast.64, s32[2048]{0:T(1024)S(1)} %bitcast.63), kind=kLoop, calls=%fused_computation.8 | loop fusion | flops 12582912 | bytes 4220928 | tf_op jit(solution)/shard_map/sub | solution.py:63
  33.5 5.0 %subtract_convert_fusion = (bf16[1,8,2048,256]{3,2,1,0:T(8,128)(2,1)S(1)}, bf16[1,8,2048,256]{3,2,1,0:T(8,128)(2,1)S(1)}) fusion(f32[2048,256]{1,0:T(8,128)S(1)} %get-tuple-element.25, f32[8,2048]{1,0:T(8,128)S(1)} %get-tuple-element.27, f32[2048,256]{1,0:T(8,128)S(1)} %get-tuple-element.24, f32[8,2048]{1,0:T(8,128)S(1)} %get-tuple-element.26), kind=kLoop, calls=%fused_computation.2 | loop fusion | flops 33554432 | bytes 21102592 | tf_op jit(solution)/shard_map/convert
  38.5 6.8 %pad_maximum_fusion.spread_ref = bf16[2,8,2048,256]{3,2,1,0:T(8,128)(2,1)} fusion(bf16[1,8,2048,256]{3,2,1,0:T(8,128)(2,1)S(1)} %get-tuple-element.11, bf16[1,8,2048,256]{3,2,1,0:T(8,128)(2,1)S(1)} %get-tuple-element.10), kind=kLoop, calls=%fused_computation | loop fusion | flops 8388608 | bytes 33554432 | tf_op jit(solution)/shard_map/stack | solution.py:151
  45.3 30.9 %all-to-all-done.spectra_ref = bf16[128,2,1,16,512]{4,3,2,1,0:T(8,128)(2,1)} async-done(((bf16[128,2,1,16,512]{4,3,2,1,0:T(8,128)(2,1)}), bf16[128,2,1,16,512]{4,3,2,1,0:T(8,128)(2,1)}, u32[]{:S(2)}, u32[]{:S(2)}) %all-to-all-start) | async-done | bytes 4194336 | tf_op jit(solution)/shard_map/all_to_all | solution.py:163
  76.2 28.3 %shard_map.68 = (f32[512,8,256]{2,1,0:T(8,128)}, f32[8,1,256]{2,1,0:T(1,128)S(1)}) custom-call(bf16[128,2,1,16,512]{4,3,2,1,0:T(8,128)(2,1)} %all-to-all-done.spectra_ref, bf16[2,8,2048,256]{3,2,1,0:T(8,128)(2,1)} %pad_maximum_fusion.spread_ref, f32[512,8,256]{2,1,0:T(8,128)} %sky_ref.1), custom_call_target="tpu_custom_call" | custom-call | flops 17179869184 | bytes 29360128 | tf_op jit(solution)/shard_map/pallas_call | solution.py:99
  104.5 0.0 collective-permute-start
  104.5 1.2 %collective-permute-done = f32[8,256]{1,0:T(8,128)S(1)} collective-permute-done((f32[8,256]{1,0:T(8,128)S(1)}, f32[8,256]{1,0:T(8,128)S(1)}, u32[]{:S(2)}, u32[]{:S(2)}) %collective-permute-start) | collective-permute-done | bytes 8224 | tf_op jit(solution)/shard_map/ppermute | solution.py:129
  105.6 1.4 %collective-permute-start.1 = (f32[8,256]{1,0:T(8,128)S(1)}, f32[8,256]{1,0:T(8,128)S(1)}, u32[]{:S(2)}, u32[]{:S(2)}) collective-permute-start(f32[8,256]{1,0:T(8,128)S(1)} %fusion.73), channel_id=1, source_target_pairs={{0,64},{32,96},{64,0},{96,32},{1,65},{33,97},{65,1},{97,33},{2,66}... | collective-permute-start | bytes 24584 | tf_op jit(solution)/shard_map/ppermute | solution.py:129
  107.1 3.7 %collective-permute-done.1 = f32[8,256]{1,0:T(8,128)S(1)} collective-permute-done((f32[8,256]{1,0:T(8,128)S(1)}, f32[8,256]{1,0:T(8,128)S(1)}, u32[]{:S(2)}, u32[]{:S(2)}) %collective-permute-start.1) | collective-permute-done | bytes 8224 | tf_op jit(solution)/shard_map/ppermute | solution.py:129
  110.8 0.6 add_multiply_fusion
  (7 shorter events, 0.2 us)
Async XLA Ops:
  0.6 3.1 %copy-start.1 = (f32[4,4096]{1,0:T(4,128)S(1)}, f32[4,4096]{1,0:T(4,128)}, u32[]{:S(2)}) copy-start(f32[4,4096]{1,0:T(4,128)} %param.6) | copy-start | bytes 196612
  11.8 12.0 %copy-start.2 = (s32[2048,2]{0,1:T(2,128)S(1)}, s32[2048,2]{0,1:T(2,128)}, u32[]{:S(2)}) copy-start(s32[2048,2]{0,1:T(2,128)} %param.7) | copy-start | bytes 49156
  11.8 12.0 %copy-start = (s32[2048,2]{0,1:T(2,128)S(1)}, s32[2048,2]{0,1:T(2,128)}, u32[]{:S(2)}) copy-start(s32[2048,2]{0,1:T(2,128)} %param.8) | copy-start | bytes 49156
  11.8 64.4 %all-to-all-start = ((bf16[128,2,1,16,512]{4,3,2,1,0:T(8,128)(2,1)}), bf16[128,2,1,16,512]{4,3,2,1,0:T(8,128)(2,1)}, u32[]{:S(2)}, u32[]{:S(2)}) async-start(bf16[128,2,1,16,512]{4,3,2,1,0:T(8,128)(2,1)} %bitcast.54), calls=%async_computation | async-start | bytes 8388608 | tf_op jit(solution)/shard_map/all_to_all | solution.py:163
  104.5 1.2 %collective-permute-start = (f32[8,256]{1,0:T(8,128)S(1)}, f32[8,256]{1,0:T(8,128)S(1)}, u32[]{:S(2)}, u32[]{:S(2)}) collective-permute-start(f32[8,256]{1,0:T(8,128)S(1)} %bitcast.69), channel_id=1, source_target_pairs={{0,32},{32,0},{64,96},{96,64},{1,33},{33,1},{65,97},{97,65},{2,34}... | collective-permute-start | bytes 24584 | tf_op jit(solution)/shard_map/ppermute | solution.py:129
  105.6 5.2 %collective-permute-start.1 = (f32[8,256]{1,0:T(8,128)S(1)}, f32[8,256]{1,0:T(8,128)S(1)}, u32[]{:S(2)}, u32[]{:S(2)}) collective-permute-start(f32[8,256]{1,0:T(8,128)S(1)} %fusion.73), channel_id=1, source_target_pairs={{0,64},{32,96},{64,0},{96,32},{1,65},{33,97},{65,1},{97,33},{2,66}... | collective-permute-start | bytes 24584 | tf_op jit(solution)/shard_map/ppermute | solution.py:129

commit v7 on v6

--- a/solution.py
+++ b/solution.py
@@ -70,15 +70,13 @@
     sources, _, _, local, span = spectra_ref.shape
     spec_re = spectra_ref[:, 0, 0].reshape(sources * local, span)
     spec_im = spectra_ref[:, 1, 0].reshape(sources * local, span)
-    table_re = spread_ref[0, 0]
-    table_im = spread_ref[1, 0]
+    table = spread_ref[0]
+    width = table.shape[1] // 2
     f32 = jnp.float32
-    sky_re = lax.dot_general(spec_re, table_re, contract, preferred_element_type=f32) - lax.dot_general(
-        spec_im, table_im, contract, preferred_element_type=f32
-    )
-    sky_im = lax.dot_general(spec_re, table_im, contract, preferred_element_type=f32) + lax.dot_general(
-        spec_im, table_re, contract, preferred_element_type=f32
-    )
+    from_re = lax.dot_general(spec_re, table, contract, preferred_element_type=f32)
+    from_im = lax.dot_general(spec_im, table, contract, preferred_element_type=f32)
+    sky_re = from_re[:, :width] - from_im[:, width:]
+    sky_im = from_re[:, width:] + from_im[:, :width]
     power = (sky_re * sky_re + sky_im * sky_im) * norm_scale
     row = pl.program_id(0)
     for index in range(out_ref.shape[1]):
@@ -93,7 +91,8 @@
 def image_block(incoming, spread, sky_model, norm_scale):
     sources, parts, frame_count, local, span = incoming.shape
     dipoles = sources * local
-    _, rows_mine, _, grid_len = spread.shape
+    rows_mine, _, grid_len = spread.shape
+    grid_len = grid_len // 2
     stacked = incoming
     flat_sky = sky_model
     residual, band = pl.pallas_call(
@@ -101,7 +100,7 @@
         grid=(rows_mine,),
         in_specs=[
             pl.BlockSpec((sources, parts, frame_count, local, span), lambda m: (0, 0, 0, 0, 0)),
-            pl.BlockSpec((2, 1, dipoles, grid_len), lambda m: (0, m, 0, 0)),
+            pl.BlockSpec((1, dipoles, 2 * grid_len), lambda m: (m, 0, 0)),
             pl.BlockSpec((span, rows_mine, grid_len), lambda m: (0, 0, 0)),
         ],
         out_specs=[
@@ -148,12 +147,12 @@
     phase_re, phase_im = row_phases(dipole_cells[:, 0], kernel_bits[:, 0], rows, grid_len)
     cols = lax.broadcasted_iota(jnp.int32, (grid_len,), 0)
     col_re, col_im = row_phases(dipole_cells[:, 1], kernel_bits[:, 1], cols, grid_len)
-    spread = jnp.stack(
+    spread = jnp.concatenate(
         [
             phase_re.T[:, :, None] * col_re[None] - phase_im.T[:, :, None] * col_im[None],
             phase_re.T[:, :, None] * col_im[None] + phase_im.T[:, :, None] * col_re[None],
         ],
-        axis=0,
+        axis=2,
     ).astype(jnp.bfloat16)
     norm_scale = 1.0 / (frame_count * dipoles)
     piece = by_block.reshape(parts, frame_count, local, groups, block).transpose(3, 0, 1, 2, 4)

time: 112 us -> 112 us (level)
    another operation x2 -> x1, other arithmetic: 11.8 us -> 5.01 us  [the longest x1 6.77 us: body(): jnp.stack([phase_re.T[:, :, None] * col_re[None] - phase_im.T[:, :, None]...]
    concatenate x0 -> x1, other arithmetic: none -> 6.68 us  [body(): jnp.concatenate([phase_re.T[:, :, None] * col_re[None] - phase_im.T[:, :,...]
where the time goes in v7:
time: 112 us; the launch traced here: 111 us
  waiting for transfers between devices  35.9 us (32%)
  Pallas kernels  28.2 us (25%)
  other arithmetic  23.3 us (21%)
  starting transfers between devices  13.3 us (12%)
  local copies, waits for them, and re-layouts  8.4 us (8%)
  matrix products  1.37 us (1%)
    all_to_all x1, waiting for transfers between devices, body(): lax.all_to_all(outgoing, ('grp', 'dev'), split_axis=0, concat_axis=0, til...  31 us
    pallas_call x1, Pallas kernels, image_block(): pl.pallas_call(functools.partial(image_kernel, norm_scale), grid=(rows_mi...  28.2 us
    all_to_all x1, starting transfers between devices, body(): lax.all_to_all(outgoing, ('grp', 'dev'), split_axis=0, concat_axis=0, til...  11.9 us
    sub x2, other arithmetic, row_phases(): real = base_re * shift_re - base_im * shift_im  9.47 us
    concatenate x1, other arithmetic, body(): jnp.concatenate([phase_re.T[:, :, None] * col_re[None] - phase_im.T[:, :,...  6.68 us
    another operation x1, other arithmetic  5.01 us
    ppermute x2, waiting for transfers between devices, group_sum(): value = value + lax.ppermute(value, 'grp', pairs)  4.9 us
    broadcast_in_dim x1, local copies, waits for them, and re-layouts, body(): jnp.broadcast_to(piece[:, None], (groups, members, parts, frame_count, lo...  2.55 us
  transfers between devices with their start and end apart: 3, of which 3 were waited for; matrix products, arithmetic and copies ran while one was open for 19% of the time, Pallas kernels for 0%

profile of v7, /device:TPU:0, one launch (start us, length us, event | category | flops | bytes accessed | tf_op | source)
XLA Modules:
  0.0 111.3 jit_solution(3727209604683048868)
XLA Ops:
  0.6 0.0 copy-start.1
  0.6 0.1 sine_negate_fusion
  0.8 0.1 fusion.49
  0.9 0.1 fusion.57
  1.0 0.1 fusion.61
  1.1 1.4 %reshape.510 = bf16[16,4,4096]{2,1,0:T(4,128)(2,1)S(1)} reshape(bf16[16,16384]{1,0:T(8,128)(2,1)} %param.5) | data formatting | bytes 1048576 | tf_op jit(solution)/shard_map/reshape | solution.py:24
  2.6 1.1 %fusion.75 = (bf16[16,1,4096]{2,1,0:T(2,128)(2,1)S(1)}, bf16[16,1,4096]{2,1,0:T(2,128)(2,1)S(1)}, bf16[16,1,4096]{2,1,0:T(2,128)(2,1)S(1)}, bf16[16,1,4096]{2,1,0:T(2,128)(2,1)S(1)}) fusion(bf16[16,4,4096]{2,1,0:T(4,128)(2,1)S(1)} %reshape.510), kind=kLoop, calls=%fused_computation.127 | loop fusion | bytes 1048576 | tf_op jit(solution)/shard_map/slice | solution.py:28
  3.7 0.0 copy-done.1
  3.8 0.7 multiply_add_fusion.1
  4.4 0.2 reshape.511
  4.7 0.2 copy.14
  4.9 0.4 fusion.33
  5.3 0.6 reshape.512
  5.9 1.1 fusion.74
  7.0 0.3 copy.23
  7.4 0.3 copy.24
  7.7 0.1 fusion.15
  7.9 0.9 fusion.9
  8.8 0.2 convert_element_type.124
  9.1 0.1 reshape_reshape.3
  9.2 2.5 %broadcast_in_dim.7 = bf16[4,32,2,16,512]{4,3,2,1,0:T(8,128)(2,1)} broadcast(bf16[4,2,16,512]{3,2,1,0:T(8,128)(2,1)S(1)} %bitcast.58), dimensions={0,2,3,4} | broadcast | bytes 4325376 | tf_op jit(solution)/shard_map/broadcast_in_dim | solution.py:159
  11.8 0.0 copy-start.2
  11.8 0.0 copy-start
  11.8 11.9 %all-to-all-start = ((bf16[128,2,1,16,512]{4,3,2,1,0:T(8,128)(2,1)}), bf16[128,2,1,16,512]{4,3,2,1,0:T(8,128)(2,1)}, u32[]{:S(2)}, u32[]{:S(2)}) async-start(bf16[128,2,1,16,512]{4,3,2,1,0:T(8,128)(2,1)} %bitcast.54), calls=%async_computation | async-start | bytes 8388608 | tf_op jit(solution)/shard_map/all_to_all | solution.py:162
  23.7 0.1 fusion.71
  23.8 0.0 copy-done.2
  23.8 0.0 copy-done
  23.8 0.1 fusion.55
  23.9 0.1 fusion.59
  24.0 0.4 fusion.17
  24.4 9.1 %fusion = (f32[2048,256]{1,0:T(8,128)S(1)}, f32[2048,256]{1,0:T(8,128)S(1)}) fusion(f32[256]{0:T(256)S(1)} %get-tuple-element.40, f32[256]{0:T(256)S(1)} %get-tuple-element.41, f32[2048]{0:T(1024)S(1)} %bitcast.65, f32[2048]{0:T(1024)S(1)} %bitcast.64, s32[2048]{0:T(1024)S(1)} %bitcast.63), kind=kLoop, calls=%fused_computation.8 | loop fusion | flops 12582912 | bytes 4220928 | tf_op jit(solution)/shard_map/sub | solution.py:63
  33.5 5.0 %subtract_convert_fusion = (bf16[8,2048,256]{2,1,0:T(8,128)(2,1)S(1)}, bf16[8,2048,256]{2,1,0:T(8,128)(2,1)S(1)}) fusion(f32[2048,256]{1,0:T(8,128)S(1)} %get-tuple-element.25, f32[8,2048]{1,0:T(8,128)S(1)} %get-tuple-element.27, f32[2048,256]{1,0:T(8,128)S(1)} %get-tuple-element.24, f32[8,2048]{1,0:T(8,128)S(1)} %get-tuple-element.26), kind=kLoop, calls=%fused_computation.2 | loop fusion | flops 33554432 | bytes 21102592 | tf_op jit(solution)/shard_map/convert
  38.5 6.7 %pad_maximum_fusion.spread_ref = bf16[8,2048,512]{2,1,0:T(8,128)(2,1)} fusion(bf16[8,2048,256]{2,1,0:T(8,128)(2,1)S(1)} %get-tuple-element.11, bf16[8,2048,256]{2,1,0:T(8,128)(2,1)S(1)} %get-tuple-element.10), kind=kLoop, calls=%fused_computation | loop fusion | flops 33554432 | bytes 33554432 | tf_op jit(solution)/shard_map/concatenate | solution.py:150
  45.2 31.0 %all-to-all-done.spectra_ref = bf16[128,2,1,16,512]{4,3,2,1,0:T(8,128)(2,1)} async-done(((bf16[128,2,1,16,512]{4,3,2,1,0:T(8,128)(2,1)}), bf16[128,2,1,16,512]{4,3,2,1,0:T(8,128)(2,1)}, u32[]{:S(2)}, u32[]{:S(2)}) %all-to-all-start) | async-done | bytes 4194336 | tf_op jit(solution)/shard_map/all_to_all | solution.py:162
  76.2 28.2 %shard_map.68 = (f32[512,8,256]{2,1,0:T(8,128)}, f32[8,1,256]{2,1,0:T(1,128)S(1)}) custom-call(bf16[128,2,1,16,512]{4,3,2,1,0:T(8,128)(2,1)} %all-to-all-done.spectra_ref, bf16[8,2048,512]{2,1,0:T(8,128)(2,1)} %pad_maximum_fusion.spread_ref, f32[512,8,256]{2,1,0:T(8,128)} %sky_ref.1), custom_call_target="tpu_custom_call" | custom-call | flops 17179869184 | bytes 29360128 | tf_op jit(solution)/shard_map/pallas_call | solution.py:98
  104.3 0.0 collective-permute-start
  104.3 1.2 %collective-permute-done = f32[8,256]{1,0:T(8,128)S(1)} collective-permute-done((f32[8,256]{1,0:T(8,128)S(1)}, f32[8,256]{1,0:T(8,128)S(1)}, u32[]{:S(2)}, u32[]{:S(2)}) %collective-permute-start) | collective-permute-done | bytes 8224 | tf_op jit(solution)/shard_map/ppermute | solution.py:128
  105.5 1.4 %collective-permute-start.1 = (f32[8,256]{1,0:T(8,128)S(1)}, f32[8,256]{1,0:T(8,128)S(1)}, u32[]{:S(2)}, u32[]{:S(2)}) collective-permute-start(f32[8,256]{1,0:T(8,128)S(1)} %fusion.73), channel_id=1, source_target_pairs={{0,64},{32,96},{64,0},{96,32},{1,65},{33,97},{65,1},{97,33},{2,66}... | collective-permute-start | bytes 24584 | tf_op jit(solution)/shard_map/ppermute | solution.py:128
  106.9 3.7 %collective-permute-done.1 = f32[8,256]{1,0:T(8,128)S(1)} collective-permute-done((f32[8,256]{1,0:T(8,128)S(1)}, f32[8,256]{1,0:T(8,128)S(1)}, u32[]{:S(2)}, u32[]{:S(2)}) %collective-permute-start.1) | collective-permute-done | bytes 8224 | tf_op jit(solution)/shard_map/ppermute | solution.py:128
  110.7 0.6 add_multiply_fusion
  (7 shorter events, 0.2 us)
Async XLA Ops:
  0.6 3.1 %copy-start.1 = (f32[4,4096]{1,0:T(4,128)S(1)}, f32[4,4096]{1,0:T(4,128)}, u32[]{:S(2)}) copy-start(f32[4,4096]{1,0:T(4,128)} %param.6) | copy-start | bytes 196612
  11.8 12.0 %copy-start.2 = (s32[2048,2]{0,1:T(2,128)S(1)}, s32[2048,2]{0,1:T(2,128)}, u32[]{:S(2)}) copy-start(s32[2048,2]{0,1:T(2,128)} %param.7) | copy-start | bytes 49156
  11.8 12.0 %copy-start = (s32[2048,2]{0,1:T(2,128)S(1)}, s32[2048,2]{0,1:T(2,128)}, u32[]{:S(2)}) copy-start(s32[2048,2]{0,1:T(2,128)} %param.8) | copy-start | bytes 49156
  11.8 64.4 %all-to-all-start = ((bf16[128,2,1,16,512]{4,3,2,1,0:T(8,128)(2,1)}), bf16[128,2,1,16,512]{4,3,2,1,0:T(8,128)(2,1)}, u32[]{:S(2)}, u32[]{:S(2)}) async-start(bf16[128,2,1,16,512]{4,3,2,1,0:T(8,128)(2,1)} %bitcast.54), calls=%async_computation | async-start | bytes 8388608 | tf_op jit(solution)/shard_map/all_to_all | solution.py:162
  104.3 1.2 %collective-permute-start = (f32[8,256]{1,0:T(8,128)S(1)}, f32[8,256]{1,0:T(8,128)S(1)}, u32[]{:S(2)}, u32[]{:S(2)}) collective-permute-start(f32[8,256]{1,0:T(8,128)S(1)} %bitcast.69), channel_id=1, source_target_pairs={{0,32},{32,0},{64,96},{96,64},{1,33},{33,1},{65,97},{97,65},{2,34}... | collective-permute-start | bytes 24584 | tf_op jit(solution)/shard_map/ppermute | solution.py:128
  105.5 5.2 %collective-permute-start.1 = (f32[8,256]{1,0:T(8,128)S(1)}, f32[8,256]{1,0:T(8,128)S(1)}, u32[]{:S(2)}, u32[]{:S(2)}) collective-permute-start(f32[8,256]{1,0:T(8,128)S(1)} %fusion.73), channel_id=1, source_target_pairs={{0,64},{32,96},{64,0},{96,32},{1,65},{33,97},{65,1},{97,33},{2,66}... | collective-permute-start | bytes 24584 | tf_op jit(solution)/shard_map/ppermute | solution.py:128

commit v8 on v7

--- a/solution.py
+++ b/solution.py
@@ -65,20 +65,23 @@
     return real, imag
 
 
-def image_kernel(norm_scale, spectra_ref, spread_ref, sky_ref, out_ref, band_ref):
-    contract = (((0,), (0,)), ((), ()))
+def image_kernel(norm_scale, spectra_ref, spread_ref, sky_ref, out_ref, band_ref, turned_ref):
     sources, _, _, local, span = spectra_ref.shape
-    spec_re = spectra_ref[:, 0, 0].reshape(sources * local, span)
-    spec_im = spectra_ref[:, 1, 0].reshape(sources * local, span)
+    row = pl.program_id(0)
+
+    @pl.when(row == 0)
+    def _():
+        for part in range(2):
+            turned_ref[part] = spectra_ref[:, part, 0].reshape(sources * local, span).T
+
     table = spread_ref[0]
     width = table.shape[1] // 2
     f32 = jnp.float32
-    from_re = lax.dot_general(spec_re, table, contract, preferred_element_type=f32)
-    from_im = lax.dot_general(spec_im, table, contract, preferred_element_type=f32)
+    from_re = jnp.dot(turned_ref[0], table, preferred_element_type=f32)
+    from_im = jnp.dot(turned_ref[1], table, preferred_element_type=f32)
     sky_re = from_re[:, :width] - from_im[:, width:]
     sky_im = from_re[:, width:] + from_im[:, :width]
     power = (sky_re * sky_re + sky_im * sky_im) * norm_scale
-    row = pl.program_id(0)
     for index in range(out_ref.shape[1]):
 
         @pl.when(row == index)
@@ -111,6 +114,7 @@
             jax.ShapeDtypeStruct((span, rows_mine, grid_len), jnp.float32),
             jax.ShapeDtypeStruct((rows_mine, 1, grid_len), jnp.float32),
         ],
+        scratch_shapes=[pltpu.VMEM((parts, span, dipoles), jnp.bfloat16)],
         compiler_params=pltpu.CompilerParams(vmem_limit_bytes=48 * 1024 * 1024),
         cost_estimate=pl.CostEstimate(
             flops=8 * span * dipoles * rows_mine * grid_len,

time: 112 us -> 113 us (level)
  no operation moved by 1% of the time
where the time goes in v8:
time: 113 us; the launch traced here: 112 us
  waiting for transfers between devices  35.9 us (32%)
  Pallas kernels  29.2 us (26%)
  other arithmetic  23.3 us (21%)
  starting transfers between devices  13.3 us (12%)
  local copies, waits for them, and re-layouts  8.4 us (7%)
  matrix products  1.37 us (1%)
    all_to_all x1, waiting for transfers between devices, body(): lax.all_to_all(outgoing, ('grp', 'dev'), split_axis=0, concat_axis=0, til...  31 us
    pallas_call x1, Pallas kernels, image_block(): pl.pallas_call(functools.partial(image_kernel, norm_scale), grid=(rows_mi...  29.2 us
    all_to_all x1, starting transfers between devices, body(): lax.all_to_all(outgoing, ('grp', 'dev'), split_axis=0, concat_axis=0, til...  11.9 us
    sub x2, other arithmetic, row_phases(): real = base_re * shift_re - base_im * shift_im  9.47 us
    concatenate x1, other arithmetic, body(): jnp.concatenate([phase_re.T[:, :, None] * col_re[None] - phase_im.T[:, :,...  6.68 us
    another operation x1, other arithmetic  5.01 us
    ppermute x2, waiting for transfers between devices, group_sum(): value = value + lax.ppermute(value, 'grp', pairs)  4.89 us
    broadcast_in_dim x1, local copies, waits for them, and re-layouts, body(): jnp.broadcast_to(piece[:, None], (groups, members, parts, frame_count, lo...  2.55 us
  transfers between devices with their start and end apart: 3, of which 3 were waited for; matrix products, arithmetic and copies ran while one was open for 19% of the time, Pallas kernels for 0%

profile of v8, /device:TPU:0, one launch (start us, length us, event | category | flops | bytes accessed | tf_op | source)
XLA Modules:
  0.0 112.3 jit_solution(4242556769246199616)
XLA Ops:
  0.6 0.0 copy-start.1
  0.6 0.1 sine_negate_fusion
  0.8 0.1 fusion.49
  0.9 0.1 fusion.57
  1.0 0.1 fusion.61
  1.1 1.4 %reshape.510 = bf16[16,4,4096]{2,1,0:T(4,128)(2,1)S(1)} reshape(bf16[16,16384]{1,0:T(8,128)(2,1)} %param.5) | data formatting | bytes 1048576 | tf_op jit(solution)/shard_map/reshape | solution.py:24
  2.6 1.1 %fusion.75 = (bf16[16,1,4096]{2,1,0:T(2,128)(2,1)S(1)}, bf16[16,1,4096]{2,1,0:T(2,128)(2,1)S(1)}, bf16[16,1,4096]{2,1,0:T(2,128)(2,1)S(1)}, bf16[16,1,4096]{2,1,0:T(2,128)(2,1)S(1)}) fusion(bf16[16,4,4096]{2,1,0:T(4,128)(2,1)S(1)} %reshape.510), kind=kLoop, calls=%fused_computation.127 | loop fusion | bytes 1048576 | tf_op jit(solution)/shard_map/slice | solution.py:28
  3.7 0.0 copy-done.1
  3.8 0.7 multiply_add_fusion.1
  4.4 0.2 reshape.511
  4.7 0.2 copy.14
  4.9 0.4 fusion.33
  5.3 0.6 reshape.512
  5.9 1.1 fusion.74
  7.0 0.3 copy.23
  7.4 0.3 copy.24
  7.7 0.1 fusion.15
  7.9 0.9 fusion.9
  8.8 0.2 convert_element_type.124
  9.1 0.1 reshape_reshape.3
  9.2 2.5 %broadcast_in_dim.7 = bf16[4,32,2,16,512]{4,3,2,1,0:T(8,128)(2,1)} broadcast(bf16[4,2,16,512]{3,2,1,0:T(8,128)(2,1)S(1)} %bitcast.58), dimensions={0,2,3,4} | broadcast | bytes 4325376 | tf_op jit(solution)/shard_map/broadcast_in_dim | solution.py:163
  11.8 0.0 copy-start.2
  11.8 0.0 copy-start
  11.8 11.9 %all-to-all-start = ((bf16[128,2,1,16,512]{4,3,2,1,0:T(8,128)(2,1)}), bf16[128,2,1,16,512]{4,3,2,1,0:T(8,128)(2,1)}, u32[]{:S(2)}, u32[]{:S(2)}) async-start(bf16[128,2,1,16,512]{4,3,2,1,0:T(8,128)(2,1)} %bitcast.54), calls=%async_computation | async-start | bytes 8388608 | tf_op jit(solution)/shard_map/all_to_all | solution.py:166
  23.7 0.1 fusion.71
  23.8 0.0 copy-done.2
  23.8 0.0 copy-done
  23.8 0.1 fusion.55
  23.9 0.1 fusion.59
  24.0 0.4 fusion.17
  24.4 9.1 %fusion = (f32[2048,256]{1,0:T(8,128)S(1)}, f32[2048,256]{1,0:T(8,128)S(1)}) fusion(f32[256]{0:T(256)S(1)} %get-tuple-element.40, f32[256]{0:T(256)S(1)} %get-tuple-element.41, f32[2048]{0:T(1024)S(1)} %bitcast.65, f32[2048]{0:T(1024)S(1)} %bitcast.64, s32[2048]{0:T(1024)S(1)} %bitcast.63), kind=kLoop, calls=%fused_computation.8 | loop fusion | flops 12582912 | bytes 4220928 | tf_op jit(solution)/shard_map/sub | solution.py:63
  33.5 5.0 %subtract_convert_fusion = (bf16[8,2048,256]{2,1,0:T(8,128)(2,1)S(1)}, bf16[8,2048,256]{2,1,0:T(8,128)(2,1)S(1)}) fusion(f32[2048,256]{1,0:T(8,128)S(1)} %get-tuple-element.25, f32[8,2048]{1,0:T(8,128)S(1)} %get-tuple-element.27, f32[2048,256]{1,0:T(8,128)S(1)} %get-tuple-element.24, f32[8,2048]{1,0:T(8,128)S(1)} %get-tuple-element.26), kind=kLoop, calls=%fused_computation.2 | loop fusion | flops 33554432 | bytes 21102592 | tf_op jit(solution)/shard_map/convert
  38.5 6.7 %pad_maximum_fusion.spread_ref = bf16[8,2048,512]{2,1,0:T(8,128)(2,1)} fusion(bf16[8,2048,256]{2,1,0:T(8,128)(2,1)S(1)} %get-tuple-element.11, bf16[8,2048,256]{2,1,0:T(8,128)(2,1)S(1)} %get-tuple-element.10), kind=kLoop, calls=%fused_computation | loop fusion | flops 33554432 | bytes 33554432 | tf_op jit(solution)/shard_map/concatenate | solution.py:154
  45.2 31.0 %all-to-all-done.spectra_ref = bf16[128,2,1,16,512]{4,3,2,1,0:T(8,128)(2,1)} async-done(((bf16[128,2,1,16,512]{4,3,2,1,0:T(8,128)(2,1)}), bf16[128,2,1,16,512]{4,3,2,1,0:T(8,128)(2,1)}, u32[]{:S(2)}, u32[]{:S(2)}) %all-to-all-start) | async-done | bytes 4194336 | tf_op jit(solution)/shard_map/all_to_all | solution.py:166
  76.2 29.2 %shard_map.68 = (f32[512,8,256]{2,1,0:T(8,128)}, f32[8,1,256]{2,1,0:T(1,128)S(1)}) custom-call(bf16[128,2,1,16,512]{4,3,2,1,0:T(8,128)(2,1)} %all-to-all-done.spectra_ref, bf16[8,2048,512]{2,1,0:T(8,128)(2,1)} %pad_maximum_fusion.spread_ref, f32[512,8,256]{2,1,0:T(8,128)} %sky_ref.1), custom_call_target="tpu_custom_call" | custom-call | flops 17179869184 | bytes 29360128 | tf_op jit(solution)/shard_map/pallas_call | solution.py:101
  105.4 0.0 collective-permute-start
  105.4 1.2 %collective-permute-done = f32[8,256]{1,0:T(8,128)S(1)} collective-permute-done((f32[8,256]{1,0:T(8,128)S(1)}, f32[8,256]{1,0:T(8,128)S(1)}, u32[]{:S(2)}, u32[]{:S(2)}) %collective-permute-start) | collective-permute-done | bytes 8224 | tf_op jit(solution)/shard_map/ppermute | solution.py:132
  106.6 1.4 %collective-permute-start.1 = (f32[8,256]{1,0:T(8,128)S(1)}, f32[8,256]{1,0:T(8,128)S(1)}, u32[]{:S(2)}, u32[]{:S(2)}) collective-permute-start(f32[8,256]{1,0:T(8,128)S(1)} %fusion.73), channel_id=1, source_target_pairs={{0,64},{32,96},{64,0},{96,32},{1,65},{33,97},{65,1},{97,33},{2,66}... | collective-permute-start | bytes 24584 | tf_op jit(solution)/shard_map/ppermute | solution.py:132
  108.0 3.7 %collective-permute-done.1 = f32[8,256]{1,0:T(8,128)S(1)} collective-permute-done((f32[8,256]{1,0:T(8,128)S(1)}, f32[8,256]{1,0:T(8,128)S(1)}, u32[]{:S(2)}, u32[]{:S(2)}) %collective-permute-start.1) | collective-permute-done | bytes 8224 | tf_op jit(solution)/shard_map/ppermute | solution.py:132
  111.7 0.6 add_multiply_fusion
  (7 shorter events, 0.2 us)
Async XLA Ops:
  0.6 3.1 %copy-start.1 = (f32[4,4096]{1,0:T(4,128)S(1)}, f32[4,4096]{1,0:T(4,128)}, u32[]{:S(2)}) copy-start(f32[4,4096]{1,0:T(4,128)} %param.6) | copy-start | bytes 196612
  11.8 12.0 %copy-start.2 = (s32[2048,2]{0,1:T(2,128)S(1)}, s32[2048,2]{0,1:T(2,128)}, u32[]{:S(2)}) copy-start(s32[2048,2]{0,1:T(2,128)} %param.7) | copy-start | bytes 49156
  11.8 12.0 %copy-start = (s32[2048,2]{0,1:T(2,128)S(1)}, s32[2048,2]{0,1:T(2,128)}, u32[]{:S(2)}) copy-start(s32[2048,2]{0,1:T(2,128)} %param.8) | copy-start | bytes 49156
  11.8 64.4 %all-to-all-start = ((bf16[128,2,1,16,512]{4,3,2,1,0:T(8,128)(2,1)}), bf16[128,2,1,16,512]{4,3,2,1,0:T(8,128)(2,1)}, u32[]{:S(2)}, u32[]{:S(2)}) async-start(bf16[128,2,1,16,512]{4,3,2,1,0:T(8,128)(2,1)} %bitcast.54), calls=%async_computation | async-start | bytes 8388608 | tf_op jit(solution)/shard_map/all_to_all | solution.py:166
  105.4 1.2 %collective-permute-start = (f32[8,256]{1,0:T(8,128)S(1)}, f32[8,256]{1,0:T(8,128)S(1)}, u32[]{:S(2)}, u32[]{:S(2)}) collective-permute-start(f32[8,256]{1,0:T(8,128)S(1)} %bitcast.69), channel_id=1, source_target_pairs={{0,32},{32,0},{64,96},{96,64},{1,33},{33,1},{65,97},{97,65},{2,34}... | collective-permute-start | bytes 24584 | tf_op jit(solution)/shard_map/ppermute | solution.py:132
  106.6 5.2 %collective-permute-start.1 = (f32[8,256]{1,0:T(8,128)S(1)}, f32[8,256]{1,0:T(8,128)S(1)}, u32[]{:S(2)}, u32[]{:S(2)}) collective-permute-start(f32[8,256]{1,0:T(8,128)S(1)} %fusion.73), channel_id=1, source_target_pairs={{0,64},{32,96},{64,0},{96,32},{1,65},{33,97},{65,1},{97,33},{2,66}... | collective-permute-start | bytes 24584 | tf_op jit(solution)/shard_map/ppermute | solution.py:132

commit v9 on v7

--- a/solution.py
+++ b/solution.py
@@ -122,12 +122,18 @@
 
 
 def group_sum(value, groups):
-    stride = 1
-    while stride < groups:
-        pairs = [(i, i ^ stride) for i in range(groups)]
-        value = value + lax.ppermute(value, "grp", pairs)
-        stride = stride * 2
-    return value
+    me = lax.axis_index("grp")
+    slots = [jnp.zeros_like(value) for _ in range(groups)]
+    for shift in range(groups):
+        if shift == 0:
+            moved = value
+        else:
+            moved = lax.ppermute(value, "grp", [(i, (i + shift) % groups) for i in range(groups)])
+        source = (me - shift) % groups
+        slots = [jnp.where(source == slot, moved, held) for slot, held in enumerate(slots)]
+    while len(slots) > 1:
+        slots = [slots[i] + slots[i + 1] for i in range(0, len(slots), 2)]
+    return slots[0]
 
 
 def body(voltages, filter_taps, dipole_cells, kernel_bits, sky_model):

time: 112 us -> 112 us (level)
  starting transfers between devices: 13.3 us -> 14.6 us
    ppermute x2 -> x3, starting transfers between devices: 1.42 us -> 2.66 us  [group_sum(): lax.ppermute(value, 'grp', [(i, (i + shift) % groups) for i in range(grou...]
    ppermute x2 -> x3, waiting for transfers between devices: 4.9 us -> 4.58 us  [group_sum(): lax.ppermute(value, 'grp', [(i, (i + shift) % groups) for i in range(grou...]
  transfers between devices with their start and end apart: 3 -> 4, of which waited for: 3 -> 3; matrix products, arithmetic and copies ran while one was open for 19% -> 19% of each run, Pallas kernels for 0% -> 0%
where the time goes in v9:
time: 112 us
  waiting for transfers between devices  35.5 us (32%)
  Pallas kernels  28.2 us (25%)
  other arithmetic  23.3 us (21%)
  starting transfers between devices  14.6 us (13%)
  local copies, waits for them, and re-layouts  8.4 us (8%)
  matrix products  1.37 us (1%)
    all_to_all x1, waiting for transfers between devices, body(): lax.all_to_all(outgoing, ('grp', 'dev'), split_axis=0, concat_axis=0, til...  31 us
    pallas_call x1, Pallas kernels, image_block(): pl.pallas_call(functools.partial(image_kernel, norm_scale), grid=(rows_mi...  28.2 us
    all_to_all x1, starting transfers between devices, body(): lax.all_to_all(outgoing, ('grp', 'dev'), split_axis=0, concat_axis=0, til...  11.9 us
    sub x2, other arithmetic, row_phases(): real = base_re * shift_re - base_im * shift_im  9.47 us
    concatenate x1, other arithmetic, body(): jnp.concatenate([phase_re.T[:, :, None] * col_re[None] - phase_im.T[:, :,...  6.69 us
    another operation x1, other arithmetic  5.01 us
    ppermute x3, waiting for transfers between devices, group_sum(): lax.ppermute(value, 'grp', [(i, (i + shift) % groups) for i in range(grou...  4.58 us
    ppermute x3, starting transfers between devices, group_sum(): lax.ppermute(value, 'grp', [(i, (i + shift) % groups) for i in range(grou...  2.66 us
  transfers between devices with their start and end apart: 4, of which 3 were waited for; matrix products, arithmetic and copies ran while one was open for 19% of the time, Pallas kernels for 0%

profile of v9, /device:TPU:0, one launch (start us, length us, event | category | flops | bytes accessed | tf_op | source)
XLA Modules:
  0.0 112.2 jit_solution(7703910679740738037)
XLA Ops:
  0.6 0.0 copy-start.1
  0.6 0.1 sine_negate_fusion
  0.8 0.1 fusion.49
  0.9 0.1 fusion.57
  1.0 0.1 fusion.61
  1.1 1.4 %reshape.510 = bf16[16,4,4096]{2,1,0:T(4,128)(2,1)S(1)} reshape(bf16[16,16384]{1,0:T(8,128)(2,1)} %param.5) | data formatting | bytes 1048576 | tf_op jit(solution)/shard_map/reshape | solution.py:24
  2.6 1.1 %fusion.74 = (bf16[16,1,4096]{2,1,0:T(2,128)(2,1)S(1)}, bf16[16,1,4096]{2,1,0:T(2,128)(2,1)S(1)}, bf16[16,1,4096]{2,1,0:T(2,128)(2,1)S(1)}, bf16[16,1,4096]{2,1,0:T(2,128)(2,1)S(1)}) fusion(bf16[16,4,4096]{2,1,0:T(4,128)(2,1)S(1)} %reshape.510), kind=kLoop, calls=%fused_computation.126 | loop fusion | bytes 1048576 | tf_op jit(solution)/shard_map/slice | solution.py:28
  3.7 0.0 copy-done.1
  3.8 0.7 multiply_add_fusion.1
  4.4 0.2 reshape.511
  4.7 0.2 copy.14
  4.9 0.4 fusion.33
  5.3 0.6 reshape.512
  5.9 1.1 fusion.73
  7.0 0.3 copy.23
  7.4 0.3 copy.24
  7.7 0.1 fusion.15
  7.9 0.9 fusion.9
  8.8 0.2 convert_element_type.124
  9.1 0.1 reshape_reshape.3
  9.2 2.5 %broadcast_in_dim.7 = bf16[4,32,2,16,512]{4,3,2,1,0:T(8,128)(2,1)} broadcast(bf16[4,2,16,512]{3,2,1,0:T(8,128)(2,1)S(1)} %bitcast.58), dimensions={0,2,3,4} | broadcast | bytes 4325376 | tf_op jit(solution)/shard_map/broadcast_in_dim | solution.py:165
  11.8 0.0 copy-start.2
  11.8 0.0 copy-start
  11.8 11.9 %all-to-all-start = ((bf16[128,2,1,16,512]{4,3,2,1,0:T(8,128)(2,1)}), bf16[128,2,1,16,512]{4,3,2,1,0:T(8,128)(2,1)}, u32[]{:S(2)}, u32[]{:S(2)}) async-start(bf16[128,2,1,16,512]{4,3,2,1,0:T(8,128)(2,1)} %bitcast.54), calls=%async_computation | async-start | bytes 8388608 | tf_op jit(solution)/shard_map/all_to_all | solution.py:168
  23.7 0.1 fusion.71
  23.8 0.0 copy-done.2
  23.8 0.0 copy-done
  23.8 0.1 fusion.55
  23.9 0.1 fusion.59
  24.0 0.4 fusion.17
  24.4 9.1 %fusion = (f32[2048,256]{1,0:T(8,128)S(1)}, f32[2048,256]{1,0:T(8,128)S(1)}) fusion(f32[256]{0:T(256)S(1)} %get-tuple-element.40, f32[256]{0:T(256)S(1)} %get-tuple-element.41, f32[2048]{0:T(1024)S(1)} %bitcast.65, f32[2048]{0:T(1024)S(1)} %bitcast.64, s32[2048]{0:T(1024)S(1)} %bitcast.63), kind=kLoop, calls=%fused_computation.8 | loop fusion | flops 12582912 | bytes 4220928 | tf_op jit(solution)/shard_map/sub | solution.py:63
  33.5 5.0 %subtract_convert_fusion = (bf16[8,2048,256]{2,1,0:T(8,128)(2,1)S(1)}, bf16[8,2048,256]{2,1,0:T(8,128)(2,1)S(1)}) fusion(f32[2048,256]{1,0:T(8,128)S(1)} %get-tuple-element.25, f32[8,2048]{1,0:T(8,128)S(1)} %get-tuple-element.27, f32[2048,256]{1,0:T(8,128)S(1)} %get-tuple-element.24, f32[8,2048]{1,0:T(8,128)S(1)} %get-tuple-element.26), kind=kLoop, calls=%fused_computation.2 | loop fusion | flops 33554432 | bytes 21102592 | tf_op jit(solution)/shard_map/convert
  38.5 6.7 %pad_maximum_fusion.spread_ref = bf16[8,2048,512]{2,1,0:T(8,128)(2,1)} fusion(bf16[8,2048,256]{2,1,0:T(8,128)(2,1)S(1)} %get-tuple-element.11, bf16[8,2048,256]{2,1,0:T(8,128)(2,1)S(1)} %get-tuple-element.10), kind=kLoop, calls=%fused_computation | loop fusion | flops 33554432 | bytes 33554432 | tf_op jit(solution)/shard_map/concatenate | solution.py:156
  45.2 31.0 %all-to-all-done.spectra_ref = bf16[128,2,1,16,512]{4,3,2,1,0:T(8,128)(2,1)} async-done(((bf16[128,2,1,16,512]{4,3,2,1,0:T(8,128)(2,1)}), bf16[128,2,1,16,512]{4,3,2,1,0:T(8,128)(2,1)}, u32[]{:S(2)}, u32[]{:S(2)}) %all-to-all-start) | async-done | bytes 4194336 | tf_op jit(solution)/shard_map/all_to_all | solution.py:168
  76.2 28.2 %shard_map.68 = (f32[512,8,256]{2,1,0:T(8,128)}, f32[8,1,256]{2,1,0:T(1,128)S(1)}) custom-call(bf16[128,2,1,16,512]{4,3,2,1,0:T(8,128)(2,1)} %all-to-all-done.spectra_ref, bf16[8,2048,512]{2,1,0:T(8,128)(2,1)} %pad_maximum_fusion.spread_ref, f32[512,8,256]{2,1,0:T(8,128)} %sky_ref.1), custom_call_target="tpu_custom_call" | custom-call | flops 17179869184 | bytes 29360128 | tf_op jit(solution)/shard_map/pallas_call | solution.py:98
  104.3 1.2 %collective-permute-start = (f32[8,256]{1,0:T(8,128)S(1)}, f32[8,256]{1,0:T(8,128)S(1)}, u32[]{:S(2)}, u32[]{:S(2)}) collective-permute-start(f32[8,256]{1,0:T(8,128)S(1)} %bitcast.69), channel_id=1, source_target_pairs={{0,96},{32,0},{64,32},{96,64},{1,97},{33,1},{65,33},{97,65},{2,98}... | collective-permute-start | bytes 24584 | tf_op jit(solution)/shard_map/ppermute | solution.py:131
  105.6 1.4 %collective-permute-start.1 = (f32[8,256]{1,0:T(8,128)S(1)}, f32[8,256]{1,0:T(8,128)S(1)}, u32[]{:S(2)}, u32[]{:S(2)}) collective-permute-start(f32[8,256]{1,0:T(8,128)S(1)} %bitcast.70), channel_id=1, source_target_pairs={{0,64},{32,96},{64,0},{96,32},{1,65},{33,97},{65,1},{97,33},{2,66}... | collective-permute-start | bytes 24584 | tf_op jit(solution)/shard_map/ppermute | solution.py:131
  107.0 0.0 collective-permute-start.2
  107.0 0.0 collective-permute-done
  107.0 3.7 %collective-permute-done.1 = f32[8,256]{1,0:T(8,128)S(1)} collective-permute-done((f32[8,256]{1,0:T(8,128)S(1)}, f32[8,256]{1,0:T(8,128)S(1)}, u32[]{:S(2)}, u32[]{:S(2)}) %collective-permute-start.1) | collective-permute-done | bytes 8224 | tf_op jit(solution)/shard_map/ppermute | solution.py:131
  110.7 0.8 collective-permute-done.2
  111.6 0.6 add_multiply_fusion
  (6 shorter events, 0.2 us)
Async XLA Ops:
  0.6 3.1 %copy-start.1 = (f32[4,4096]{1,0:T(4,128)S(1)}, f32[4,4096]{1,0:T(4,128)}, u32[]{:S(2)}) copy-start(f32[4,4096]{1,0:T(4,128)} %param.6) | copy-start | bytes 196612
  11.8 12.0 %copy-start.2 = (s32[2048,2]{0,1:T(2,128)S(1)}, s32[2048,2]{0,1:T(2,128)}, u32[]{:S(2)}) copy-start(s32[2048,2]{0,1:T(2,128)} %param.7) | copy-start | bytes 49156
  11.8 12.0 %copy-start = (s32[2048,2]{0,1:T(2,128)S(1)}, s32[2048,2]{0,1:T(2,128)}, u32[]{:S(2)}) copy-start(s32[2048,2]{0,1:T(2,128)} %param.8) | copy-start | bytes 49156
  11.8 64.4 %all-to-all-start = ((bf16[128,2,1,16,512]{4,3,2,1,0:T(8,128)(2,1)}), bf16[128,2,1,16,512]{4,3,2,1,0:T(8,128)(2,1)}, u32[]{:S(2)}, u32[]{:S(2)}) async-start(bf16[128,2,1,16,512]{4,3,2,1,0:T(8,128)(2,1)} %bitcast.54), calls=%async_computation | async-start | bytes 8388608 | tf_op jit(solution)/shard_map/all_to_all | solution.py:168
  104.3 2.7 %collective-permute-start = (f32[8,256]{1,0:T(8,128)S(1)}, f32[8,256]{1,0:T(8,128)S(1)}, u32[]{:S(2)}, u32[]{:S(2)}) collective-permute-start(f32[8,256]{1,0:T(8,128)S(1)} %bitcast.69), channel_id=1, source_target_pairs={{0,96},{32,0},{64,32},{96,64},{1,97},{33,1},{65,33},{97,65},{2,98}... | collective-permute-start | bytes 24584 | tf_op jit(solution)/shard_map/ppermute | solution.py:131
  105.6 5.2 %collective-permute-start.1 = (f32[8,256]{1,0:T(8,128)S(1)}, f32[8,256]{1,0:T(8,128)S(1)}, u32[]{:S(2)}, u32[]{:S(2)}) collective-permute-start(f32[8,256]{1,0:T(8,128)S(1)} %bitcast.70), channel_id=1, source_target_pairs={{0,64},{32,96},{64,0},{96,32},{1,65},{33,97},{65,1},{97,33},{2,66}... | collective-permute-start | bytes 24584 | tf_op jit(solution)/shard_map/ppermute | solution.py:131
  107.0 4.6 %collective-permute-start.2 = (f32[8,256]{1,0:T(8,128)S(1)}, f32[8,256]{1,0:T(8,128)S(1)}, u32[]{:S(2)}, u32[]{:S(2)}) collective-permute-start(f32[8,256]{1,0:T(8,128)S(1)} %bitcast.71), channel_id=1, source_target_pairs={{0,32},{32,64},{64,96},{96,0},{1,33},{33,65},{65,97},{97,1},{2,34}... | collective-permute-start | bytes 24584 | tf_op jit(solution)/shard_map/ppermute | solution.py:131

commit v10 on v8

--- a/solution.py
+++ b/solution.py
@@ -77,8 +77,9 @@
     table = spread_ref[0]
     width = table.shape[1] // 2
     f32 = jnp.float32
-    from_re = jnp.dot(turned_ref[0], table, preferred_element_type=f32)
-    from_im = jnp.dot(turned_ref[1], table, preferred_element_type=f32)
+    both = jnp.dot(turned_ref[...].reshape(2 * span, sources * local), table, preferred_element_type=f32)
+    from_re = both[:span]
+    from_im = both[span:]
     sky_re = from_re[:, :width] - from_im[:, width:]
     sky_im = from_re[:, width:] + from_im[:, :width]
     power = (sky_re * sky_re + sky_im * sky_im) * norm_scale

time: 113 us -> 113 us (level)
  no operation moved by 1% of the time
where the time goes in v10:
time: 113 us; the launch traced here: 112 us
  waiting for transfers between devices  35.9 us (32%)
  Pallas kernels  29.2 us (26%)
  other arithmetic  23.3 us (21%)
  starting transfers between devices  13.3 us (12%)
  local copies, waits for them, and re-layouts  8.4 us (7%)
  matrix products  1.37 us (1%)
    all_to_all x1, waiting for transfers between devices, body(): lax.all_to_all(outgoing, ('grp', 'dev'), split_axis=0, concat_axis=0, til...  31 us
    pallas_call x1, Pallas kernels, image_block(): pl.pallas_call(functools.partial(image_kernel, norm_scale), grid=(rows_mi...  29.2 us
    all_to_all x1, starting transfers between devices, body(): lax.all_to_all(outgoing, ('grp', 'dev'), split_axis=0, concat_axis=0, til...  11.9 us
    sub x2, other arithmetic, row_phases(): real = base_re * shift_re - base_im * shift_im  9.47 us
    concatenate x1, other arithmetic, body(): jnp.concatenate([phase_re.T[:, :, None] * col_re[None] - phase_im.T[:, :,...  6.68 us
    another operation x1, other arithmetic  5.01 us
    ppermute x2, waiting for transfers between devices, group_sum(): value = value + lax.ppermute(value, 'grp', pairs)  4.89 us
    broadcast_in_dim x1, local copies, waits for them, and re-layouts, body(): jnp.broadcast_to(piece[:, None], (groups, members, parts, frame_count, lo...  2.55 us
  transfers between devices with their start and end apart: 3, of which 3 were waited for; matrix products, arithmetic and copies ran while one was open for 19% of the time, Pallas kernels for 0%

profile of v10, /device:TPU:0, one launch (start us, length us, event | category | flops | bytes accessed | tf_op | source)
XLA Modules:
  0.0 112.3 jit_solution(8647015440683845300)
XLA Ops:
  0.6 0.0 copy-start.1
  0.6 0.1 sine_negate_fusion
  0.8 0.1 fusion.49
  0.9 0.1 fusion.57
  1.0 0.1 fusion.61
  1.1 1.4 %reshape.510 = bf16[16,4,4096]{2,1,0:T(4,128)(2,1)S(1)} reshape(bf16[16,16384]{1,0:T(8,128)(2,1)} %param.5) | data formatting | bytes 1048576 | tf_op jit(solution)/shard_map/reshape | solution.py:24
  2.6 1.1 %fusion.75 = (bf16[16,1,4096]{2,1,0:T(2,128)(2,1)S(1)}, bf16[16,1,4096]{2,1,0:T(2,128)(2,1)S(1)}, bf16[16,1,4096]{2,1,0:T(2,128)(2,1)S(1)}, bf16[16,1,4096]{2,1,0:T(2,128)(2,1)S(1)}) fusion(bf16[16,4,4096]{2,1,0:T(4,128)(2,1)S(1)} %reshape.510), kind=kLoop, calls=%fused_computation.127 | loop fusion | bytes 1048576 | tf_op jit(solution)/shard_map/slice | solution.py:28
  3.7 0.0 copy-done.1
  3.8 0.7 multiply_add_fusion.1
  4.4 0.2 reshape.511
  4.7 0.2 copy.14
  4.9 0.4 fusion.33
  5.3 0.6 reshape.512
  5.9 1.1 fusion.74
  7.0 0.3 copy.23
  7.4 0.3 copy.24
  7.7 0.1 fusion.15
  7.9 0.9 fusion.9
  8.8 0.2 convert_element_type.124
  9.1 0.1 reshape_reshape.3
  9.2 2.5 %broadcast_in_dim.7 = bf16[4,32,2,16,512]{4,3,2,1,0:T(8,128)(2,1)} broadcast(bf16[4,2,16,512]{3,2,1,0:T(8,128)(2,1)S(1)} %bitcast.58), dimensions={0,2,3,4} | broadcast | bytes 4325376 | tf_op jit(solution)/shard_map/broadcast_in_dim | solution.py:164
  11.8 0.0 copy-start.2
  11.8 0.0 copy-start
  11.8 11.9 %all-to-all-start = ((bf16[128,2,1,16,512]{4,3,2,1,0:T(8,128)(2,1)}), bf16[128,2,1,16,512]{4,3,2,1,0:T(8,128)(2,1)}, u32[]{:S(2)}, u32[]{:S(2)}) async-start(bf16[128,2,1,16,512]{4,3,2,1,0:T(8,128)(2,1)} %bitcast.54), calls=%async_computation | async-start | bytes 8388608 | tf_op jit(solution)/shard_map/all_to_all | solution.py:167
  23.7 0.1 fusion.71
  23.8 0.0 copy-done.2
  23.8 0.0 copy-done
  23.8 0.1 fusion.55
  23.9 0.1 fusion.59
  24.0 0.4 fusion.17
  24.4 9.1 %fusion = (f32[2048,256]{1,0:T(8,128)S(1)}, f32[2048,256]{1,0:T(8,128)S(1)}) fusion(f32[256]{0:T(256)S(1)} %get-tuple-element.40, f32[256]{0:T(256)S(1)} %get-tuple-element.41, f32[2048]{0:T(1024)S(1)} %bitcast.65, f32[2048]{0:T(1024)S(1)} %bitcast.64, s32[2048]{0:T(1024)S(1)} %bitcast.63), kind=kLoop, calls=%fused_computation.8 | loop fusion | flops 12582912 | bytes 4220928 | tf_op jit(solution)/shard_map/sub | solution.py:63
  33.5 5.0 %subtract_convert_fusion = (bf16[8,2048,256]{2,1,0:T(8,128)(2,1)S(1)}, bf16[8,2048,256]{2,1,0:T(8,128)(2,1)S(1)}) fusion(f32[2048,256]{1,0:T(8,128)S(1)} %get-tuple-element.25, f32[8,2048]{1,0:T(8,128)S(1)} %get-tuple-element.27, f32[2048,256]{1,0:T(8,128)S(1)} %get-tuple-element.24, f32[8,2048]{1,0:T(8,128)S(1)} %get-tuple-element.26), kind=kLoop, calls=%fused_computation.2 | loop fusion | flops 33554432 | bytes 21102592 | tf_op jit(solution)/shard_map/convert
  38.5 6.7 %pad_maximum_fusion.spread_ref = bf16[8,2048,512]{2,1,0:T(8,128)(2,1)} fusion(bf16[8,2048,256]{2,1,0:T(8,128)(2,1)S(1)} %get-tuple-element.11, bf16[8,2048,256]{2,1,0:T(8,128)(2,1)S(1)} %get-tuple-element.10), kind=kLoop, calls=%fused_computation | loop fusion | flops 33554432 | bytes 33554432 | tf_op jit(solution)/shard_map/concatenate | solution.py:155
  45.2 31.0 %all-to-all-done.spectra_ref = bf16[128,2,1,16,512]{4,3,2,1,0:T(8,128)(2,1)} async-done(((bf16[128,2,1,16,512]{4,3,2,1,0:T(8,128)(2,1)}), bf16[128,2,1,16,512]{4,3,2,1,0:T(8,128)(2,1)}, u32[]{:S(2)}, u32[]{:S(2)}) %all-to-all-start) | async-done | bytes 4194336 | tf_op jit(solution)/shard_map/all_to_all | solution.py:167
  76.2 29.2 %shard_map.68 = (f32[512,8,256]{2,1,0:T(8,128)}, f32[8,1,256]{2,1,0:T(1,128)S(1)}) custom-call(bf16[128,2,1,16,512]{4,3,2,1,0:T(8,128)(2,1)} %all-to-all-done.spectra_ref, bf16[8,2048,512]{2,1,0:T(8,128)(2,1)} %pad_maximum_fusion.spread_ref, f32[512,8,256]{2,1,0:T(8,128)} %sky_ref.1), custom_call_target="tpu_custom_call" | custom-call | flops 17179869184 | bytes 29360128 | tf_op jit(solution)/shard_map/pallas_call | solution.py:102
  105.4 0.0 collective-permute-start
  105.4 1.2 %collective-permute-done = f32[8,256]{1,0:T(8,128)S(1)} collective-permute-done((f32[8,256]{1,0:T(8,128)S(1)}, f32[8,256]{1,0:T(8,128)S(1)}, u32[]{:S(2)}, u32[]{:S(2)}) %collective-permute-start) | collective-permute-done | bytes 8224 | tf_op jit(solution)/shard_map/ppermute | solution.py:133
  106.5 1.4 %collective-permute-start.1 = (f32[8,256]{1,0:T(8,128)S(1)}, f32[8,256]{1,0:T(8,128)S(1)}, u32[]{:S(2)}, u32[]{:S(2)}) collective-permute-start(f32[8,256]{1,0:T(8,128)S(1)} %fusion.73), channel_id=1, source_target_pairs={{0,64},{32,96},{64,0},{96,32},{1,65},{33,97},{65,1},{97,33},{2,66}... | collective-permute-start | bytes 24584 | tf_op jit(solution)/shard_map/ppermute | solution.py:133
  108.0 3.7 %collective-permute-done.1 = f32[8,256]{1,0:T(8,128)S(1)} collective-permute-done((f32[8,256]{1,0:T(8,128)S(1)}, f32[8,256]{1,0:T(8,128)S(1)}, u32[]{:S(2)}, u32[]{:S(2)}) %collective-permute-start.1) | collective-permute-done | bytes 8224 | tf_op jit(solution)/shard_map/ppermute | solution.py:133
  111.7 0.6 add_multiply_fusion
  (7 shorter events, 0.2 us)
Async XLA Ops:
  0.6 3.1 %copy-start.1 = (f32[4,4096]{1,0:T(4,128)S(1)}, f32[4,4096]{1,0:T(4,128)}, u32[]{:S(2)}) copy-start(f32[4,4096]{1,0:T(4,128)} %param.6) | copy-start | bytes 196612
  11.8 12.0 %copy-start.2 = (s32[2048,2]{0,1:T(2,128)S(1)}, s32[2048,2]{0,1:T(2,128)}, u32[]{:S(2)}) copy-start(s32[2048,2]{0,1:T(2,128)} %param.7) | copy-start | bytes 49156
  11.8 12.0 %copy-start = (s32[2048,2]{0,1:T(2,128)S(1)}, s32[2048,2]{0,1:T(2,128)}, u32[]{:S(2)}) copy-start(s32[2048,2]{0,1:T(2,128)} %param.8) | copy-start | bytes 49156
  11.8 64.4 %all-to-all-start = ((bf16[128,2,1,16,512]{4,3,2,1,0:T(8,128)(2,1)}), bf16[128,2,1,16,512]{4,3,2,1,0:T(8,128)(2,1)}, u32[]{:S(2)}, u32[]{:S(2)}) async-start(bf16[128,2,1,16,512]{4,3,2,1,0:T(8,128)(2,1)} %bitcast.54), calls=%async_computation | async-start | bytes 8388608 | tf_op jit(solution)/shard_map/all_to_all | solution.py:167
  105.4 1.2 %collective-permute-start = (f32[8,256]{1,0:T(8,128)S(1)}, f32[8,256]{1,0:T(8,128)S(1)}, u32[]{:S(2)}, u32[]{:S(2)}) collective-permute-start(f32[8,256]{1,0:T(8,128)S(1)} %bitcast.69), channel_id=1, source_target_pairs={{0,32},{32,0},{64,96},{96,64},{1,33},{33,1},{65,97},{97,65},{2,34}... | collective-permute-start | bytes 24584 | tf_op jit(solution)/shard_map/ppermute | solution.py:133
  106.5 5.2 %collective-permute-start.1 = (f32[8,256]{1,0:T(8,128)S(1)}, f32[8,256]{1,0:T(8,128)S(1)}, u32[]{:S(2)}, u32[]{:S(2)}) collective-permute-start(f32[8,256]{1,0:T(8,128)S(1)} %fusion.73), channel_id=1, source_target_pairs={{0,64},{32,96},{64,0},{96,32},{1,65},{33,97},{65,1},{97,33},{2,66}... | collective-permute-start | bytes 24584 | tf_op jit(solution)/shard_map/ppermute | solution.py:133

commit v11 on v7

--- a/solution.py
+++ b/solution.py
@@ -78,14 +78,14 @@
     sky_re = from_re[:, :width] - from_im[:, width:]
     sky_im = from_re[:, width:] + from_im[:, :width]
     power = (sky_re * sky_re + sky_im * sky_im) * norm_scale
-    row = pl.program_id(0)
+    row = pl.program_id(1)
     for index in range(out_ref.shape[1]):
 
         @pl.when(row == index)
         def _():
             residual = power - sky_ref[:, index, :]
             out_ref[:, index, :] = residual
-            band_ref[0] = jnp.sum(residual, axis=0, keepdims=True)
+            band_ref[0, 0] = jnp.sum(residual, axis=0, keepdims=True)
 
 
 def image_block(incoming, spread, sky_model, norm_scale):
@@ -95,21 +95,23 @@
     grid_len = grid_len // 2
     stacked = incoming
     flat_sky = sky_model
+    halves = 2
+    half = span // halves
     residual, band = pl.pallas_call(
         functools.partial(image_kernel, norm_scale),
-        grid=(rows_mine,),
+        grid=(halves, rows_mine),
         in_specs=[
-            pl.BlockSpec((sources, parts, frame_count, local, span), lambda m: (0, 0, 0, 0, 0)),
-            pl.BlockSpec((1, dipoles, 2 * grid_len), lambda m: (m, 0, 0)),
-            pl.BlockSpec((span, rows_mine, grid_len), lambda m: (0, 0, 0)),
+            pl.BlockSpec((sources, parts, frame_count, local, half), lambda h, m: (0, 0, 0, 0, h)),
+            pl.BlockSpec((1, dipoles, 2 * grid_len), lambda h, m: (m, 0, 0)),
+            pl.BlockSpec((half, rows_mine, grid_len), lambda h, m: (h, 0, 0)),
         ],
         out_specs=[
-            pl.BlockSpec((span, rows_mine, grid_len), lambda m: (0, 0, 0)),
-            pl.BlockSpec((1, 1, grid_len), lambda m: (m, 0, 0)),
+            pl.BlockSpec((half, rows_mine, grid_len), lambda h, m: (h, 0, 0)),
+            pl.BlockSpec((1, 1, 1, grid_len), lambda h, m: (h, m, 0, 0)),
         ],
         out_shape=[
             jax.ShapeDtypeStruct((span, rows_mine, grid_len), jnp.float32),
-            jax.ShapeDtypeStruct((rows_mine, 1, grid_len), jnp.float32),
+            jax.ShapeDtypeStruct((halves, rows_mine, 1, grid_len), jnp.float32),
         ],
         compiler_params=pltpu.CompilerParams(vmem_limit_bytes=48 * 1024 * 1024),
         cost_estimate=pl.CostEstimate(
@@ -118,7 +120,7 @@
             bytes_accessed=2 * stacked.size + 2 * spread.size + 8 * flat_sky.size,
         ),
     )(stacked, spread, flat_sky)
-    return residual, band.reshape(rows_mine, grid_len)
+    return residual, jnp.sum(band, axis=0).reshape(rows_mine, grid_len)
 
 
 def group_sum(value, groups):

time: 112 us -> 115 us (1.027)
  Pallas kernels: 28.2 us -> 31.1 us
    pallas_call x1, Pallas kernels: 28.2 us -> 31.1 us  [image_block(): pl.pallas_call(functools.partial(image_kernel, norm_scale), grid=(halves,...]
where the time goes in v11:
time: 115 us; the launch traced here: 114 us
  waiting for transfers between devices  35.9 us (31%)
  Pallas kernels  31.1 us (27%)
  other arithmetic  23.3 us (20%)
  starting transfers between devices  13.4 us (12%)
  local copies, waits for them, and re-layouts  8.39 us (7%)
  matrix products  1.37 us (1%)
    pallas_call x1, Pallas kernels, image_block(): pl.pallas_call(functools.partial(image_kernel, norm_scale), grid=(halves,...  31.1 us
    all_to_all x1, waiting for transfers between devices, body(): lax.all_to_all(outgoing, ('grp', 'dev'), split_axis=0, concat_axis=0, til...  31 us
    all_to_all x1, starting transfers between devices, body(): lax.all_to_all(outgoing, ('grp', 'dev'), split_axis=0, concat_axis=0, til...  11.9 us
    sub x2, other arithmetic, row_phases(): real = base_re * shift_re - base_im * shift_im  9.47 us
    concatenate x1, other arithmetic, body(): jnp.concatenate([phase_re.T[:, :, None] * col_re[None] - phase_im.T[:, :,...  6.69 us
    another operation x1, other arithmetic  5.01 us
    ppermute x2, waiting for transfers between devices, group_sum(): value = value + lax.ppermute(value, 'grp', pairs)  4.88 us
    broadcast_in_dim x1, local copies, waits for them, and re-layouts, body(): jnp.broadcast_to(piece[:, None], (groups, members, parts, frame_count, lo...  2.55 us
  transfers between devices with their start and end apart: 3, of which 3 were waited for; matrix products, arithmetic and copies ran while one was open for 19% of the time, Pallas kernels for 0%

profile of v11, /device:TPU:0, one launch (start us, length us, event | category | flops | bytes accessed | tf_op | source)
XLA Modules:
  0.0 114.3 jit_solution(4828999572659482273)
XLA Ops:
  0.6 0.0 copy-start.1
  0.6 0.1 sine_negate_fusion
  0.8 0.1 fusion.49
  0.9 0.1 fusion.57
  1.0 0.1 fusion.61
  1.1 1.4 %reshape.510 = bf16[16,4,4096]{2,1,0:T(4,128)(2,1)S(1)} reshape(bf16[16,16384]{1,0:T(8,128)(2,1)} %param.5) | data formatting | bytes 1048576 | tf_op jit(solution)/shard_map/reshape | solution.py:24
  2.6 1.1 fusion.74
  3.7 0.0 copy-done.1
  3.8 0.7 multiply_add_fusion.1
  4.4 0.2 reshape.511
  4.7 0.2 copy.14
  4.9 0.4 fusion.33
  5.3 0.6 reshape.512
  5.9 1.1 fusion.73
  7.0 0.3 copy.22
  7.4 0.3 copy.23
  7.7 0.1 fusion.15
  7.9 0.9 fusion.9
  8.8 0.2 convert_element_type.124
  9.1 0.1 reshape_reshape.3
  9.2 2.5 %broadcast_in_dim.7 = bf16[4,32,2,16,512]{4,3,2,1,0:T(8,128)(2,1)} broadcast(bf16[4,2,16,512]{3,2,1,0:T(8,128)(2,1)S(1)} %bitcast.53), dimensions={0,2,3,4} | broadcast | bytes 4325376 | tf_op jit(solution)/shard_map/broadcast_in_dim | solution.py:161
  11.8 0.0 copy-start.2
  11.8 0.0 copy-start
  11.8 11.9 %all-to-all-start = ((bf16[128,2,1,16,512]{4,3,2,1,0:T(8,128)(2,1)}), bf16[128,2,1,16,512]{4,3,2,1,0:T(8,128)(2,1)}, u32[]{:S(2)}, u32[]{:S(2)}) async-start(bf16[128,2,1,16,512]{4,3,2,1,0:T(8,128)(2,1)} %bitcast.49), calls=%async_computation | async-start | bytes 8388608 | tf_op jit(solution)/shard_map/all_to_all | solution.py:164
  23.7 0.1 fusion.71
  23.8 0.0 copy-done.2
  23.8 0.0 copy-done
  23.8 0.1 fusion.55
  23.9 0.1 fusion.59
  24.0 0.4 fusion.17
  24.4 9.1 %fusion = (f32[2048,256]{1,0:T(8,128)S(1)}, f32[2048,256]{1,0:T(8,128)S(1)}) fusion(f32[256]{0:T(256)S(1)} %get-tuple-element.40, f32[256]{0:T(256)S(1)} %get-tuple-element.41, f32[2048]{0:T(1024)S(1)} %bitcast.60, f32[2048]{0:T(1024)S(1)} %bitcast.59, s32[2048]{0:T(1024)S(1)} %bitcast.58), kind=kLoop, calls=%fused_computation.8 | loop fusion | flops 12582912 | bytes 4220928 | tf_op jit(solution)/shard_map/sub | solution.py:63
  33.5 5.0 %subtract_convert_fusion = (bf16[8,2048,256]{2,1,0:T(8,128)(2,1)S(1)}, bf16[8,2048,256]{2,1,0:T(8,128)(2,1)S(1)}) fusion(f32[2048,256]{1,0:T(8,128)S(1)} %get-tuple-element.25, f32[8,2048]{1,0:T(8,128)S(1)} %get-tuple-element.27, f32[2048,256]{1,0:T(8,128)S(1)} %get-tuple-element.24, f32[8,2048]{1,0:T(8,128)S(1)} %get-tuple-element.26), kind=kLoop, calls=%fused_computation.2 | loop fusion | flops 33554432 | bytes 21102592 | tf_op jit(solution)/shard_map/convert
  38.5 6.7 %pad_maximum_fusion.spread_ref = bf16[8,2048,512]{2,1,0:T(8,128)(2,1)} fusion(bf16[8,2048,256]{2,1,0:T(8,128)(2,1)S(1)} %get-tuple-element.11, bf16[8,2048,256]{2,1,0:T(8,128)(2,1)S(1)} %get-tuple-element.10), kind=kLoop, calls=%fused_computation | loop fusion | flops 33554432 | bytes 33554432 | tf_op jit(solution)/shard_map/concatenate | solution.py:152
  45.2 31.0 %all-to-all-done.spectra_ref = bf16[128,2,1,16,512]{4,3,2,1,0:T(8,128)(2,1)} async-done(((bf16[128,2,1,16,512]{4,3,2,1,0:T(8,128)(2,1)}), bf16[128,2,1,16,512]{4,3,2,1,0:T(8,128)(2,1)}, u32[]{:S(2)}, u32[]{:S(2)}) %all-to-all-start) | async-done | bytes 4194336 | tf_op jit(solution)/shard_map/all_to_all | solution.py:164
  76.2 31.1 %shard_map.68 = (f32[512,8,256]{2,1,0:T(8,128)}, f32[2,8,1,256]{3,2,1,0:T(1,128)S(1)}) custom-call(bf16[128,2,1,16,512]{4,3,2,1,0:T(8,128)(2,1)} %all-to-all-done.spectra_ref, bf16[8,2048,512]{2,1,0:T(8,128)(2,1)} %pad_maximum_fusion.spread_ref, f32[512,8,256]{2,1,0:T(8,128)} %sky_ref.1), custom_call_target="tpu_custom_call" | custom-call | flops 17179869184 | bytes 29360128 | tf_op jit(solution)/shard_map/pallas_call | solution.py:100
  107.3 0.1 collective-permute-start
  107.4 1.2 %collective-permute-done = f32[8,256]{1,0:T(8,128)S(1)} collective-permute-done((f32[8,256]{1,0:T(8,128)S(1)}, f32[8,256]{1,0:T(8,128)S(1)}, u32[]{:S(2)}, u32[]{:S(2)}) %collective-permute-start) | collective-permute-done | bytes 8224 | tf_op jit(solution)/shard_map/ppermute | solution.py:130
  108.6 1.4 %collective-permute-start.1 = (f32[8,256]{1,0:T(8,128)S(1)}, f32[8,256]{1,0:T(8,128)S(1)}, u32[]{:S(2)}, u32[]{:S(2)}) collective-permute-start(f32[8,256]{1,0:T(8,128)S(1)} %add.221), channel_id=1, source_target_pairs={{0,64},{32,96},{64,0},{96,32},{1,65},{33,97},{65,1},{97,33},{2,66}... | collective-permute-start | bytes 24584 | tf_op jit(solution)/shard_map/ppermute | solution.py:130
  110.0 3.7 %collective-permute-done.1 = f32[8,256]{1,0:T(8,128)S(1)} collective-permute-done((f32[8,256]{1,0:T(8,128)S(1)}, f32[8,256]{1,0:T(8,128)S(1)}, u32[]{:S(2)}, u32[]{:S(2)}) %collective-permute-start.1) | collective-permute-done | bytes 8224 | tf_op jit(solution)/shard_map/ppermute | solution.py:130
  113.7 0.6 add_multiply_fusion
  (7 shorter events, 0.2 us)
Async XLA Ops:
  0.6 3.1 %copy-start.1 = (f32[4,4096]{1,0:T(4,128)S(1)}, f32[4,4096]{1,0:T(4,128)}, u32[]{:S(2)}) copy-start(f32[4,4096]{1,0:T(4,128)} %param.6) | copy-start | bytes 196612
  11.8 12.0 %copy-start.2 = (s32[2048,2]{0,1:T(2,128)S(1)}, s32[2048,2]{0,1:T(2,128)}, u32[]{:S(2)}) copy-start(s32[2048,2]{0,1:T(2,128)} %param.7) | copy-start | bytes 49156
  11.8 12.0 %copy-start = (s32[2048,2]{0,1:T(2,128)S(1)}, s32[2048,2]{0,1:T(2,128)}, u32[]{:S(2)}) copy-start(s32[2048,2]{0,1:T(2,128)} %param.8) | copy-start | bytes 49156
  11.8 64.4 %all-to-all-start = ((bf16[128,2,1,16,512]{4,3,2,1,0:T(8,128)(2,1)}), bf16[128,2,1,16,512]{4,3,2,1,0:T(8,128)(2,1)}, u32[]{:S(2)}, u32[]{:S(2)}) async-start(bf16[128,2,1,16,512]{4,3,2,1,0:T(8,128)(2,1)} %bitcast.49), calls=%async_computation | async-start | bytes 8388608 | tf_op jit(solution)/shard_map/all_to_all | solution.py:164
  107.3 1.3 %collective-permute-start = (f32[8,256]{1,0:T(8,128)S(1)}, f32[8,256]{1,0:T(8,128)S(1)}, u32[]{:S(2)}, u32[]{:S(2)}) collective-permute-start(f32[8,256]{1,0:T(8,128)S(1)} %reduce_sum.9), channel_id=1, source_target_pairs={{0,32},{32,0},{64,96},{96,64},{1,33},{33,1},{65,97},{97,65},{2,34}... | collective-permute-start | bytes 24584 | tf_op jit(solution)/shard_map/ppermute | solution.py:130
  108.6 5.2 %collective-permute-start.1 = (f32[8,256]{1,0:T(8,128)S(1)}, f32[8,256]{1,0:T(8,128)S(1)}, u32[]{:S(2)}, u32[]{:S(2)}) collective-permute-start(f32[8,256]{1,0:T(8,128)S(1)} %add.221), channel_id=1, source_target_pairs={{0,64},{32,96},{64,0},{96,32},{1,65},{33,97},{65,1},{97,33},{2,66}... | collective-permute-start | bytes 24584 | tf_op jit(solution)/shard_map/ppermute | solution.py:130

commit v12 on v7

--- a/solution.py
+++ b/solution.py
@@ -21,13 +21,17 @@
 def channelize(voltages, filter_taps, channels):
     tap_count, points = filter_taps.shape
     dipoles = voltages.shape[0]
-    segments = voltages.reshape(dipoles, -1, points)
-    frame_count = segments.shape[1] - tap_count + 1
-    framed = jnp.zeros((dipoles, frame_count, points), jnp.float32)
-    for tap_index in range(tap_count):
-        framed = framed + filter_taps[tap_index][None, None, :] * segments[
-            :, tap_index : tap_index + frame_count, :
-        ].astype(jnp.float32)
+    frame_count = voltages.shape[1] // points - tap_count + 1
+    frames = []
+    for frame in range(frame_count):
+        total = jnp.zeros((dipoles, points), jnp.float32)
+        for tap_index in range(tap_count):
+            start = (frame + tap_index) * points
+            total = total + filter_taps[tap_index][None, :] * voltages[:, start : start + points].astype(
+                jnp.float32
+            )
+        frames.append(total)
+    framed = jnp.stack(frames, axis=1)
     outer = 64
     inner = points // outer
     kept = channels // outer

time: 112 us -> 111 us (level)
  local copies, waits for them, and re-layouts: 8.4 us -> 6.83 us
    reshape x3 -> x0, local copies, waits for them, and re-layouts: 1.85 us -> none  [the longest x1 1.43 us: channelize(): segments = voltages.reshape(dipoles, -1, points)]
where the time goes in v12:
time: 111 us; the launch traced here: 110 us
  waiting for transfers between devices  35.9 us (32%)
  Pallas kernels  28.2 us (25%)
  other arithmetic  23.8 us (21%)
  starting transfers between devices  13.3 us (12%)
  local copies, waits for them, and re-layouts  6.83 us (6%)
  matrix products  1.38 us (1%)
    all_to_all x1, waiting for transfers between devices, body(): lax.all_to_all(outgoing, ('grp', 'dev'), split_axis=0, concat_axis=0, til...  31 us
    pallas_call x1, Pallas kernels, image_block(): pl.pallas_call(functools.partial(image_kernel, norm_scale), grid=(rows_mi...  28.2 us
    all_to_all x1, starting transfers between devices, body(): lax.all_to_all(outgoing, ('grp', 'dev'), split_axis=0, concat_axis=0, til...  11.9 us
    sub x2, other arithmetic, row_phases(): real = base_re * shift_re - base_im * shift_im  9.47 us
    concatenate x1, other arithmetic, body(): jnp.concatenate([phase_re.T[:, :, None] * col_re[None] - phase_im.T[:, :,...  6.69 us
    another operation x1, other arithmetic  5.01 us
    ppermute x2, waiting for transfers between devices, group_sum(): value = value + lax.ppermute(value, 'grp', pairs)  4.89 us
    broadcast_in_dim x1, local copies, waits for them, and re-layouts, body(): jnp.broadcast_to(piece[:, None], (groups, members, parts, frame_count, lo...  2.55 us
  transfers between devices with their start and end apart: 3, of which 3 were waited for; matrix products, arithmetic and copies ran while one was open for 19% of the time, Pallas kernels for 0%

profile of v12, /device:TPU:0, one launch (start us, length us, event | category | flops | bytes accessed | tf_op | source)
XLA Modules:
  0.0 110.2 jit_solution(14640689635656317900)
XLA Ops:
  0.6 0.1 sine_negate_fusion
  0.8 0.1 fusion.49
  0.9 0.1 fusion.57
  1.0 0.1 fusion.61
  1.1 1.1 fusion.75
  2.2 1.2 %multiply_add_fusion.1 = f32[16,4096]{1,0:T(8,128)S(1)} fusion(bf16[16,16384]{1,0:T(8,128)(2,1)} %param.5, f32[4096]{0:T(1024)S(1)} %bitcast.59, f32[4096]{0:T(1024)S(1)} %bitcast.60, f32[4096]{0:T(1024)S(1)} %bitcast.58, f32[4096]{0:T(1024)S(1)} %bitcast.57), kind=kLoop, calls=%fused_computation.31 | loop fusion | flops 720896 | bytes 851968 | tf_op jit(solution)/shard_map/add | solution.py:30
  3.4 0.2 reshape_stack.3
  3.6 0.2 copy.7
  3.8 0.4 fusion.33
  4.2 0.6 reshape.492
  4.9 1.1 %fusion.74 = (f32[16,1,64,64]{2,1,3,0:T(1,128)S(1)}, f32[16,1,64,64]{2,1,3,0:T(1,128)S(1)}) fusion(f32[16,2,64,64]{2,1,3,0:T(2,128)S(1)} %reshape.492), kind=kLoop, calls=%fused_computation.126 | loop fusion | bytes 1048576 | tf_op jit(solution)/shard_map/slice | solution.py:45
  6.0 0.3 copy.12
  6.3 0.3 copy.13
  6.7 0.1 fusion.15
  6.8 0.9 fusion.9
  7.8 0.2 convert_element_type.124
  8.0 0.1 reshape_reshape.3
  8.2 2.5 %broadcast_in_dim.7 = bf16[4,32,2,16,512]{4,3,2,1,0:T(8,128)(2,1)} broadcast(bf16[4,2,16,512]{3,2,1,0:T(8,128)(2,1)S(1)} %bitcast.56), dimensions={0,2,3,4} | broadcast | bytes 4325376 | tf_op jit(solution)/shard_map/broadcast_in_dim | solution.py:163
  10.7 0.0 copy-start.1
  10.7 0.0 copy-start
  10.7 11.9 %all-to-all-start = ((bf16[128,2,1,16,512]{4,3,2,1,0:T(8,128)(2,1)}), bf16[128,2,1,16,512]{4,3,2,1,0:T(8,128)(2,1)}, u32[]{:S(2)}, u32[]{:S(2)}) async-start(bf16[128,2,1,16,512]{4,3,2,1,0:T(8,128)(2,1)} %bitcast.52), calls=%async_computation | async-start | bytes 8388608 | tf_op jit(solution)/shard_map/all_to_all | solution.py:166
  22.7 0.1 fusion.71
  22.7 0.0 copy-done.1
  22.8 0.0 copy-done
  22.8 0.1 fusion.55
  22.8 0.1 fusion.59
  22.9 0.4 fusion.17
  23.3 9.1 %fusion = (f32[2048,256]{1,0:T(8,128)S(1)}, f32[2048,256]{1,0:T(8,128)S(1)}) fusion(f32[256]{0:T(256)S(1)} %get-tuple-element.36, f32[256]{0:T(256)S(1)} %get-tuple-element.37, f32[2048]{0:T(1024)S(1)} %bitcast.63, f32[2048]{0:T(1024)S(1)} %bitcast.62, s32[2048]{0:T(1024)S(1)} %bitcast.61), kind=kLoop, calls=%fused_computation.8 | loop fusion | flops 12582912 | bytes 4220928 | tf_op jit(solution)/shard_map/sub | solution.py:67
  32.4 5.0 %subtract_convert_fusion = (bf16[8,2048,256]{2,1,0:T(8,128)(2,1)S(1)}, bf16[8,2048,256]{2,1,0:T(8,128)(2,1)S(1)}) fusion(f32[2048,256]{1,0:T(8,128)S(1)} %get-tuple-element.21, f32[8,2048]{1,0:T(8,128)S(1)} %get-tuple-element.23, f32[2048,256]{1,0:T(8,128)S(1)} %get-tuple-element.20, f32[8,2048]{1,0:T(8,128)S(1)} %get-tuple-element.22), kind=kLoop, calls=%fused_computation.2 | loop fusion | flops 33554432 | bytes 21102592 | tf_op jit(solution)/shard_map/convert
  37.4 6.7 %pad_maximum_fusion.spread_ref = bf16[8,2048,512]{2,1,0:T(8,128)(2,1)} fusion(bf16[8,2048,256]{2,1,0:T(8,128)(2,1)S(1)} %get-tuple-element.11, bf16[8,2048,256]{2,1,0:T(8,128)(2,1)S(1)} %get-tuple-element.10), kind=kLoop, calls=%fused_computation | loop fusion | flops 33554432 | bytes 33554432 | tf_op jit(solution)/shard_map/concatenate | solution.py:154
  44.1 31.0 %all-to-all-done.spectra_ref = bf16[128,2,1,16,512]{4,3,2,1,0:T(8,128)(2,1)} async-done(((bf16[128,2,1,16,512]{4,3,2,1,0:T(8,128)(2,1)}), bf16[128,2,1,16,512]{4,3,2,1,0:T(8,128)(2,1)}, u32[]{:S(2)}, u32[]{:S(2)}) %all-to-all-start) | async-done | bytes 4194336 | tf_op jit(solution)/shard_map/all_to_all | solution.py:166
  75.1 28.2 %shard_map.68 = (f32[512,8,256]{2,1,0:T(8,128)}, f32[8,1,256]{2,1,0:T(1,128)S(1)}) custom-call(bf16[128,2,1,16,512]{4,3,2,1,0:T(8,128)(2,1)} %all-to-all-done.spectra_ref, bf16[8,2048,512]{2,1,0:T(8,128)(2,1)} %pad_maximum_fusion.spread_ref, f32[512,8,256]{2,1,0:T(8,128)} %sky_ref.1), custom_call_target="tpu_custom_call" | custom-call | flops 17179869184 | bytes 29360128 | tf_op jit(solution)/shard_map/pallas_call | solution.py:102
  103.3 0.0 collective-permute-start
  103.3 1.2 %collective-permute-done = f32[8,256]{1,0:T(8,128)S(1)} collective-permute-done((f32[8,256]{1,0:T(8,128)S(1)}, f32[8,256]{1,0:T(8,128)S(1)}, u32[]{:S(2)}, u32[]{:S(2)}) %collective-permute-start) | collective-permute-done | bytes 8224 | tf_op jit(solution)/shard_map/ppermute | solution.py:132
  104.4 1.4 %collective-permute-start.1 = (f32[8,256]{1,0:T(8,128)S(1)}, f32[8,256]{1,0:T(8,128)S(1)}, u32[]{:S(2)}, u32[]{:S(2)}) collective-permute-start(f32[8,256]{1,0:T(8,128)S(1)} %fusion.73), channel_id=1, source_target_pairs={{0,64},{32,96},{64,0},{96,32},{1,65},{33,97},{65,1},{97,33},{2,66}... | collective-permute-start | bytes 24584 | tf_op jit(solution)/shard_map/ppermute | solution.py:132
  105.9 3.7 %collective-permute-done.1 = f32[8,256]{1,0:T(8,128)S(1)} collective-permute-done((f32[8,256]{1,0:T(8,128)S(1)}, f32[8,256]{1,0:T(8,128)S(1)}, u32[]{:S(2)}, u32[]{:S(2)}) %collective-permute-start.1) | collective-permute-done | bytes 8224 | tf_op jit(solution)/shard_map/ppermute | solution.py:132
  109.6 0.6 add_multiply_fusion
  (6 shorter events, 0.1 us)
Async XLA Ops:
  10.7 12.0 %copy-start.1 = (s32[2048,2]{0,1:T(2,128)S(1)}, s32[2048,2]{0,1:T(2,128)}, u32[]{:S(2)}) copy-start(s32[2048,2]{0,1:T(2,128)} %param.7) | copy-start | bytes 49156
  10.7 12.0 %copy-start = (s32[2048,2]{0,1:T(2,128)S(1)}, s32[2048,2]{0,1:T(2,128)}, u32[]{:S(2)}) copy-start(s32[2048,2]{0,1:T(2,128)} %param.8) | copy-start | bytes 49156
  10.7 64.4 %all-to-all-start = ((bf16[128,2,1,16,512]{4,3,2,1,0:T(8,128)(2,1)}), bf16[128,2,1,16,512]{4,3,2,1,0:T(8,128)(2,1)}, u32[]{:S(2)}, u32[]{:S(2)}) async-start(bf16[128,2,1,16,512]{4,3,2,1,0:T(8,128)(2,1)} %bitcast.52), calls=%async_computation | async-start | bytes 8388608 | tf_op jit(solution)/shard_map/all_to_all | solution.py:166
  103.3 1.2 %collective-permute-start = (f32[8,256]{1,0:T(8,128)S(1)}, f32[8,256]{1,0:T(8,128)S(1)}, u32[]{:S(2)}, u32[]{:S(2)}) collective-permute-start(f32[8,256]{1,0:T(8,128)S(1)} %bitcast.67), channel_id=1, source_target_pairs={{0,32},{32,0},{64,96},{96,64},{1,33},{33,1},{65,97},{97,65},{2,34}... | collective-permute-start | bytes 24584 | tf_op jit(solution)/shard_map/ppermute | solution.py:132
  104.4 5.2 %collective-permute-start.1 = (f32[8,256]{1,0:T(8,128)S(1)}, f32[8,256]{1,0:T(8,128)S(1)}, u32[]{:S(2)}, u32[]{:S(2)}) collective-permute-start(f32[8,256]{1,0:T(8,128)S(1)} %fusion.73), channel_id=1, source_target_pairs={{0,64},{32,96},{64,0},{96,32},{1,65},{33,97},{65,1},{97,33},{2,66}... | collective-permute-start | bytes 24584 | tf_op jit(solution)/shard_map/ppermute | solution.py:132
